TPU v7x, 512 devices: a whole 4x8x8 slice. The times are simulated.
512 devices in a mesh: seq: 128 (over x, z_hi, y, core), tp: 4 (over z_lo).
Axes of the slice: x: 4, y: 8, z: 8 (z_hi: 2, z_lo: 4; z = z_hi * 4 + z_lo), core: 2. Of those that a mesh axis runs over, the one named last changes fastest.
Arguments:
- queries: bfloat16 [16384, 4096], P('seq', 'tp'), may hold values from -6 to 6
- suffix_entries: bfloat16 [16384, 4096], P('seq', 'tp'), may hold values from -6 to 6
- prefix_cache: bfloat16 [2048, 4096], P(('seq', 'tp')), may hold values from -6 to 6
- block_prefix: int32 [512], replicated, may hold values from 0 to 1, as said below
- request_lengths: int32 [512], P('seq'), may hold values from 0 to 128, as said below
- request_prefix: int32 [512], P('seq'), may hold values from 0 to 1
Outputs:
- attended: bfloat16 [16384, 4096], P('seq', 'tp')
Inputs may be any that keep to these rules, and one draw needn't show every extreme that they name: `request_lengths`: the lengths of one index of seq's requests sum to at most 128; at some index they sum to exactly 128, and there one request alone takes all 128 slots. `block_prefix`: exactly half of the blocks belong to each prefix.
All inputs are finite; a program needn't handle non-finite values.
Results may differ from a plain program's by a relative error of at most 0.0049.
Values may be sent and summed in bfloat16 or wider, within the bound.
No kernel may reach another device: no remote copies, remote signals or barrier semaphores. Data moves between devices by JAX's collectives and lax.ppermute only.
A program may use at most 64 MiB of HBM per device.

v0:
```python
import math

import jax
import jax.numpy as jnp
from jax import lax
from jax.sharding import PartitionSpec as P

HEADS = 16
HEAD = 128


masked_score = -1e30
section_rows = 512


def token_layout(lengths, prefixes, slots):
    cumulative = jnp.cumsum(lengths)
    slot_ids = jnp.arange(slots, dtype=jnp.int32)
    request_ids = jnp.sum((slot_ids[:, None] >= cumulative[None, :]).astype(jnp.int32), axis=1)
    live_slots = slot_ids < cumulative[-1]
    onehot = request_ids[:, None] == jnp.arange(lengths.shape[0], dtype=jnp.int32)[None, :]
    token_group = jnp.sum(jnp.where(onehot, prefixes[None, :], 0), axis=1)
    return (slot_ids, request_ids, live_slots, token_group)


def attend(running, query_rows, key_rows, value_rows, allowed):
    old_max, old_total, old_sum = running
    scores = jnp.einsum("thed,rhd->ther", query_rows, key_rows, preferred_element_type=jnp.float32)
    scores = scores * (1.0 / math.sqrt(query_rows.shape[-1]))
    allowed_grid = allowed[:, None, None, :]
    scores = jnp.where(allowed_grid, scores, masked_score)
    new_max = jnp.maximum(old_max, jnp.max(scores, axis=-1))
    rescale = jnp.exp(old_max - new_max)
    weights = jnp.where(allowed_grid, jnp.exp(scores - new_max[..., None]), 0.0)
    new_total = old_total * rescale + jnp.sum(weights, axis=-1)
    products = jnp.einsum(
        "ther,rhd->thed",
        weights.astype(jnp.bfloat16),
        value_rows,
        preferred_element_type=jnp.float32,
    )
    new_sum = old_sum * rescale[..., None] + products
    return (new_max, new_total, new_sum)


def owner_lookup(block_ids, block_prefix):
    match = block_ids[:, None] == jnp.arange(block_prefix.shape[0], dtype=jnp.int32)[None, :]
    return jnp.sum(jnp.where(match, block_prefix[None, :], 0), axis=1)


def empty_state(token_rows, head_count):
    return (
        jnp.full((token_rows, head_count, 2), masked_score, jnp.float32),
        jnp.zeros((token_rows, head_count, 2), jnp.float32),
        jnp.zeros((token_rows, head_count, 2, HEAD), jnp.float32),
    )


def sweep(running, query_rows, rows, head_count, block_of, block_prefix, token_group, live_slots):
    total_rows = rows.shape[0]
    for offset in range(0, total_rows, section_rows):
        row_count = min(section_rows, total_rows - offset)
        section = rows[offset : offset + row_count].reshape(row_count, head_count, 2, HEAD)
        positions = offset + jnp.arange(row_count, dtype=jnp.int32)
        owners = owner_lookup(block_of(positions), block_prefix)
        allowed = (token_group[:, None] == owners[None, :]) & live_slots[:, None]
        running = attend(running, query_rows, section[:, :, 0], section[:, :, 1], allowed)
    return running


def per_device(
    queries, suffix_entries, prefix_cache, block_prefix, request_lengths, request_prefix
):
    tensor_count = lax.axis_size("tp")
    seq_count = lax.axis_size("seq")
    local_heads = HEADS // tensor_count
    token_rows = queries.shape[0]
    block_rows = prefix_cache.shape[0]
    slot_ids, request_ids, live_slots, token_group = token_layout(
        request_lengths, request_prefix, token_rows
    )
    own_query = queries.reshape(token_rows, local_heads, 2, HEAD)
    own_entries = suffix_entries.reshape(token_rows, local_heads, 2, HEAD)
    gathered = lax.all_gather(prefix_cache, "seq", axis=0, tiled=True)
    cached = lax.all_to_all(gathered, "tp", split_axis=1, concat_axis=0, tiled=True)
    span = seq_count * block_rows

    def block_of(positions):
        return positions % span // block_rows * tensor_count + positions // span

    running = sweep(
        empty_state(token_rows, local_heads),
        own_query,
        cached,
        local_heads,
        block_of,
        block_prefix,
        token_group,
        live_slots,
    )
    suffix_allowed = (
        (request_ids[:, None] == request_ids[None, :])
        & (slot_ids[None, :] <= slot_ids[:, None])
        & live_slots[:, None]
    )
    running = attend(running, own_query, own_entries[:, :, 0], own_entries[:, :, 1], suffix_allowed)
    final_max, final_total, final_sum = running
    live_grid = live_slots[:, None, None]
    safe_total = jnp.where(live_grid, final_total, 1.0)
    result = jnp.where(live_grid[..., None], final_sum / safe_total[..., None], 0.0)
    return result.astype(jnp.bfloat16).reshape(token_rows, local_heads * 2 * HEAD)


def solution(mesh):
    in_specs = (P("seq", "tp"), P("seq", "tp"), P(("seq", "tp"), None), P(), P("seq"), P("seq"))
    out_specs = P("seq", "tp")
    return jax.shard_map(
        per_device, mesh=mesh, in_specs=in_specs, out_specs=out_specs, check_vma=False
    )
```

profile of v0, /device:TPU:1, one launch (start us, length us, event | category | flops | bytes accessed | tf_op | source)
XLA Modules:
  0.0 292.7 jit_solution(12591821938182171553)
XLA Ops:
  6.5 0.0 all-gather.3.cloned.1.call-start
  6.5 0.7 all-gather.3.cloned.1.call-update
  7.3 150.3 %all-gather.3.cloned.1.call-done = bf16[128,4,4096]{2,1,0:T(4,128)(2,1)} async-done(((bf16[1,4,4096]{2,1,0:T(4,128)(2,1)}), bf16[128,4,4096]{2,1,0:T(4,128)(2,1)}) %all-gather.3.cloned.1.call-update) | async-done | bytes 4194320 | tf_op jit(solution)/shard_map/all_gather | solution.py:84
  157.6 7.9 %all_to_all.12 = bf16[512,4,1024]{2,1,0:T(4,128)(2,1)} reshape(bf16[128,4,4096]{2,1,0:T(4,128)(2,1)} %all-gather.3.cloned.1.call-done) | data formatting | bytes 8388608 | tf_op jit(solution)/shard_map/all_to_all | solution.py:85
  165.4 5.5 %copy.96 = bf16[512,4,1024]{2,0,1:T(8,128)(2,1)} copy(bf16[512,4,1024]{2,1,0:T(4,128)(2,1)} %all_to_all.12) | data formatting | bytes 8388608 | tf_op jit(solution)/shard_map/all_to_all | solution.py:85
  170.9 0.0 copy-start.3
  170.9 0.0 copy-start
  170.9 0.0 copy-start.1
  170.9 0.0 copy-start.4
  171.0 0.0 copy-start.2
  171.0 5.0 %all-to-all-start = ((bf16[512,4,1024]{2,0,1:T(8,128)(2,1)}), bf16[512,4,1024]{2,0,1:T(8,128)(2,1)}, u32[]{:S(2)}, u32[]{:S(2)}) async-start(bf16[512,4,1024]{2,0,1:T(8,128)(2,1)} %copy.96), calls=%async_computation | async-start | bytes 8388608 | tf_op jit(solution)/shard_map/all_to_all | solution.py:85
  176.0 0.0 copy-done.3
  176.0 0.2 reduce-window.4
  176.2 0.6 slice.50
  176.7 0.0 copy-done
  176.7 0.2 reshape.520
  176.9 0.0 copy-done.1
  176.9 0.2 copy.114
  177.1 0.7 iota_compare_fusion.7
  177.8 0.1 convert_reduce_fusion
  177.9 0.0 copy-done.4
  177.9 0.1 select_reduce_fusion.4
  178.0 0.0 copy-done.2
  178.0 0.9 select_reduce_fusion
  178.9 0.1 fusion.62
  179.0 0.3 compare_and_fusion.2
  179.3 0.3 fusion.109
  179.6 89.3 %all-to-all-done = bf16[512,4,1024]{2,0,1:T(8,128)(2,1)} async-done(((bf16[512,4,1024]{2,0,1:T(8,128)(2,1)}), bf16[512,4,1024]{2,0,1:T(8,128)(2,1)}, u32[]{:S(2)}, u32[]{:S(2)}) %all-to-all-start) | async-done | bytes 4194336 | tf_op jit(solution)/shard_map/all_to_all | solution.py:85
  269.0 6.2 %copy.97 = bf16[512,4,1024]{0,2,1:T(8,128)(2,1)} copy(bf16[512,4,1024]{2,0,1:T(8,128)(2,1)} %all-to-all-done) | data formatting | bytes 8388608 | tf_op jit(solution)/shard_map/all_to_all | solution.py:85
  275.2 2.4 fusion.108
  277.6 0.5 fusion.1
  278.2 0.5 fusion.2
  278.7 0.5 fusion.3
  279.3 0.5 fusion
  279.8 0.5 fusion.4
  280.4 0.1 fusion.50
  280.5 0.5 fusion.10
  281.0 0.5 fusion.8
  281.5 0.5 fusion.6
  282.1 0.7 fusion.19
  282.8 0.7 fusion.17
  283.4 0.7 fusion.15
  284.1 0.7 fusion.13
  284.8 0.3 fusion.25
  285.1 0.9 copy.119
  (4 shorter events, 0.1 us)
Async XLA Ops:
  6.5 151.0 %all-gather.3.cloned.1.call-start = ((), (), s32[]{:S(2)}) async-start(), calls=%async_computation.1 | async-start | bytes 4227072 | tf_op jit(solution)/shard_map/all_gather | solution.py:84
  170.9 5.0 %copy-start.3 = (s32[4]{0:T(128)S(1)}, s32[4]{0:T(128)}, u32[]{:S(2)}) copy-start(s32[4]{0:T(128)} %param.10) | copy-start | bytes 52
  170.9 5.8 %copy-start = (bf16[128,1024]{1,0:T(8,128)(2,1)S(1)}, bf16[128,1024]{1,0:T(8,128)(2,1)}, u32[]{:S(2)}) copy-start(bf16[128,1024]{1,0:T(8,128)(2,1)} %param.6) | copy-start | bytes 786436
  170.9 6.0 %copy-start.1 = (bf16[128,1024]{1,0:T(8,128)(2,1)S(1)}, bf16[128,1024]{1,0:T(8,128)(2,1)}, u32[]{:S(2)}) copy-start(bf16[128,1024]{1,0:T(8,128)(2,1)} %param.7) | copy-start | bytes 786436
  170.9 6.9 %copy-start.4 = (s32[4]{0:T(128)S(1)}, s32[4]{0:T(128)}, u32[]{:S(2)}) copy-start(s32[4]{0:T(128)} %param.11) | copy-start | bytes 52
  171.0 7.0 %copy-start.2 = (s32[512]{0:T(512)S(1)}, s32[512]{0:T(512)}, u32[]{:S(2)}) copy-start(s32[512]{0:T(512)} %param.9) | copy-start | bytes 6148
  171.0 98.0 %all-to-all-start = ((bf16[512,4,1024]{2,0,1:T(8,128)(2,1)}), bf16[512,4,1024]{2,0,1:T(8,128)(2,1)}, u32[]{:S(2)}, u32[]{:S(2)}) async-start(bf16[512,4,1024]{2,0,1:T(8,128)(2,1)} %copy.96), calls=%async_computation | async-start | bytes 8388608 | tf_op jit(solution)/shard_map/all_to_all | solution.py:85
Sparse Core Ops, SparseCore 0:
  11.9 145.6 all-gather.2
where the time goes:
time: 293 us
  waiting for transfers between devices  240 us (82%)
  local copies, waits for them, and re-layouts  23.8 us (8%)
  between operations  13.6 us (5%)
  matrix products  5.38 us (2%)
  starting transfers between devices  5 us (2%)
  other arithmetic  4.64 us (2%)
    all_gather x1, waiting for transfers between devices, per_device(): gathered = lax.all_gather(prefix_cache, 'seq', axis=0, tiled=True)  150 us
    all_to_all x1, waiting for transfers between devices, per_device(): lax.all_to_all(gathered, 'tp', split_axis=1, concat_axis=0, tiled=True)  89.3 us
    all_to_all x3, local copies, waits for them, and re-layouts, per_device(): lax.all_to_all(gathered, 'tp', split_axis=1, concat_axis=0, tiled=True)  19.6 us
  transfers between devices with their start and end apart: 2, of which 2 were waited for; matrix products, arithmetic and copies ran while one was open for 1% of the time, Pallas kernels for 0%

commit v1 on v0

v1 whole, which is shorter than its diff:
```python
import math

import jax
import jax.numpy as jnp
import numpy as np
from jax import lax
from jax.sharding import Mesh
from jax.sharding import PartitionSpec as P

HEADS = 16
HEAD = 128

masked_score = -1e30

SEQ_PARTS = (("x", 4), ("zh", 2), ("y", 8), ("core", 2))
STAGES = (("x", "zh", "y"), ("core",))
TP_FIRST = "a2a"


def block_table(stages, per_block_rows, tensor_count):
    names = [n for n, _ in SEQ_PARTS]
    sizes = [s for _, s in SEQ_PARTS]
    coords = np.indices(sizes).reshape(len(sizes), -1).T
    seq_index = np.ravel_multi_index(coords.T, sizes)
    local = {}
    for c, s in zip(map(tuple, coords), seq_index):
        blocks = s * tensor_count + np.arange(tensor_count)
        local[c] = np.repeat(blocks, per_block_rows)
    gathered = set()
    for stage in stages:
        axes = [names.index(n) for n in stage]
        new = {}
        for c in local:
            parts = []
            for sub in np.ndindex(*[sizes[a] for a in axes]):
                other = list(c)
                for a, v in zip(axes, sub):
                    other[a] = v
                parts.append(local[tuple(other)])
            new[c] = np.concatenate(parts)
        local = new
        gathered.update(stage)
    tables = {tuple(v) for v in local.values()}
    assert len(tables) == 1
    return np.asarray(tables.pop(), np.int32)


def token_layout(lengths, prefixes, slots):
    cumulative = jnp.cumsum(lengths)
    slot_ids = jnp.arange(slots, dtype=jnp.int32)
    request_ids = jnp.sum((slot_ids[:, None] >= cumulative[None, :]).astype(jnp.int32), axis=1)
    live_slots = slot_ids < cumulative[-1]
    onehot = request_ids[:, None] == jnp.arange(lengths.shape[0], dtype=jnp.int32)[None, :]
    token_group = jnp.sum(jnp.where(onehot, prefixes[None, :], 0), axis=1)
    return (slot_ids, request_ids, live_slots, token_group)


def per_device(
    queries, suffix_entries, prefix_cache, block_prefix, request_lengths, request_prefix
):
    tensor_count = lax.axis_size("tp")
    local_heads = HEADS // tensor_count
    token_rows = queries.shape[0]
    block_rows = prefix_cache.shape[0]
    column_count = prefix_cache.shape[1] // tensor_count
    slot_ids, request_ids, live_slots, token_group = token_layout(
        request_lengths, request_prefix, token_rows
    )
    if TP_FIRST == "a2a":
        mine = lax.all_to_all(prefix_cache, "tp", split_axis=1, concat_axis=0, tiled=True)
    else:
        whole = lax.all_gather(prefix_cache, "tp", axis=0, tiled=True)
        start = lax.axis_index("tp") * column_count
        mine = lax.dynamic_slice_in_dim(whole, start, column_count, 1)
    for stage in STAGES:
        mine = lax.all_gather(mine, stage, axis=0, tiled=True)
    cached = mine.reshape(-1, local_heads, 2, HEAD)
    table = jnp.asarray(block_table(STAGES, block_rows, tensor_count))
    owners = jnp.take(block_prefix, table)

    query_rows = queries.reshape(token_rows, local_heads, 2, HEAD)
    own_entries = suffix_entries.reshape(token_rows, local_heads, 2, HEAD)
    scale = 1.0 / math.sqrt(HEAD)
    prefix_scores = jnp.einsum(
        "thed,phd->thep", query_rows, cached[:, :, 0], preferred_element_type=jnp.float32
    ) * scale
    suffix_scores = jnp.einsum(
        "thed,uhd->theu", query_rows, own_entries[:, :, 0], preferred_element_type=jnp.float32
    ) * scale
    prefix_allowed = ((token_group[:, None] == owners[None, :]) & live_slots[:, None])[:, None, None, :]
    suffix_allowed = (
        (request_ids[:, None] == request_ids[None, :])
        & (slot_ids[None, :] <= slot_ids[:, None])
        & live_slots[:, None]
    )[:, None, None, :]
    prefix_scores = jnp.where(prefix_allowed, prefix_scores, masked_score)
    suffix_scores = jnp.where(suffix_allowed, suffix_scores, masked_score)
    row_max = jnp.maximum(jnp.max(prefix_scores, axis=-1), jnp.max(suffix_scores, axis=-1))
    prefix_weight = jnp.where(prefix_allowed, jnp.exp(prefix_scores - row_max[..., None]), 0.0)
    suffix_weight = jnp.where(suffix_allowed, jnp.exp(suffix_scores - row_max[..., None]), 0.0)
    total_weight = jnp.sum(prefix_weight, axis=-1) + jnp.sum(suffix_weight, axis=-1)
    weighted = jnp.einsum(
        "thep,phd->thed", prefix_weight.astype(jnp.bfloat16), cached[:, :, 1],
        preferred_element_type=jnp.float32,
    )
    weighted = weighted + jnp.einsum(
        "theu,uhd->thed", suffix_weight.astype(jnp.bfloat16), own_entries[:, :, 1],
        preferred_element_type=jnp.float32,
    )
    live_grid = live_slots[:, None, None]
    safe_total = jnp.where(live_grid, total_weight, 1.0)
    result = jnp.where(live_grid[..., None], weighted / safe_total[..., None], 0.0)
    return result.astype(jnp.bfloat16).reshape(token_rows, local_heads * 2 * HEAD)


def solution(mesh):
    sizes = tuple(s for _, s in SEQ_PARTS) + (mesh.shape["tp"],)
    names = tuple(n for n, _ in SEQ_PARTS) + ("tp",)
    fine = Mesh(mesh.devices.reshape(sizes), names)
    seq = names[:-1]
    in_specs = (P(seq, "tp"), P(seq, "tp"), P(seq + ("tp",), None), P(), P(seq), P(seq))
    out_specs = P(seq, "tp")
    return jax.shard_map(
        per_device, mesh=fine, in_specs=in_specs, out_specs=out_specs, check_vma=False
    )
```

time: 293 us -> 203 us (0.69)
  waiting for transfers between devices: 240 us -> 142 us
  blocking collectives: 0 us -> 12.4 us
  starting transfers between devices: 5 us -> 0.04 us
    all_to_all x1 -> x0, waiting for transfers between devices: 89.3 us -> none  [per_device(): lax.all_to_all(gathered, 'tp', split_axis=1, concat_axis=0, tiled=True)]
    all_to_all x3 -> x1, local copies, waits for them, and re-layouts: 19.6 us -> 0.63 us  [per_device(): lax.all_to_all(prefix_cache, 'tp', split_axis=1, concat_axis=0, tiled=True)]
    gather x0 -> x1, local copies, waits for them, and re-layouts: none -> 13.2 us  [per_device(): owners = jnp.take(block_prefix, table)]
    all_to_all x0 -> x1, blocking collectives: none -> 12.4 us  [per_device(): lax.all_to_all(prefix_cache, 'tp', split_axis=1, concat_axis=0, tiled=True)]
    all_gather x1 -> x2, waiting for transfers between devices: 150 us -> 142 us  [per_device(): mine = lax.all_gather(mine, stage, axis=0, tiled=True)]
    all_gather x0 -> x1, local copies, waits for them, and re-layouts: none -> 6.52 us  [per_device(): mine = lax.all_gather(mine, stage, axis=0, tiled=True)]
    all_to_all x1 -> x0, starting transfers between devices: 5 us -> none  [per_device(): lax.all_to_all(gathered, 'tp', split_axis=1, concat_axis=0, tiled=True)]
    dot_general x10 -> x4, matrix products: 5.38 us -> 5.95 us  [the longest x1 3.34 us: per_device(): jnp.einsum('thed,phd->thep', query_rows, cached[:, :, 0], preferred_eleme...]
  transfers between devices with their start and end apart: 2 -> 2, of which waited for: 2 -> 2; matrix products, arithmetic and copies ran while one was open for 1% -> 9% of each run, Pallas kernels for 0% -> 0%
where the time goes in v1:
time: 203 us
  waiting for transfers between devices  142 us (70%)
  local copies, waits for them, and re-layouts  24 us (12%)
  between operations  13.5 us (7%)
  blocking collectives  12.4 us (6%)
  matrix products  5.95 us (3%)
  other arithmetic  4.94 us (2%)
    all_gather x2, waiting for transfers between devices, per_device(): mine = lax.all_gather(mine, stage, axis=0, tiled=True)  142 us
    gather x1, local copies, waits for them, and re-layouts, per_device(): owners = jnp.take(block_prefix, table)  13.2 us
    all_to_all x1, blocking collectives, per_device(): lax.all_to_all(prefix_cache, 'tp', split_axis=1, concat_axis=0, tiled=True)  12.4 us
    all_gather x1, local copies, waits for them, and re-layouts, per_device(): mine = lax.all_gather(mine, stage, axis=0, tiled=True)  6.52 us
  transfers between devices with their start and end apart: 2, of which 2 were waited for; matrix products, arithmetic and copies ran while one was open for 9% of the time, Pallas kernels for 0%

profile of v1, /device:TPU:1, one launch (start us, length us, event | category | flops | bytes accessed | tf_op | source)
XLA Modules:
  0.0 202.8 jit_solution(8286302683828630251)
XLA Ops:
  6.5 0.0 copy-start
  6.5 0.0 copy-start.2
  6.5 0.0 all-gather.3.cloned.1.call-start
  6.5 12.4 %all_to_all.19 = bf16[4,4,1024]{2,0,1:T(4,128)(2,1)S(1)} all-to-all(bf16[4,4,1024]{2,0,1:T(4,128)(2,1)} %bitcast.71), channel_id=1, replica_groups=mesh['x'=4,'zh'=2,'y'=8,'core'=2,'tp'=4] {'tp'}, dimensions={1} | all-to-all | bytes 65536 | tf_op jit(solution)/shard_map/all_to_all | solution.py:70
  19.0 0.6 all_to_all.17
  19.6 0.0 all-gather.3.cloned.1.call-update
  19.6 0.0 all-gather.5.cloned.1.call-start
  19.7 137.8 %all-gather.3.cloned.1.call-done = bf16[1024,1024]{1,0:T(8,128)(2,1)} async-done(((bf16[16,1024]{1,0:T(8,128)(2,1)}), bf16[1024,1024]{1,0:T(8,128)(2,1)}) %all-gather.3.cloned.1.call-update) | async-done | bytes 2097168 | tf_op jit(solution)/shard_map/all_gather | solution.py:76
  157.5 0.0 all-gather.5.cloned.1.call-update
  157.5 0.8 reduce-window.4
  158.3 0.6 slice.16
  158.9 1.1 reshape.140
  160.0 1.1 copy.31
  161.2 0.7 broadcast_clamp_fusion
  161.9 0.0 copy-done
  161.9 13.2 %gather_fusion = s32[2048]{0:T(1024)S(1)} fusion(s32[512]{0:T(512)S(1)} %copy-done, s32[2048]{0:T(1024)S(1)} %broadcast_clamp_fusion), kind=kCustom, calls=%fused_computation | custom fusion | bytes 24576 | tf_op jit(solution)/shard_map/jit(_take)/gather | solution.py:79
  175.1 0.7 iota_compare_fusion.3
  175.7 0.1 convert_reduce_fusion
  175.8 0.0 copy-done.2
  175.8 0.1 select_reduce_fusion
  175.9 0.1 fusion.22
  176.0 0.3 fusion.27
  176.3 0.3 compare_and_fusion
  176.6 4.1 %all-gather.5.cloned.1.call-done = bf16[2048,1024]{1,0:T(8,128)(2,1)} async-done(((bf16[1024,1024]{1,0:T(8,128)(2,1)}), bf16[2048,1024]{1,0:T(8,128)(2,1)}) %all-gather.5.cloned.1.call-update) | async-done | bytes 4194320 | tf_op jit(solution)/shard_map/all_gather | solution.py:76
  180.7 6.5 %copy.28 = bf16[2048,1024]{0,1:T(8,128)(2,1)} copy(bf16[2048,1024]{1,0:T(8,128)(2,1)} %all-gather.5.cloned.1.call-done) | data formatting | bytes 8388608 | tf_op jit(solution)/shard_map/all_gather | solution.py:76
  187.3 0.0 copy-start.1
  187.3 3.3 %fusion = (f32[128,4,2]{0,2,1:T(2,128)S(1)}, f32[4,2048,128,2]{2,1,3,0:T(8,128)S(1)}) fusion(pred[128,2048]{0,1:T(8,128)(4,1)S(1)} %compare_and_fusion, bf16[128,4,2,128]{3,2,1,0:T(2,128)(2,1)S(1)} %reshape.140, bf16[2048,4,2,128]{0,3,2,1:T(8,128)(2,1)} %bitcast.65), kind=kOutput, calls=%fused_computation.3 | convolution fusion | flops 543161344 | bytes 11014144 | tf_op jit(solution)/shard_map/thed,phd->thep/dot_general | solution.py:84
  190.6 0.0 copy-done.1
  190.6 2.1 %fusion.3 = f32[4,128,2,128]{1,3,2,0:T(8,128)S(1)} fusion(f32[4,2048,128,2]{2,1,3,0:T(8,128)S(1)} %get-tuple-element.6, f32[128,4,2]{0,2,1:T(2,128)S(1)} %max.7, pred[128,2048]{0,1:T(8,128)(4,1)S(1)} %compare_and_fusion, bf16[2048,4,2,128]{0,3,2,1:T(8,128)(2,1)S(1)} %bitcast.66), kind=kOutput, calls=%fused_computation.6 | convolution fusion | flops 547356672 | bytes 11276288 | tf_op jit(solution)/shard_map/thep,phd->thed/dot_general | solution.py:102
  192.7 2.0 %fusion.1 = f32[128,4,2]{0,2,1:T(2,128)S(1)} fusion(f32[4,2048,128,2]{2,1,3,0:T(8,128)S(1)} %get-tuple-element.6, f32[128,4,2]{0,2,1:T(2,128)S(1)} %max.7, pred[128,2048]{0,1:T(8,128)(4,1)S(1)} %compare_and_fusion), kind=kLoop, calls=%fused_computation.4 | loop fusion | flops 10484736 | bytes 8658944 | tf_op jit(solution)/shard_map/reduce_sum | solution.py:101
  194.7 0.1 fusion.13
  194.9 0.3 fusion.12
  195.1 0.9 copy.38
  (2 shorter events, 0.0 us)
Async XLA Ops:
  6.5 155.3 %copy-start = (s32[512]{0:T(512)S(1)}, s32[512]{0:T(512)}, u32[]{:S(2)}) copy-start(s32[512]{0:T(512)} %param.10) | copy-start | bytes 6148
  6.5 169.3 %copy-start.2 = (s32[4]{0:T(128)S(1)}, s32[4]{0:T(128)}, u32[]{:S(2)}) copy-start(s32[4]{0:T(128)} %param.12) | copy-start | bytes 52
  6.5 150.9 %all-gather.3.cloned.1.call-start = ((), (), s32[]{:S(2)}) async-start(), calls=%async_computation.1 | async-start | bytes 2129920 | tf_op jit(solution)/shard_map/all_gather | solution.py:76
  19.6 161.1 %all-gather.5.cloned.1.call-start = ((), (), s32[]{:S(2)}) async-start(), calls=%async_computation.2 | async-start | bytes 6291456 | tf_op jit(solution)/shard_map/all_gather | solution.py:76
  187.3 3.4 %copy-start.1 = (bf16[2048,1024]{0,1:T(8,128)(2,1)S(1)}, bf16[2048,1024]{0,1:T(8,128)(2,1)}, u32[]{:S(2)}) copy-start(bf16[2048,1024]{0,1:T(8,128)(2,1)} %copy.28) | copy-start | bytes 12582916
Sparse Core Ops, SparseCore 0:
  19.7 137.6 all-gather.2
  159.6 21.1 all-gather.4

commit v2 on v1

--- a/solution.py
+++ b/solution.py
@@ -13,36 +13,29 @@
 masked_score = -1e30
 
 SEQ_PARTS = (("x", 4), ("zh", 2), ("y", 8), ("core", 2))
-STAGES = (("x", "zh", "y"), ("core",))
-TP_FIRST = "a2a"
 
 
-def block_table(stages, per_block_rows, tensor_count):
-    names = [n for n, _ in SEQ_PARTS]
-    sizes = [s for _, s in SEQ_PARTS]
-    coords = np.indices(sizes).reshape(len(sizes), -1).T
-    seq_index = np.ravel_multi_index(coords.T, sizes)
-    local = {}
-    for c, s in zip(map(tuple, coords), seq_index):
-        blocks = s * tensor_count + np.arange(tensor_count)
-        local[c] = np.repeat(blocks, per_block_rows)
-    gathered = set()
-    for stage in stages:
-        axes = [names.index(n) for n in stage]
-        new = {}
-        for c in local:
-            parts = []
-            for sub in np.ndindex(*[sizes[a] for a in axes]):
-                other = list(c)
-                for a, v in zip(axes, sub):
-                    other[a] = v
-                parts.append(local[tuple(other)])
-            new[c] = np.concatenate(parts)
-        local = new
-        gathered.update(stage)
-    tables = {tuple(v) for v in local.values()}
-    assert len(tables) == 1
-    return np.asarray(tables.pop(), np.int32)
+def gather_cache(prefix_cache, block_prefix, tensor_count):
+    block_rows, width = prefix_cache.shape
+    column_count = width // tensor_count
+    far = ("x", "zh", "y", "tp")
+    peers = 1
+    for name, size in SEQ_PARTS:
+        if name != "core":
+            peers *= size
+    parts = prefix_cache.reshape(block_rows, tensor_count, column_count).transpose(1, 0, 2)
+    outgoing = jnp.broadcast_to(parts[None], (peers,) + parts.shape).reshape(-1, column_count)
+    mine = lax.all_to_all(outgoing, far, split_axis=0, concat_axis=0, tiled=True)
+    other = lax.ppermute(mine, "core", [(0, 1), (1, 0)])
+    sizes = [s for _, s in SEQ_PARTS] + [tensor_count]
+    grid = block_prefix.reshape(sizes)
+    core = lax.axis_index("core")
+    core_axis = [n for n, _ in SEQ_PARTS].index("core")
+    own_owner = jnp.take(grid, core, axis=core_axis).reshape(-1)
+    other_owner = jnp.take(grid, 1 - core, axis=core_axis).reshape(-1)
+    owners = jnp.repeat(jnp.concatenate([own_owner, other_owner]), block_rows)
+    cached = jnp.concatenate([mine, other])
+    return cached, owners
 
 
 def token_layout(lengths, prefixes, slots):
@@ -66,17 +59,8 @@
     slot_ids, request_ids, live_slots, token_group = token_layout(
         request_lengths, request_prefix, token_rows
     )
-    if TP_FIRST == "a2a":
-        mine = lax.all_to_all(prefix_cache, "tp", split_axis=1, concat_axis=0, tiled=True)
-    else:
-        whole = lax.all_gather(prefix_cache, "tp", axis=0, tiled=True)
-        start = lax.axis_index("tp") * column_count
-        mine = lax.dynamic_slice_in_dim(whole, start, column_count, 1)
-    for stage in STAGES:
-        mine = lax.all_gather(mine, stage, axis=0, tiled=True)
-    cached = mine.reshape(-1, local_heads, 2, HEAD)
-    table = jnp.asarray(block_table(STAGES, block_rows, tensor_count))
-    owners = jnp.take(block_prefix, table)
+    cached, owners = gather_cache(prefix_cache, block_prefix, tensor_count)
+    cached = cached.reshape(-1, local_heads, 2, HEAD)
 
     query_rows = queries.reshape(token_rows, local_heads, 2, HEAD)
     own_entries = suffix_entries.reshape(token_rows, local_heads, 2, HEAD)

time: 203 us -> 108 us (0.53)
  waiting for transfers between devices: 142 us -> 0.01 us
  blocking collectives: 12.4 us -> 74 us
  between operations: 13.5 us -> 0.26 us
  starting transfers between devices: 0.04 us -> 5.78 us
  local copies, waits for them, and re-layouts: 24 us -> 18.3 us
    all_gather x2 -> x0, waiting for transfers between devices: 142 us -> none  [per_device(): mine = lax.all_gather(mine, stage, axis=0, tiled=True)]
    all_to_all x1, blocking collectives: 12.4 us -> 74 us  [gather_cache(): lax.all_to_all(outgoing, far, split_axis=0, concat_axis=0, tiled=True)]
    gather x1 -> x0, local copies, waits for them, and re-layouts: 13.2 us -> none  [per_device(): owners = jnp.take(block_prefix, table)]
    concatenate x0 -> x3, local copies, waits for them, and re-layouts: none -> 8.07 us  [gather_cache(): cached = jnp.concatenate([mine, other])]
    all_gather x1 -> x0, local copies, waits for them, and re-layouts: 6.52 us -> none  [per_device(): mine = lax.all_gather(mine, stage, axis=0, tiled=True)]
    ppermute x0 -> x1, starting transfers between devices: none -> 5.78 us  [gather_cache(): other = lax.ppermute(mine, 'core', [(0, 1), (1, 0)])]
    ppermute x0 -> x1, local copies, waits for them, and re-layouts: none -> 3.96 us  [gather_cache(): other = lax.ppermute(mine, 'core', [(0, 1), (1, 0)])]
  transfers between devices with their start and end apart: 2 -> 1, of which waited for: 2 -> 0; matrix products, arithmetic and copies ran while one was open for 9% -> 7% of each run, Pallas kernels for 0% -> 0%
where the time goes in v2:
time: 108 us
  blocking collectives  74 us (69%)
  local copies, waits for them, and re-layouts  18.3 us (17%)
  starting transfers between devices  5.78 us (5%)
  matrix products  5.56 us (5%)
  other arithmetic  3.66 us (3%)
    all_to_all x1, blocking collectives, gather_cache(): lax.all_to_all(outgoing, far, split_axis=0, concat_axis=0, tiled=True)  74 us
    concatenate x3, local copies, waits for them, and re-layouts, gather_cache(): cached = jnp.concatenate([mine, other])  8.07 us
    ppermute x1, starting transfers between devices, gather_cache(): other = lax.ppermute(mine, 'core', [(0, 1), (1, 0)])  5.78 us
    ppermute x1, local copies, waits for them, and re-layouts, gather_cache(): other = lax.ppermute(mine, 'core', [(0, 1), (1, 0)])  3.96 us
    dot_general x1, matrix products, per_device(): jnp.einsum('thed,phd->thep', query_rows, cached[:, :, 0], preferred_eleme...  2.56 us
    dot_general x1, matrix products, per_device(): jnp.einsum('thep,phd->thed', prefix_weight.astype(jnp.bfloat16), cached[:...  2.47 us
  transfers between devices with their start and end apart: 1, of which 0 were waited for; matrix products, arithmetic and copies ran while one was open for 7% of the time, Pallas kernels for 0%

profile of v2, /device:TPU:1, one launch (start us, length us, event | category | flops | bytes accessed | tf_op | source)
XLA Modules:
  0.0 107.6 jit_solution(15354426319159227902)
XLA Ops:
  0.0 0.8 reshape.148
  0.8 1.0 broadcast_in_dim.107
  1.8 0.0 copy-start.1
  1.8 0.0 copy-start.2
  1.9 0.0 copy-start.4
  1.9 0.0 copy-start.3
  1.9 0.0 copy-start.5
  1.9 74.0 %all_to_all.12 = bf16[256,4,1024]{2,1,0:T(4,128)(2,1)S(1)} all-to-all(bf16[256,4,1024]{2,1,0:T(4,128)(2,1)S(1)} %bitcast.93), channel_id=1, replica_groups=mesh['x'=4,'zh'=2,'y'=8,'core'=2,'tp'=4] {'x','zh','y','tp'}, dimensions={0} | all-to-all | bytes 4194304 | tf_op jit(solution)/shard_map/all_to_all | solution.py:28
  75.9 2.0 %all_to_all.10 = bf16[1024,1024]{1,0:T(8,128)(2,1)} reshape(bf16[256,4,1024]{2,1,0:T(4,128)(2,1)S(1)} %all_to_all.12) | data formatting | bytes 4194304 | tf_op jit(solution)/shard_map/all_to_all | solution.py:28
  77.9 5.8 %collective-permute-start = (bf16[1024,1024]{1,0:T(8,128)(2,1)}, bf16[1024,1024]{1,0:T(8,128)(2,1)}, u32[]{:S(2)}, u32[]{:S(2)}) collective-permute-start(bf16[1024,1024]{1,0:T(8,128)(2,1)} %all_to_all.10), channel_id=1, source_target_pairs={{0,4},{4,0},{1,5},{5,1},{2,6},{6,2},{3,7},{7,3},{8,12},{12,8},{9,1... | collective-permute-start | bytes 6291464 | tf_op jit(solution)/shard_map/ppermute | solution.py:29
  83.7 0.0 copy-done.1
  83.7 0.2 reshape.152
  83.9 0.0 copy-done.2
  83.9 0.2 copy.46
  84.1 0.0 copy-done.4
  84.1 0.2 reduce-window.4
  84.3 0.6 slice.16
  84.9 0.0 copy-done.3
  84.9 0.1 reshape.149
  85.0 0.1 broadcast_select_fusion.1
  85.1 0.1 reshape.151
  85.2 0.1 reshape.150
  85.3 0.1 broadcast_in_dim.110
  85.5 0.2 eq.53
  85.6 0.7 iota_compare_fusion.3
  86.3 0.1 convert_reduce_fusion
  86.4 0.0 copy-done.5
  86.4 0.1 select_reduce_fusion
  86.5 0.1 fusion.49
  86.6 0.3 fusion.56
  86.9 0.3 compare_and_fusion
  87.2 2.3 %concatenate.11 = bf16[1024,4,2,128]{3,2,1,0:T(2,128)(2,1)} reshape(bf16[256,4,1024]{2,1,0:T(4,128)(2,1)S(1)} %all_to_all.12) | data formatting | bytes 4194304 | tf_op jit(solution)/shard_map/concatenate | solution.py:37
  89.5 1.9 %copy.43 = bf16[1024,4,2,128]{3,0,1,2:T(8,128)(2,1)S(1)} copy(bf16[1024,4,2,128]{3,2,1,0:T(2,128)(2,1)} %concatenate.11) | data formatting | bytes 4194304 | tf_op jit(solution)/shard_map/concatenate | solution.py:37
  91.3 0.0 collective-permute-done
  91.3 4.0 %copy.42 = bf16[1024,1024]{0,1:T(8,128)(2,1)} copy(bf16[1024,1024]{1,0:T(8,128)(2,1)} %collective-permute-done) | data formatting | bytes 4194304 | tf_op jit(solution)/shard_map/ppermute | solution.py:29
  95.3 4.0 %copy.44 = bf16[1024,4,2,128]{3,0,1,2:T(8,128)(2,1)} copy(bf16[1024,4,2,128]{0,3,2,1:T(8,128)(2,1)} %bitcast.94) | data formatting | bytes 4194304 | tf_op jit(solution)/shard_map/concatenate | solution.py:37
  99.3 2.6 %fusion = (f32[128,4,2]{0,2,1:T(2,128)S(1)}, f32[4,2048,128,2]{2,1,3,0:T(8,128)S(1)}) fusion(pred[128,2048]{0,1:T(8,128)(4,1)S(1)} %compare_and_fusion, bf16[128,4,2,128]{3,2,1,0:T(2,128)(2,1)S(1)} %reshape.152, bf16[1024,4,2,128]{3,0,1,2:T(8,128)(2,1)} %copy.44, bf16[1024,4,2,128]{3,0,1,2:T(8,128)(2,1)S(1)} %copy.43), kind=kOutput, calls=%fused_computation.2 | convolution fusion | flops 547355648 | bytes 13111296 | tf_op jit(solution)/shard_map/thed,phd->thep/dot_general | solution.py:68
  101.8 0.2 convolution_bitcast_fusion
  102.1 0.1 fusion.40
  102.2 0.0 copy-start
  102.2 2.0 %fusion.1 = f32[128,4,2]{0,2,1:T(2,128)S(1)} fusion(f32[4,2048,128,2]{2,1,3,0:T(8,128)S(1)} %get-tuple-element.20, f32[128,4,2]{0,2,1:T(2,128)S(1)} %max.7, pred[128,2048]{0,1:T(8,128)(4,1)S(1)} %compare_and_fusion), kind=kLoop, calls=%fused_computation.3 | loop fusion | flops 10484736 | bytes 8658944 | tf_op jit(solution)/shard_map/reduce_sum | solution.py:85
  104.3 0.0 copy-done
  104.3 2.5 %fusion.35 = bf16[128,4,2,128]{0,3,2,1:T(8,128)(2,1)S(1)} fusion(f32[128,4,2,128]{0,3,2,1:T(8,128)S(1)} %convolution_bitcast_fusion, f32[4,2048,128,2]{2,1,3,0:T(8,128)S(1)} %get-tuple-element.20, f32[128,4,2]{0,2,1:T(2,128)S(1)} %max.7, pred[128,2048]{0,1:T(8,128)(4,1)S(1)} %compare_and_fusion, bf16[1024,4,2,128]{3,0,1,2:T(8,128)(2,1)S(1)} %copy.43, ...), kind=kOutput, calls=%fused_computation.24 | convolution fusion | flops 552075264 | bytes 13639808 | tf_op jit(solution)/shard_map/thep,phd->thed/dot_general | solution.py:86
  106.7 0.9 copy.53
  (4 shorter events, 0.0 us)
Async XLA Ops:
  1.8 81.9 %copy-start.1 = (bf16[128,1024]{1,0:T(8,128)(2,1)S(1)}, bf16[128,1024]{1,0:T(8,128)(2,1)}, u32[]{:S(2)}) copy-start(bf16[128,1024]{1,0:T(8,128)(2,1)} %param.8) | copy-start | bytes 786436
  1.8 82.1 %copy-start.2 = (bf16[128,1024]{1,0:T(8,128)(2,1)S(1)}, bf16[128,1024]{1,0:T(8,128)(2,1)}, u32[]{:S(2)}) copy-start(bf16[128,1024]{1,0:T(8,128)(2,1)} %param.9) | copy-start | bytes 786436
  1.9 82.2 %copy-start.4 = (s32[4]{0:T(128)S(1)}, s32[4]{0:T(128)}, u32[]{:S(2)}) copy-start(s32[4]{0:T(128)} %param.12) | copy-start | bytes 52
  1.9 83.0 %copy-start.3 = (s32[512]{0:T(512)S(1)}, s32[512]{0:T(512)}, u32[]{:S(2)}) copy-start(s32[512]{0:T(512)} %param.11) | copy-start | bytes 6148
  1.9 84.5 %copy-start.5 = (s32[4]{0:T(128)S(1)}, s32[4]{0:T(128)}, u32[]{:S(2)}) copy-start(s32[4]{0:T(128)} %param.13) | copy-start | bytes 52
  77.9 13.4 %collective-permute-start = (bf16[1024,1024]{1,0:T(8,128)(2,1)}, bf16[1024,1024]{1,0:T(8,128)(2,1)}, u32[]{:S(2)}, u32[]{:S(2)}) collective-permute-start(bf16[1024,1024]{1,0:T(8,128)(2,1)} %all_to_all.10), channel_id=1, source_target_pairs={{0,4},{4,0},{1,5},{5,1},{2,6},{6,2},{3,7},{7,3},{8,12},{12,8},{9,1... | collective-permute-start | bytes 6291464 | tf_op jit(solution)/shard_map/ppermute | solution.py:29
  102.2 2.1 %copy-start = (bf16[1024,4,2,128]{3,0,1,2:T(8,128)(2,1)S(1)}, bf16[1024,4,2,128]{3,0,1,2:T(8,128)(2,1)}, u32[]{:S(2)}) copy-start(bf16[1024,4,2,128]{3,0,1,2:T(8,128)(2,1)} %copy.44) | copy-start | bytes 6291460

commit v3 on v2

v3 whole, which is shorter than its diff:
```python
import math

import jax
import jax.numpy as jnp
import numpy as np
from jax import lax
from jax.sharding import Mesh
from jax.sharding import PartitionSpec as P

HEADS = 16
HEAD = 128

masked_score = -1e30

SEQ_PARTS = (("x", 4), ("zh", 2), ("y", 8), ("core", 2))


def spread(held, axes, count):
    outgoing = jnp.broadcast_to(held[None], (count,) + held.shape)
    return lax.all_to_all(outgoing, axes, split_axis=0, concat_axis=3, tiled=True)[0]


def gather_cache(prefix_cache, block_prefix, tensor_count, local_heads):
    block_rows = prefix_cache.shape[0]
    size = dict(SEQ_PARTS)
    local = prefix_cache.reshape(block_rows, tensor_count, local_heads, 2, HEAD).transpose(1, 3, 2, 0, 4)
    outgoing = jnp.broadcast_to(local[None], (size["zh"],) + local.shape)
    outgoing = outgoing.reshape((size["zh"] * tensor_count,) + local.shape[1:])
    mine = lax.all_to_all(outgoing, ("zh", "tp"), split_axis=0, concat_axis=3, tiled=True)[0]
    mine = spread(mine, ("y",), size["y"])
    mine = spread(mine, ("x",), size["x"])
    other = lax.ppermute(mine, "core", [(0, 1), (1, 0)])
    grid = block_prefix.reshape(size["x"], size["zh"], size["y"], size["core"], tensor_count)
    grid = grid.transpose(0, 2, 1, 3, 4)
    core = lax.axis_index("core")
    own_owner = jnp.repeat(jnp.take(grid, core, axis=3).reshape(-1), block_rows)
    other_owner = jnp.repeat(jnp.take(grid, 1 - core, axis=3).reshape(-1), block_rows)
    return (mine, own_owner), (other, other_owner)


def token_layout(lengths, prefixes, slots):
    cumulative = jnp.cumsum(lengths)
    slot_ids = jnp.arange(slots, dtype=jnp.int32)
    request_ids = jnp.sum((slot_ids[:, None] >= cumulative[None, :]).astype(jnp.int32), axis=1)
    live_slots = slot_ids < cumulative[-1]
    onehot = request_ids[:, None] == jnp.arange(lengths.shape[0], dtype=jnp.int32)[None, :]
    token_group = jnp.sum(jnp.where(onehot, prefixes[None, :], 0), axis=1)
    return (slot_ids, request_ids, live_slots, token_group)


def per_device(
    queries, suffix_entries, prefix_cache, block_prefix, request_lengths, request_prefix
):
    tensor_count = lax.axis_size("tp")
    local_heads = HEADS // tensor_count
    token_rows = queries.shape[0]
    block_rows = prefix_cache.shape[0]
    column_count = prefix_cache.shape[1] // tensor_count
    slot_ids, request_ids, live_slots, token_group = token_layout(
        request_lengths, request_prefix, token_rows
    )
    halves = gather_cache(prefix_cache, block_prefix, tensor_count, local_heads)

    query_rows = queries.reshape(token_rows, local_heads, 2, HEAD)
    own_entries = suffix_entries.reshape(token_rows, local_heads, 2, HEAD)
    scale = 1.0 / math.sqrt(HEAD)
    suffix_allowed = (
        (request_ids[:, None] == request_ids[None, :])
        & (slot_ids[None, :] <= slot_ids[:, None])
        & live_slots[:, None]
    )[:, None, None, :]
    suffix_scores = jnp.einsum(
        "thed,uhd->theu", query_rows, own_entries[:, :, 0], preferred_element_type=jnp.float32
    ) * scale
    suffix_scores = jnp.where(suffix_allowed, suffix_scores, masked_score)
    parts = []
    row_max = jnp.max(suffix_scores, axis=-1)
    for rows, owners in halves:
        allowed = ((token_group[:, None] == owners[None, :]) & live_slots[:, None])[:, None, None, :]
        scores = jnp.einsum(
            "thed,hpd->thep", query_rows, rows[0], preferred_element_type=jnp.float32
        ) * scale
        scores = jnp.where(allowed, scores, masked_score)
        row_max = jnp.maximum(row_max, jnp.max(scores, axis=-1))
        parts.append((scores, allowed, rows[1]))
    suffix_weight = jnp.where(suffix_allowed, jnp.exp(suffix_scores - row_max[..., None]), 0.0)
    total_weight = jnp.sum(suffix_weight, axis=-1)
    weighted = jnp.einsum(
        "theu,uhd->thed", suffix_weight.astype(jnp.bfloat16), own_entries[:, :, 1],
        preferred_element_type=jnp.float32,
    )
    for scores, allowed, values in parts:
        weight = jnp.where(allowed, jnp.exp(scores - row_max[..., None]), 0.0)
        total_weight = total_weight + jnp.sum(weight, axis=-1)
        weighted = weighted + jnp.einsum(
            "thep,hpd->thed", weight.astype(jnp.bfloat16), values,
            preferred_element_type=jnp.float32,
        )
    live_grid = live_slots[:, None, None]
    safe_total = jnp.where(live_grid, total_weight, 1.0)
    result = jnp.where(live_grid[..., None], weighted / safe_total[..., None], 0.0)
    return result.astype(jnp.bfloat16).reshape(token_rows, local_heads * 2 * HEAD)


def solution(mesh):
    sizes = tuple(s for _, s in SEQ_PARTS) + (mesh.shape["tp"],)
    names = tuple(n for n, _ in SEQ_PARTS) + ("tp",)
    fine = Mesh(mesh.devices.reshape(sizes), names)
    seq = names[:-1]
    in_specs = (P(seq, "tp"), P(seq, "tp"), P(seq + ("tp",), None), P(), P(seq), P(seq))
    out_specs = P(seq, "tp")
    return jax.shard_map(
        per_device, mesh=fine, in_specs=in_specs, out_specs=out_specs, check_vma=False
    )
```

time: 108 us -> 94.8 us (0.88)
  blocking collectives: 74 us -> 64.9 us
  local copies, waits for them, and re-layouts: 18.3 us -> 9.27 us
  matrix products: 5.56 us -> 8.33 us
  starting transfers between devices: 5.78 us -> 7.26 us
    all_to_all x1 -> x3, blocking collectives: 74 us -> 64.9 us  [the longest x2 47 us: spread(): lax.all_to_all(outgoing, axes, split_axis=0, concat_axis=3, tiled=True)[0]]
    concatenate x3 -> x0, local copies, waits for them, and re-layouts: 8.07 us -> none  [gather_cache(): cached = jnp.concatenate([mine, other])]
    ppermute x1 -> x0, local copies, waits for them, and re-layouts: 3.96 us -> none  [gather_cache(): other = lax.ppermute(mine, 'core', [(0, 1), (1, 0)])]
    slice x0 -> x3, local copies, waits for them, and re-layouts: none -> 2.92 us  [the longest x2 2.84 us: per_device(): parts.append((scores, allowed, rows[1]))]
    ppermute x1, starting transfers between devices: 5.78 us -> 7.26 us  [gather_cache(): other = lax.ppermute(mine, 'core', [(0, 1), (1, 0)])]
    dot_general x1, matrix products: 0.29 us -> 1.67 us  [per_device(): jnp.einsum('thed,uhd->theu', query_rows, own_entries[:, :, 0], preferred_...]
    dot_general x2 -> x4, matrix products: 5.03 us -> 6.41 us  [the longest x2 3.65 us: per_device(): jnp.einsum('thep,hpd->thed', weight.astype(jnp.bfloat16), values, preferr...]
  transfers between devices with their start and end apart: 1 -> 1, of which waited for: 0 -> 0; matrix products, arithmetic and copies ran while one was open for 7% -> 11% of each run, Pallas kernels for 0% -> 0%
where the time goes in v3:
time: 94.8 us; the launch traced here: 94.4 us
  blocking collectives  64.9 us (68%)
  local copies, waits for them, and re-layouts  9.27 us (10%)
  matrix products  8.33 us (9%)
  starting transfers between devices  7.26 us (8%)
  other arithmetic  4.27 us (5%)
    all_to_all x2, blocking collectives, spread(): lax.all_to_all(outgoing, axes, split_axis=0, concat_axis=3, tiled=True)[0]  47 us
    all_to_all x1, blocking collectives, gather_cache(): lax.all_to_all(outgoing, ('zh', 'tp'), split_axis=0, concat_axis=3, tiled...  17.9 us
    ppermute x1, starting transfers between devices, gather_cache(): other = lax.ppermute(mine, 'core', [(0, 1), (1, 0)])  7.26 us
    dot_general x2, matrix products, per_device(): jnp.einsum('thep,hpd->thed', weight.astype(jnp.bfloat16), values, preferr...  3.65 us
    slice x2, local copies, waits for them, and re-layouts, per_device(): parts.append((scores, allowed, rows[1]))  2.84 us
    dot_general x2, matrix products, per_device(): jnp.einsum('thed,hpd->thep', query_rows, rows[0], preferred_element_type=...  2.76 us
    reduce_sum x1, other arithmetic, per_device(): total_weight = total_weight + jnp.sum(weight, axis=-1)  2.04 us
  transfers between devices with their start and end apart: 1, of which 0 were waited for; matrix products, arithmetic and copies ran while one was open for 11% of the time, Pallas kernels for 0%

profile of v3, /device:TPU:1, one launch (start us, length us, event | category | flops | bytes accessed | tf_op | source)
XLA Modules:
  0.0 94.4 jit_solution(14371368947994200200)
XLA Ops:
  0.0 0.8 reshape.197
  0.9 17.9 %all_to_all.45 = bf16[8,2,4,4,128]{4,3,2,1,0:T(4,128)(2,1)S(1)} all-to-all(bf16[8,2,4,4,128]{4,3,2,1,0:T(4,128)(2,1)S(1)} %bitcast.129), channel_id=1, replica_groups=mesh['x'=4,'zh'=2,'y'=8,'core'=2,'tp'=4] {'zh','tp'}, dimensions={0} | all-to-all | bytes 131072 | tf_op jit(solution)/shard_map/all_to_all | solution.py:29
  18.8 0.1 broadcast_in_dim.146
  18.9 21.1 %all_to_all.46 = bf16[8,2,4,32,128]{4,3,2,1,0:T(8,128)(2,1)S(1)} all-to-all(bf16[8,2,4,32,128]{4,3,2,1,0:T(8,128)(2,1)S(1)} %broadcast_in_dim.146), channel_id=1, replica_groups=mesh['x'=4,'zh'=2,'y'=8,'core'=2,'tp'=4] {'y'}, dimensions={0} | all-to-all | bytes 1048576 | tf_op jit(solution)/shard_map/all_to_all | solution.py:20
  40.0 0.5 broadcast_in_dim.148
  40.5 0.0 copy-start.10
  40.5 0.0 copy-start.9
  40.5 0.0 copy-start.4
  40.6 0.0 copy-start.5
  40.6 0.0 copy-start.11
  40.6 25.9 %all_to_all.47 = bf16[4,2,4,256,128]{4,3,2,1,0:T(8,128)(2,1)S(1)} all-to-all(bf16[4,2,4,256,128]{4,3,2,1,0:T(8,128)(2,1)S(1)} %broadcast_in_dim.148), channel_id=1, replica_groups=mesh['x'=4,'zh'=2,'y'=8,'core'=2,'tp'=4] {'x'}, dimensions={0} | all-to-all | bytes 4194304 | tf_op jit(solution)/shard_map/all_to_all | solution.py:20
  66.4 1.4 %copy.79 = bf16[1,2,4,4,256,128]{5,4,3,2,1,0:T(8,128)(2,1)} copy(bf16[1,2,4,4,256,128]{5,4,2,1,3,0:T(8,128)(2,1)S(1)} %bitcast.120) | data formatting | bytes 4194304 | tf_op jit(solution)/shard_map/all_to_all | solution.py:20
  67.9 7.3 %collective-permute-start = (bf16[2,4,1024,128]{3,2,1,0:T(8,128)(2,1)}, bf16[2,4,1024,128]{3,2,1,0:T(8,128)(2,1)}, u32[]{:S(2)}, u32[]{:S(2)}) collective-permute-start(bf16[2,4,1024,128]{3,2,1,0:T(8,128)(2,1)} %bitcast.26), channel_id=1, source_target_pairs={{0,4},{4,0},{1,5},{5,1},{2,6},{6,2},{3,7},{7,3},{8,12},{12,8},{9,1... | collective-permute-start | bytes 6291464 | tf_op jit(solution)/shard_map/ppermute | solution.py:32
  75.2 0.0 copy-done.10
  75.2 0.2 reduce-window.4
  75.4 0.6 slice.24
  75.9 0.0 copy-done.9
  75.9 0.1 reshape.195
  76.1 0.1 broadcast_select_fusion.1
  76.2 0.1 reshape.196
  76.4 0.1 reshape.199
  76.5 0.1 broadcast_in_dim.150
  76.6 0.1 eq.76
  76.7 0.1 broadcast_in_dim.142
  76.8 0.1 eq.73
  76.9 0.0 copy-done.4
  76.9 0.2 reshape.194
  77.1 0.0 copy-done.5
  77.1 0.2 copy.69
  77.3 0.0 copy-start.1
  77.3 0.6 iota_compare_fusion.3
  77.9 0.0 copy-start.6
  77.9 0.1 convert_reduce_fusion
  78.0 0.0 copy-done.11
  78.0 0.1 select_reduce_fusion
  78.1 0.1 fusion.42
  78.2 1.0 %compare_and_fusion.1 = (pred[128,1024]{0,1:T(8,128)(4,1)S(1)}, pred[128,1024]{0,1:T(8,128)(4,1)}) fusion(s32[128]{0:T(128)S(1)} %select_reduce_fusion, s32[1024]{0:T(1024)S(1)} %eq.73, pred[128]{0:T(512)(128)(4,1)S(1)} %iota_compare_fusion.3, s32[1024]{0:T(1024)S(1)} %eq.76), kind=kLoop, calls=%fused_computation.29 | loop fusion | flops 524288 | bytes 270976 | tf_op jit(solution)/shard_map/and | solution.py:79
  79.2 0.0 copy-done.1
  79.2 0.0 copy-done.6
  79.2 1.7 %fusion.51 = (f32[128,4,2]{0,2,1:T(2,128)}, f32[128,4,2,128]{0,3,2,1:T(8,128)}) fusion(bf16[128,4,2,128]{3,2,1,0:T(2,128)(2,1)S(1)} %reshape.194, bf16[128,4,2,128]{0,3,2,1:T(8,128)(2,1)S(1)} %bitcast.124, pred[128,128]{0,1:T(8,128)(4,1)S(1)} %fusion.42), kind=kOutput, calls=%fused_computation.61 | convolution fusion | flops 33946624 | bytes 937984 | tf_op jit(solution)/shard_map/thed,uhd->theu/dot_general | solution.py:72
  80.9 1.2 %fusion.50 = (bf16[1,1,4,4,256,128]{5,4,2,1,3,0:T(8,128)(2,1)}, bf16[1,1,4,4,256,128]{5,4,2,1,3,0:T(8,128)(2,1)S(1)}) fusion(bf16[1,2,4,4,256,128]{5,4,2,1,3,0:T(8,128)(2,1)S(1)} %bitcast.121), kind=kLoop, calls=%fused_computation.60 | loop fusion | bytes 4194304 | tf_op jit(solution)/shard_map/slice | solution.py:85
  82.0 1.7 %copy.83 = bf16[1,1,4,4,256,128]{4,3,5,2,1,0:T(4,128)(2,1)S(1)} copy(bf16[1,1,4,4,256,128]{5,4,2,1,3,0:T(8,128)(2,1)} %get-tuple-element.19) | data formatting | bytes 2097152 | tf_op jit(solution)/shard_map/slice | solution.py:85
  83.7 0.8 reshape.266
  84.5 0.0 copy-start.3
  84.5 0.1 copy.76
  84.6 0.8 fusion
  85.3 0.0 copy-start.8
  85.4 0.0 collective-permute-done
  85.4 0.0 copy-done.3
  85.4 2.0 %fusion.1 = (f32[128,4,2]{0,2,1:T(2,128)S(1)}, f32[4,1024,128,2]{2,1,3,0:T(8,128)S(1)}) fusion(pred[128,1024]{0,1:T(8,128)(4,1)S(1)} %copy-done.3, bf16[128,4,2,128]{3,2,1,0:T(2,128)(2,1)S(1)} %reshape.194, bf16[2,4,1024,128]{3,2,1,0:T(8,128)(2,1)} %collective-permute-done), kind=kOutput, calls=%fused_computation.5 | convolution fusion | flops 271580160 | bytes 5640192 | tf_op jit(solution)/shard_map/thed,hpd->thep/dot_general | solution.py:80
  87.4 0.0 copy-done.8
  87.4 1.2 %fusion.8 = f32[4,128,2,128]{1,3,2,0:T(8,128)S(1)} fusion(f32[4,1024,128,2]{2,1,3,0:T(8,128)S(1)} %get-tuple-element.30, f32[128,4,2]{0,2,1:T(2,128)S(1)} %bitcast.134, pred[128,1024]{0,1:T(8,128)(4,1)S(1)} %get-tuple-element.23, bf16[4,1024,128,1]{1,2,0,3:T(8,128)(2,1)S(1)} %reshape.266), kind=kOutput, calls=%fused_computation.11 | convolution fusion | flops 273678336 | bytes 5902336 | tf_op jit(solution)/shard_map/thep,hpd->thed/dot_general | solution.py:95
  88.6 0.0 copy-start
  88.6 0.0 copy-start.2
  88.6 0.0 copy-start.7
  88.6 2.0 %fusion.2 = (f32[128,4,2]{0,2,1:T(2,128)S(1)}, f32[128,4,2]{0,2,1:T(2,128)S(1)}) fusion(f32[4,1024,128,2]{2,1,3,0:T(8,128)S(1)} %get-tuple-element.30, f32[128,4,2]{0,2,1:T(2,128)S(1)} %bitcast.135, pred[128,1024]{0,1:T(8,128)(4,1)S(1)} %get-tuple-element.23, f32[4,1024,128,2]{2,1,3,0:T(8,128)S(1)} %get-tuple-element.26, pred[128,1024]{0,1:T(8,128)(4,1)S(1)} %copy-done.3), kind=kLoop, calls=%fused_computation.6 | loop fusion | flops 10483712 | bytes 8663040 | tf_op jit(solution)/shard_map/reduce_sum | solution.py:94
  90.6 0.0 copy-done
  90.7 0.1 fusion.31
  90.8 0.0 copy-done.2
  90.8 0.2 convolution_add_fusion
  91.0 0.0 copy-done.7
  91.1 2.5 %fusion.28 = bf16[128,4,2,128]{0,3,2,1:T(8,128)(2,1)S(1)} fusion(f32[4,128,2,128]{1,3,2,0:T(8,128)S(1)} %convolution_add_fusion, bf16[2,4,1024,128]{3,2,1,0:T(8,128)(2,1)} %collective-permute-done, f32[4,1024,128,2]{2,1,3,0:T(8,128)S(1)} %get-tuple-element.26, f32[128,4,2]{0,2,1:T(2,128)S(1)} %bitcast.138, pred[128,1024]{0,1:T(8,128)(4,1)S(1)} %copy-done.3, ...), kind=kOutput, calls=%fused_computation.26 | convolution fusion | flops 274202624 | bytes 6168704 | tf_op jit(solution)/shard_map/thep,hpd->thed/dot_general | solution.py:95
  93.6 0.9 copy.87
  (8 shorter events, 0.2 us)
Async XLA Ops:
  40.5 34.6 %copy-start.10 = (s32[4]{0:T(128)S(1)}, s32[4]{0:T(128)}, u32[]{:S(2)}) copy-start(s32[4]{0:T(128)} %param.12) | copy-start | bytes 52
  40.5 35.4 %copy-start.9 = (s32[512]{0:T(512)S(1)}, s32[512]{0:T(512)}, u32[]{:S(2)}) copy-start(s32[512]{0:T(512)} %param.11) | copy-start | bytes 6148
  40.5 36.4 %copy-start.4 = (bf16[128,1024]{1,0:T(8,128)(2,1)S(1)}, bf16[128,1024]{1,0:T(8,128)(2,1)}, u32[]{:S(2)}) copy-start(bf16[128,1024]{1,0:T(8,128)(2,1)} %param.8) | copy-start | bytes 786436
  40.6 36.6 %copy-start.5 = (bf16[128,1024]{1,0:T(8,128)(2,1)S(1)}, bf16[128,1024]{1,0:T(8,128)(2,1)}, u32[]{:S(2)}) copy-start(bf16[128,1024]{1,0:T(8,128)(2,1)} %param.9) | copy-start | bytes 786436
  40.6 37.5 %copy-start.11 = (s32[4]{0:T(128)S(1)}, s32[4]{0:T(128)}, u32[]{:S(2)}) copy-start(s32[4]{0:T(128)} %param.13) | copy-start | bytes 52
  67.9 17.5 %collective-permute-start = (bf16[2,4,1024,128]{3,2,1,0:T(8,128)(2,1)}, bf16[2,4,1024,128]{3,2,1,0:T(8,128)(2,1)}, u32[]{:S(2)}, u32[]{:S(2)}) collective-permute-start(bf16[2,4,1024,128]{3,2,1,0:T(8,128)(2,1)} %bitcast.26), channel_id=1, source_target_pairs={{0,4},{4,0},{1,5},{5,1},{2,6},{6,2},{3,7},{7,3},{8,12},{12,8},{9,1... | collective-permute-start | bytes 6291464 | tf_op jit(solution)/shard_map/ppermute | solution.py:32
  77.3 1.9 %copy-start.1 = (bf16[128,1024]{0,1:T(8,128)(2,1)}, bf16[128,1024]{0,1:T(8,128)(2,1)S(1)}, u32[]{:S(2)}) copy-start(bf16[128,1024]{0,1:T(8,128)(2,1)S(1)} %copy.69) | copy-start | bytes 786436
  77.9 1.3 %copy-start.6 = (pred[128]{0:T(512)(128)(4,1)}, pred[128]{0:T(512)(128)(4,1)S(1)}, u32[]{:S(2)}) copy-start(pred[128]{0:T(512)(128)(4,1)S(1)} %iota_compare_fusion.3) | copy-start | bytes 388
  84.5 0.9 copy-start.3
  85.3 2.0 %copy-start.8 = (f32[128,4,2]{0,2,1:T(2,128)S(1)}, f32[128,4,2]{0,2,1:T(2,128)}, u32[]{:S(2)}) copy-start(f32[128,4,2]{0,2,1:T(2,128)} %get-tuple-element.27) | copy-start | bytes 12292
  88.6 2.1 %copy-start = (f32[128,4,2,128]{0,3,2,1:T(8,128)S(1)}, f32[128,4,2,128]{0,3,2,1:T(8,128)}, u32[]{:S(2)}) copy-start(f32[128,4,2,128]{0,3,2,1:T(8,128)} %get-tuple-element.28) | copy-start | bytes 1572868
  88.6 2.2 %copy-start.2 = (bf16[128,1024]{0,1:T(8,128)(2,1)S(1)}, bf16[128,1024]{0,1:T(8,128)(2,1)}, u32[]{:S(2)}) copy-start(bf16[128,1024]{0,1:T(8,128)(2,1)} %copy-done.1) | copy-start | bytes 786436
  88.6 2.4 %copy-start.7 = (pred[128]{0:T(512)(128)(4,1)S(1)}, pred[128]{0:T(512)(128)(4,1)}, u32[]{:S(2)}) copy-start(pred[128]{0:T(512)(128)(4,1)} %copy-done.6) | copy-start | bytes 388

commit v4 on v3

--- a/solution.py
+++ b/solution.py
@@ -24,10 +24,10 @@
     block_rows = prefix_cache.shape[0]
     size = dict(SEQ_PARTS)
     local = prefix_cache.reshape(block_rows, tensor_count, local_heads, 2, HEAD).transpose(1, 3, 2, 0, 4)
-    outgoing = jnp.broadcast_to(local[None], (size["zh"],) + local.shape)
-    outgoing = outgoing.reshape((size["zh"] * tensor_count,) + local.shape[1:])
-    mine = lax.all_to_all(outgoing, ("zh", "tp"), split_axis=0, concat_axis=3, tiled=True)[0]
-    mine = spread(mine, ("y",), size["y"])
+    lines = size["y"] * size["zh"]
+    outgoing = jnp.broadcast_to(local[None], (lines,) + local.shape)
+    outgoing = outgoing.reshape((lines * tensor_count,) + local.shape[1:])
+    mine = lax.all_to_all(outgoing, ("y", "zh", "tp"), split_axis=0, concat_axis=3, tiled=True)[0]
     mine = spread(mine, ("x",), size["x"])
     other = lax.ppermute(mine, "core", [(0, 1), (1, 0)])
     grid = block_prefix.reshape(size["x"], size["zh"], size["y"], size["core"], tensor_count)

time: 94.8 us -> 89.8 us (0.947)
  blocking collectives: 64.9 us -> 59.9 us
    all_to_all x2 -> x1, blocking collectives: 47 us -> 26.5 us  [spread(): lax.all_to_all(outgoing, axes, split_axis=0, concat_axis=3, tiled=True)[0]]
    all_to_all x1, blocking collectives: 17.9 us -> 33.4 us  [gather_cache(): lax.all_to_all(outgoing, ('y', 'zh', 'tp'), split_axis=0, concat_axis=3,...]
where the time goes in v4:
time: 89.8 us; the launch traced here: 89 us
  blocking collectives  59.9 us (67%)
  local copies, waits for them, and re-layouts  9.47 us (11%)
  matrix products  8.33 us (9%)
  starting transfers between devices  6.63 us (7%)
  other arithmetic  4.27 us (5%)
    all_to_all x1, blocking collectives, gather_cache(): lax.all_to_all(outgoing, ('y', 'zh', 'tp'), split_axis=0, concat_axis=3,...  33.4 us
    all_to_all x1, blocking collectives, spread(): lax.all_to_all(outgoing, axes, split_axis=0, concat_axis=3, tiled=True)[0]  26.5 us
    ppermute x1, starting transfers between devices, gather_cache(): other = lax.ppermute(mine, 'core', [(0, 1), (1, 0)])  6.63 us
    dot_general x2, matrix products, per_device(): jnp.einsum('thep,hpd->thed', weight.astype(jnp.bfloat16), values, preferr...  3.65 us
    slice x2, local copies, waits for them, and re-layouts, per_device(): parts.append((scores, allowed, rows[1]))  2.84 us
    dot_general x2, matrix products, per_device(): jnp.einsum('thed,hpd->thep', query_rows, rows[0], preferred_element_type=...  2.76 us
    reduce_sum x1, other arithmetic, per_device(): total_weight = total_weight + jnp.sum(weight, axis=-1)  2.04 us
  transfers between devices with their start and end apart: 1, of which 0 were waited for; matrix products, arithmetic and copies ran while one was open for 11% of the time, Pallas kernels for 0%

profile of v4, /device:TPU:1, one launch (start us, length us, event | category | flops | bytes accessed | tf_op | source)
XLA Modules:
  0.0 89.0 jit_solution(3923019696852297557)
XLA Ops:
  0.0 0.8 reshape.196
  0.8 0.2 broadcast_in_dim.137
  1.0 33.4 %all_to_all.30 = bf16[64,2,4,4,128]{4,3,2,1,0:T(4,128)(2,1)S(1)} all-to-all(bf16[64,2,4,4,128]{4,3,2,1,0:T(4,128)(2,1)S(1)} %bitcast.119), channel_id=1, replica_groups=mesh['x'=4,'zh'=2,'y'=8,'core'=2,'tp'=4] {'y','zh','tp'}, dimensions={0} | all-to-all | bytes 1048576 | tf_op jit(solution)/shard_map/all_to_all | solution.py:30
  34.4 0.2 copy.73
  34.6 0.5 broadcast_in_dim.139
  35.1 0.0 copy-start.10
  35.1 0.0 copy-start.9
  35.1 0.0 copy-start.4
  35.1 0.0 copy-start.5
  35.1 0.0 copy-start.11
  35.1 26.5 %all_to_all.31 = bf16[4,2,4,256,128]{4,3,2,1,0:T(8,128)(2,1)S(1)} all-to-all(bf16[4,2,4,256,128]{4,3,2,1,0:T(8,128)(2,1)S(1)} %broadcast_in_dim.139), channel_id=1, replica_groups=mesh['x'=4,'zh'=2,'y'=8,'core'=2,'tp'=4] {'x'}, dimensions={0} | all-to-all | bytes 4194304 | tf_op jit(solution)/shard_map/all_to_all | solution.py:20
  61.6 1.4 %copy.77 = bf16[1,2,4,4,256,128]{5,4,3,2,1,0:T(8,128)(2,1)} copy(bf16[1,2,4,4,256,128]{5,4,2,1,3,0:T(8,128)(2,1)S(1)} %bitcast.115) | data formatting | bytes 4194304 | tf_op jit(solution)/shard_map/all_to_all | solution.py:20
  63.1 6.6 %collective-permute-start = (bf16[2,4,1024,128]{3,2,1,0:T(8,128)(2,1)}, bf16[2,4,1024,128]{3,2,1,0:T(8,128)(2,1)}, u32[]{:S(2)}, u32[]{:S(2)}) collective-permute-start(bf16[2,4,1024,128]{3,2,1,0:T(8,128)(2,1)} %bitcast.23), channel_id=1, source_target_pairs={{0,4},{4,0},{1,5},{5,1},{2,6},{6,2},{3,7},{7,3},{8,12},{12,8},{9,1... | collective-permute-start | bytes 6291464 | tf_op jit(solution)/shard_map/ppermute | solution.py:32
  69.7 0.0 copy-done.10
  69.7 0.2 reduce-window.4
  69.9 0.6 slice.24
  70.5 0.0 copy-done.9
  70.5 0.1 reshape.194
  70.7 0.1 broadcast_select_fusion.1
  70.8 0.1 reshape.195
  70.9 0.1 reshape.198
  71.0 0.1 broadcast_in_dim.141
  71.1 0.1 eq.76
  71.3 0.1 broadcast_in_dim.135
  71.4 0.1 eq.73
  71.5 0.0 copy-done.4
  71.5 0.2 reshape.193
  71.7 0.0 copy-done.5
  71.7 0.2 copy.68
  71.9 0.0 copy-start.1
  71.9 0.6 iota_compare_fusion.3
  72.5 0.0 copy-start.6
  72.5 0.1 convert_reduce_fusion
  72.6 0.0 copy-done.11
  72.6 0.1 select_reduce_fusion
  72.7 0.1 fusion.42
  72.8 1.0 %compare_and_fusion.1 = (pred[128,1024]{0,1:T(8,128)(4,1)S(1)}, pred[128,1024]{0,1:T(8,128)(4,1)}) fusion(s32[128]{0:T(128)S(1)} %select_reduce_fusion, s32[1024]{0:T(1024)S(1)} %eq.73, pred[128]{0:T(512)(128)(4,1)S(1)} %iota_compare_fusion.3, s32[1024]{0:T(1024)S(1)} %eq.76), kind=kLoop, calls=%fused_computation.29 | loop fusion | flops 524288 | bytes 270976 | tf_op jit(solution)/shard_map/and | solution.py:79
  73.7 0.0 copy-done.1
  73.7 0.0 copy-done.6
  73.7 1.7 %fusion.51 = (f32[128,4,2]{0,2,1:T(2,128)}, f32[128,4,2,128]{0,3,2,1:T(8,128)}) fusion(bf16[128,4,2,128]{3,2,1,0:T(2,128)(2,1)S(1)} %reshape.193, bf16[128,4,2,128]{0,3,2,1:T(8,128)(2,1)S(1)} %bitcast.121, pred[128,128]{0,1:T(8,128)(4,1)S(1)} %fusion.42), kind=kOutput, calls=%fused_computation.61 | convolution fusion | flops 33946624 | bytes 937984 | tf_op jit(solution)/shard_map/thed,uhd->theu/dot_general | solution.py:72
  75.4 1.2 %fusion.50 = (bf16[1,1,4,4,256,128]{5,4,2,1,3,0:T(8,128)(2,1)}, bf16[1,1,4,4,256,128]{5,4,2,1,3,0:T(8,128)(2,1)S(1)}) fusion(bf16[1,2,4,4,256,128]{5,4,2,1,3,0:T(8,128)(2,1)S(1)} %bitcast.116), kind=kLoop, calls=%fused_computation.60 | loop fusion | bytes 4194304 | tf_op jit(solution)/shard_map/slice | solution.py:85
  76.6 1.7 %copy.81 = bf16[1,1,4,4,256,128]{4,3,5,2,1,0:T(4,128)(2,1)S(1)} copy(bf16[1,1,4,4,256,128]{5,4,2,1,3,0:T(8,128)(2,1)} %get-tuple-element.19) | data formatting | bytes 2097152 | tf_op jit(solution)/shard_map/slice | solution.py:85
  78.3 0.8 reshape.265
  79.0 0.0 copy-start.3
  79.1 0.1 copy.74
  79.1 0.8 fusion
  79.9 0.0 copy-start.8
  79.9 0.0 collective-permute-done
  79.9 0.0 copy-done.3
  80.0 2.0 %fusion.1 = (f32[128,4,2]{0,2,1:T(2,128)S(1)}, f32[4,1024,128,2]{2,1,3,0:T(8,128)S(1)}) fusion(pred[128,1024]{0,1:T(8,128)(4,1)S(1)} %copy-done.3, bf16[128,4,2,128]{3,2,1,0:T(2,128)(2,1)S(1)} %reshape.193, bf16[2,4,1024,128]{3,2,1,0:T(8,128)(2,1)} %collective-permute-done), kind=kOutput, calls=%fused_computation.5 | convolution fusion | flops 271580160 | bytes 5640192 | tf_op jit(solution)/shard_map/thed,hpd->thep/dot_general | solution.py:80
  81.9 0.0 copy-done.8
  82.0 1.2 %fusion.8 = f32[4,128,2,128]{1,3,2,0:T(8,128)S(1)} fusion(f32[4,1024,128,2]{2,1,3,0:T(8,128)S(1)} %get-tuple-element.30, f32[128,4,2]{0,2,1:T(2,128)S(1)} %bitcast.128, pred[128,1024]{0,1:T(8,128)(4,1)S(1)} %get-tuple-element.23, bf16[4,1024,128,1]{1,2,0,3:T(8,128)(2,1)S(1)} %reshape.265), kind=kOutput, calls=%fused_computation.11 | convolution fusion | flops 273678336 | bytes 5902336 | tf_op jit(solution)/shard_map/thep,hpd->thed/dot_general | solution.py:95
  83.1 0.0 copy-start
  83.2 0.0 copy-start.2
  83.2 0.0 copy-start.7
  83.2 2.0 %fusion.2 = (f32[128,4,2]{0,2,1:T(2,128)S(1)}, f32[128,4,2]{0,2,1:T(2,128)S(1)}) fusion(f32[4,1024,128,2]{2,1,3,0:T(8,128)S(1)} %get-tuple-element.30, f32[128,4,2]{0,2,1:T(2,128)S(1)} %bitcast.129, pred[128,1024]{0,1:T(8,128)(4,1)S(1)} %get-tuple-element.23, f32[4,1024,128,2]{2,1,3,0:T(8,128)S(1)} %get-tuple-element.26, pred[128,1024]{0,1:T(8,128)(4,1)S(1)} %copy-done.3), kind=kLoop, calls=%fused_computation.6 | loop fusion | flops 10483712 | bytes 8663040 | tf_op jit(solution)/shard_map/reduce_sum | solution.py:94
  85.2 0.0 copy-done
  85.2 0.1 fusion.31
  85.3 0.0 copy-done.2
  85.4 0.2 convolution_add_fusion
  85.6 0.0 copy-done.7
  85.6 2.5 %fusion.28 = bf16[128,4,2,128]{0,3,2,1:T(8,128)(2,1)S(1)} fusion(f32[4,128,2,128]{1,3,2,0:T(8,128)S(1)} %convolution_add_fusion, bf16[2,4,1024,128]{3,2,1,0:T(8,128)(2,1)} %collective-permute-done, f32[4,1024,128,2]{2,1,3,0:T(8,128)S(1)} %get-tuple-element.26, f32[128,4,2]{0,2,1:T(2,128)S(1)} %bitcast.132, pred[128,1024]{0,1:T(8,128)(4,1)S(1)} %copy-done.3, ...), kind=kOutput, calls=%fused_computation.26 | convolution fusion | flops 274202624 | bytes 6168704 | tf_op jit(solution)/shard_map/thep,hpd->thed/dot_general | solution.py:95
  88.1 0.9 copy.85
  (5 shorter events, 0.1 us)
Async XLA Ops:
  35.1 34.6 %copy-start.10 = (s32[4]{0:T(128)S(1)}, s32[4]{0:T(128)}, u32[]{:S(2)}) copy-start(s32[4]{0:T(128)} %param.12) | copy-start | bytes 52
  35.1 35.4 %copy-start.9 = (s32[512]{0:T(512)S(1)}, s32[512]{0:T(512)}, u32[]{:S(2)}) copy-start(s32[512]{0:T(512)} %param.11) | copy-start | bytes 6148
  35.1 36.4 %copy-start.4 = (bf16[128,1024]{1,0:T(8,128)(2,1)S(1)}, bf16[128,1024]{1,0:T(8,128)(2,1)}, u32[]{:S(2)}) copy-start(bf16[128,1024]{1,0:T(8,128)(2,1)} %param.8) | copy-start | bytes 786436
  35.1 36.6 %copy-start.5 = (bf16[128,1024]{1,0:T(8,128)(2,1)S(1)}, bf16[128,1024]{1,0:T(8,128)(2,1)}, u32[]{:S(2)}) copy-start(bf16[128,1024]{1,0:T(8,128)(2,1)} %param.9) | copy-start | bytes 786436
  35.1 37.5 %copy-start.11 = (s32[4]{0:T(128)S(1)}, s32[4]{0:T(128)}, u32[]{:S(2)}) copy-start(s32[4]{0:T(128)} %param.13) | copy-start | bytes 52
  63.1 16.8 %collective-permute-start = (bf16[2,4,1024,128]{3,2,1,0:T(8,128)(2,1)}, bf16[2,4,1024,128]{3,2,1,0:T(8,128)(2,1)}, u32[]{:S(2)}, u32[]{:S(2)}) collective-permute-start(bf16[2,4,1024,128]{3,2,1,0:T(8,128)(2,1)} %bitcast.23), channel_id=1, source_target_pairs={{0,4},{4,0},{1,5},{5,1},{2,6},{6,2},{3,7},{7,3},{8,12},{12,8},{9,1... | collective-permute-start | bytes 6291464 | tf_op jit(solution)/shard_map/ppermute | solution.py:32
  71.9 1.9 %copy-start.1 = (bf16[128,1024]{0,1:T(8,128)(2,1)}, bf16[128,1024]{0,1:T(8,128)(2,1)S(1)}, u32[]{:S(2)}) copy-start(bf16[128,1024]{0,1:T(8,128)(2,1)S(1)} %copy.68) | copy-start | bytes 786436
  72.5 1.3 %copy-start.6 = (pred[128]{0:T(512)(128)(4,1)}, pred[128]{0:T(512)(128)(4,1)S(1)}, u32[]{:S(2)}) copy-start(pred[128]{0:T(512)(128)(4,1)S(1)} %iota_compare_fusion.3) | copy-start | bytes 388
  79.0 0.9 %copy-start.3 = (pred[128,1024]{0,1:T(8,128)(4,1)S(1)}, pred[128,1024]{0,1:T(8,128)(4,1)}, u32[]{:S(2)}) copy-start(pred[128,1024]{0,1:T(8,128)(4,1)} %get-tuple-element.24) | copy-start | bytes 393220
  79.9 2.0 %copy-start.8 = (f32[128,4,2]{0,2,1:T(2,128)S(1)}, f32[128,4,2]{0,2,1:T(2,128)}, u32[]{:S(2)}) copy-start(f32[128,4,2]{0,2,1:T(2,128)} %get-tuple-element.27) | copy-start | bytes 12292
  83.1 2.1 %copy-start = (f32[128,4,2,128]{0,3,2,1:T(8,128)S(1)}, f32[128,4,2,128]{0,3,2,1:T(8,128)}, u32[]{:S(2)}) copy-start(f32[128,4,2,128]{0,3,2,1:T(8,128)} %get-tuple-element.28) | copy-start | bytes 1572868
  83.2 2.2 %copy-start.2 = (bf16[128,1024]{0,1:T(8,128)(2,1)S(1)}, bf16[128,1024]{0,1:T(8,128)(2,1)}, u32[]{:S(2)}) copy-start(bf16[128,1024]{0,1:T(8,128)(2,1)} %copy-done.1) | copy-start | bytes 786436
  83.2 2.4 %copy-start.7 = (pred[128]{0:T(512)(128)(4,1)S(1)}, pred[128]{0:T(512)(128)(4,1)}, u32[]{:S(2)}) copy-start(pred[128]{0:T(512)(128)(4,1)} %copy-done.6) | copy-start | bytes 388

commit v5 on v4

--- a/solution.py
+++ b/solution.py
@@ -28,14 +28,29 @@
     outgoing = jnp.broadcast_to(local[None], (lines,) + local.shape)
     outgoing = outgoing.reshape((lines * tensor_count,) + local.shape[1:])
     mine = lax.all_to_all(outgoing, ("y", "zh", "tp"), split_axis=0, concat_axis=3, tiled=True)[0]
-    mine = spread(mine, ("x",), size["x"])
-    other = lax.ppermute(mine, "core", [(0, 1), (1, 0)])
+    rows = mine.shape[2]
+    count = size["x"]
+    here = lax.axis_index("x")
+    core = lax.axis_index("core")
+    swap = [(0, 1), (1, 0)]
+
+    def shift(held, step):
+        return lax.ppermute(held, "x", [(i, (i + step) % count) for i in range(count)])
+
+    far = shift(mine[:, :, : rows // 2], 2)
+    near = shift(mine[:, :, rows // 2 :], -2)
+    pieces = [(mine, 0), (shift(mine, 1), -1), (shift(mine, -1), 1), (jnp.concatenate([far, near], axis=2), 2)]
     grid = block_prefix.reshape(size["x"], size["zh"], size["y"], size["core"], tensor_count)
     grid = grid.transpose(0, 2, 1, 3, 4)
-    core = lax.axis_index("core")
-    own_owner = jnp.repeat(jnp.take(grid, core, axis=3).reshape(-1), block_rows)
-    other_owner = jnp.repeat(jnp.take(grid, 1 - core, axis=3).reshape(-1), block_rows)
-    return (mine, own_owner), (other, other_owner)
+    blocks = []
+    for held, offset in pieces:
+        source = (here + offset) % count
+        line = jnp.take(grid, source, axis=0)
+        own_owner = jnp.repeat(jnp.take(line, core, axis=2).reshape(-1), block_rows)
+        other_owner = jnp.repeat(jnp.take(line, 1 - core, axis=2).reshape(-1), block_rows)
+        blocks.append((held, own_owner))
+        blocks.append((lax.ppermute(held, "core", swap), other_owner))
+    return blocks
 
 
 def token_layout(lengths, prefixes, slots):

time: 89.8 us -> 83.8 us (0.933)
  blocking collectives: 59.9 us -> 0 us
  starting transfers between devices: 6.63 us -> 44.9 us
  waiting for transfers between devices: 0.01 us -> 18.4 us
  matrix products: 8.33 us -> 5.78 us
    all_to_all x2 -> x0, blocking collectives: 59.9 us -> none  [the longest x1 33.4 us: gather_cache(): lax.all_to_all(outgoing, ('y', 'zh', 'tp'), split_axis=0, concat_axis=3,...]
    ppermute x1 -> x8, starting transfers between devices: 6.63 us -> 27.7 us  [the longest x4 14.6 us: gather_cache(): blocks.append((lax.ppermute(held, 'core', swap), other_owner))]
    all_to_all x0 -> x1, starting transfers between devices: none -> 17.1 us  [gather_cache(): lax.all_to_all(outgoing, ('y', 'zh', 'tp'), split_axis=0, concat_axis=3,...]
    ppermute x1 -> x8, waiting for transfers between devices: 0.01 us -> 10.4 us  [the longest x4 10.2 us: shift(): lax.ppermute(held, 'x', [(i, (i + step) % count) for i in range(count)])]
    all_to_all x0 -> x1, waiting for transfers between devices: none -> 7.97 us  [gather_cache(): lax.all_to_all(outgoing, ('y', 'zh', 'tp'), split_axis=0, concat_axis=3,...]
    slice x2, local copies, waits for them, and re-layouts: 2.84 us -> 0.28 us  [per_device(): parts.append((scores, allowed, rows[1]))]
    unnamed x25 -> x12, local copies, waits for them, and re-layouts: 0.25 us -> 2.18 us
    all_to_all x1 -> x0, local copies, waits for them, and re-layouts: 1.44 us -> none  [spread(): lax.all_to_all(outgoing, axes, split_axis=0, concat_axis=3, tiled=True)[0]]
  transfers between devices with their start and end apart: 1 -> 9, of which waited for: 0 -> 3; matrix products, arithmetic and copies ran while one was open for 11% -> 10% of each run, Pallas kernels for 0% -> 0%
where the time goes in v5:
time: 83.8 us; the launch traced here: 82.8 us
  starting transfers between devices  44.9 us (54%)
  waiting for transfers between devices  18.4 us (22%)
  local copies, waits for them, and re-layouts  9.76 us (12%)
  matrix products  5.78 us (7%)
  other arithmetic  3.5 us (4%)
    all_to_all x1, starting transfers between devices, gather_cache(): lax.all_to_all(outgoing, ('y', 'zh', 'tp'), split_axis=0, concat_axis=3,...  17.1 us
    ppermute x4, starting transfers between devices, gather_cache(): blocks.append((lax.ppermute(held, 'core', swap), other_owner))  14.6 us
    ppermute x4, starting transfers between devices, shift(): lax.ppermute(held, 'x', [(i, (i + step) % count) for i in range(count)])  13.1 us
    ppermute x4, waiting for transfers between devices, shift(): lax.ppermute(held, 'x', [(i, (i + step) % count) for i in range(count)])  10.2 us
    all_to_all x1, waiting for transfers between devices, gather_cache(): lax.all_to_all(outgoing, ('y', 'zh', 'tp'), split_axis=0, concat_axis=3,...  7.97 us
    dot_general x8, matrix products, per_device(): jnp.einsum('thep,hpd->thed', weight.astype(jnp.bfloat16), values, preferr...  2.72 us
    dot_general x8, matrix products, per_device(): jnp.einsum('thed,hpd->thep', query_rows, rows[0], preferred_element_type=...  2.53 us
    unnamed x12, local copies, waits for them, and re-layouts  2.18 us
  transfers between devices with their start and end apart: 9, of which 3 were waited for; matrix products, arithmetic and copies ran while one was open for 10% of the time, Pallas kernels for 0%

profile of v5, /device:TPU:1, one launch (start us, length us, event | category | flops | bytes accessed | tf_op | source)
XLA Modules:
  0.0 82.8 jit_solution(9680380052050492406)
XLA Ops:
  0.0 0.8 reshape.466
  0.8 1.0 %broadcast_in_dim.241 = bf16[16,4,2,4,4,128]{5,4,3,2,1,0:T(4,128)(2,1)} broadcast(bf16[4,2,4,4,128]{4,3,2,1,0:T(4,128)(2,1)S(1)} %copy.138), dimensions={1,2,3,4,5} | broadcast | bytes 557056 | tf_op jit(solution)/shard_map/broadcast_in_dim | solution.py:28
  1.8 17.1 %all-to-all-start = ((bf16[64,2,4,4,128]{4,3,2,1,0:T(4,128)(2,1)}), bf16[64,2,4,4,128]{4,3,2,1,0:T(4,128)(2,1)S(1)}, u32[]{:S(2)}, u32[]{:S(2)}) async-start(bf16[64,2,4,4,128]{4,3,2,1,0:T(4,128)(2,1)} %bitcast.12), calls=%async_computation | async-start | bytes 1048576 | tf_op jit(solution)/shard_map/all_to_all | solution.py:30
  19.1 0.6 copy-done.3
  19.7 0.2 reduce-window.4
  19.9 0.6 slice.66
  20.5 0.1 reshape.464
  20.7 0.1 copy.136
  20.8 0.1 copy.154
  20.9 0.1 copy.149
  21.3 0.1 reshape.474
  21.5 0.1 reshape.472
  21.8 0.1 copy.144
  22.0 0.1 reshape.469
  22.2 0.1 reshape.470
  22.4 0.1 reshape.468
  22.8 0.1 eq.180
  22.9 0.1 eq.183
  23.1 0.1 eq.189
  23.3 0.1 eq.186
  23.5 0.1 eq.192
  23.7 0.1 eq.195
  23.9 0.1 eq.201
  24.1 0.1 eq.198
  24.2 0.2 reshape.463
  24.4 0.8 copy-done.1
  25.1 0.2 copy.133
  25.3 0.7 iota_compare_fusion.3
  26.1 0.6 copy-done.4
  26.8 0.3 compare_and_fusion.7
  27.2 0.3 fusion.112
  27.4 8.0 %all-to-all-done = bf16[64,2,4,4,128]{4,3,2,1,0:T(4,128)(2,1)S(1)} async-done(((bf16[64,2,4,4,128]{4,3,2,1,0:T(4,128)(2,1)}), bf16[64,2,4,4,128]{4,3,2,1,0:T(4,128)(2,1)S(1)}, u32[]{:S(2)}, u32[]{:S(2)}) %all-to-all-start) | async-done | bytes 524320 | tf_op jit(solution)/shard_map/all_to_all | solution.py:30
  35.4 0.2 copy.142
  35.6 0.2 fusion.103
  35.8 4.4 %collective-permute-start.3 = (bf16[2,4,256,128]{3,2,1,0:T(8,128)(2,1)S(1)}, bf16[2,4,256,128]{3,2,1,0:T(8,128)(2,1)S(1)}, u32[]{:S(2)}, u32[]{:S(2)}) collective-permute-start(bf16[2,4,256,128]{3,2,1,0:T(8,128)(2,1)S(1)} %bitcast.231), channel_id=1, source_target_pairs={{0,384},{128,0},{256,128},{384,256},{1,385},{129,1},{257,129},{385... | collective-permute-start | bytes 1572872 | tf_op jit(solution)/shard_map/ppermute | solution.py:38
  40.2 1.9 %collective-permute-start.1 = (bf16[2,4,256,128]{3,2,1,0:T(8,128)(2,1)S(1)}, bf16[2,4,256,128]{3,2,1,0:T(8,128)(2,1)S(1)}, u32[]{:S(2)}, u32[]{:S(2)}) collective-permute-start(bf16[2,4,256,128]{3,2,1,0:T(8,128)(2,1)S(1)} %bitcast.232), channel_id=1, source_target_pairs={{0,128},{128,256},{256,384},{384,0},{1,129},{129,257},{257,385},{3... | collective-permute-start | bytes 1572872 | tf_op jit(solution)/shard_map/ppermute | solution.py:38
  42.2 5.8 %collective-permute-start = (bf16[2,4,256,128]{3,2,1,0:T(8,128)(2,1)S(1)}, bf16[2,4,256,128]{3,2,1,0:T(8,128)(2,1)S(1)}, u32[]{:S(2)}, u32[]{:S(2)}) collective-permute-start(bf16[2,4,256,128]{3,2,1,0:T(8,128)(2,1)S(1)} %bitcast.233), channel_id=1, source_target_pairs={{0,4},{4,0},{1,5},{5,1},{2,6},{6,2},{3,7},{7,3},{8,12},{12,8},{9,1... | collective-permute-start | bytes 1572872 | tf_op jit(solution)/shard_map/ppermute | solution.py:52
  48.1 3.9 %collective-permute-start.6 = (bf16[2,4,128,128]{3,2,1,0:T(8,128)(2,1)S(1)}, bf16[2,4,128,128]{3,2,1,0:T(8,128)(2,1)S(1)}, u32[]{:S(2)}, u32[]{:S(2)}) collective-permute-start(bf16[2,4,128,128]{3,2,1,0:T(8,128)(2,1)S(1)} %get-tuple-element.39), channel_id=1, source_target_pairs={{0,256},{128,384},{256,0},{384,128},{1,257},{129,385},{257,1},{385... | collective-permute-start | bytes 786440 | tf_op jit(solution)/shard_map/ppermute | solution.py:38
  52.0 2.9 %collective-permute-start.5 = (bf16[2,4,128,128]{3,2,1,0:T(8,128)(2,1)S(1)}, bf16[2,4,128,128]{3,2,1,0:T(8,128)(2,1)S(1)}, u32[]{:S(2)}, u32[]{:S(2)}) collective-permute-start(bf16[2,4,128,128]{3,2,1,0:T(8,128)(2,1)S(1)} %get-tuple-element.40), channel_id=1, source_target_pairs={{0,256},{128,384},{256,0},{384,128},{1,257},{129,385},{257,1},{385... | collective-permute-start | bytes 786440 | tf_op jit(solution)/shard_map/ppermute | solution.py:38
  54.9 0.3 fusion.113
  55.3 10.2 %collective-permute-done.5 = bf16[2,4,128,128]{3,2,1,0:T(8,128)(2,1)S(1)} collective-permute-done((bf16[2,4,128,128]{3,2,1,0:T(8,128)(2,1)S(1)}, bf16[2,4,128,128]{3,2,1,0:T(8,128)(2,1)S(1)}, u32[]{:S(2)}, u32[]{:S(2)}) %collective-permute-start.5) | collective-permute-done | bytes 262176 | tf_op jit(solution)/shard_map/ppermute | solution.py:38
  65.5 4.5 %collective-permute-start.7 = (bf16[2,4,256,128]{3,2,1,0:T(8,128)(2,1)S(1)}, bf16[2,4,256,128]{3,2,1,0:T(8,128)(2,1)S(1)}, u32[]{:S(2)}, u32[]{:S(2)}) collective-permute-start(bf16[2,4,256,128]{3,2,1,0:T(8,128)(2,1)S(1)} %constant_dynamic-update-slice_fusion), channel_id=1, source_target_pairs={{0,4},{4,0},{1,5},{5,1},{2,6},{6,2},{3,7},{7,3},{8,12},{12,8},{9,1... | collective-permute-start | bytes 1572872 | tf_op jit(solution)/shard_map/ppermute | solution.py:52
  70.1 0.3 fusion.106
  70.4 1.9 %collective-permute-start.4 = (bf16[2,4,256,128]{3,2,1,0:T(8,128)(2,1)S(1)}, bf16[2,4,256,128]{3,2,1,0:T(8,128)(2,1)S(1)}, u32[]{:S(2)}, u32[]{:S(2)}) collective-permute-start(bf16[2,4,256,128]{3,2,1,0:T(8,128)(2,1)S(1)} %collective-permute-done.3), channel_id=1, source_target_pairs={{0,4},{4,0},{1,5},{5,1},{2,6},{6,2},{3,7},{7,3},{8,12},{12,8},{9,1... | collective-permute-start | bytes 1572872 | tf_op jit(solution)/shard_map/ppermute | solution.py:52
  72.3 2.4 %collective-permute-start.2 = (bf16[2,4,256,128]{3,2,1,0:T(8,128)(2,1)S(1)}, bf16[2,4,256,128]{3,2,1,0:T(8,128)(2,1)S(1)}, u32[]{:S(2)}, u32[]{:S(2)}) collective-permute-start(bf16[2,4,256,128]{3,2,1,0:T(8,128)(2,1)S(1)} %collective-permute-done.1), channel_id=1, source_target_pairs={{0,4},{4,0},{1,5},{5,1},{2,6},{6,2},{3,7},{7,3},{8,12},{12,8},{9,1... | collective-permute-start | bytes 1572872 | tf_op jit(solution)/shard_map/ppermute | solution.py:52
  74.7 0.3 fusion.110
  75.1 0.3 fusion.108
  75.4 0.3 fusion.111
  75.7 0.3 fusion.105
  76.0 0.2 collective-permute-done.2
  76.3 0.3 fusion.109
  76.6 0.3 fusion.107
  76.9 0.3 convolution_bitcast_fusion.1
  77.3 0.1 fusion.77
  77.4 0.3 fusion.51
  77.7 0.2 convolution_add_fusion
  78.0 1.9 %fusion.26 = (f32[128,4,2]{0,2,1:T(2,128)S(1)}, f32[128,4,2]{0,2,1:T(2,128)S(1)}, f32[128,4,2]{0,2,1:T(2,128)S(1)}, f32[128,4,2]{0,2,1:T(2,128)S(1)}, f32[128,4,...) fusion(f32[128,4,2,256]{0,3,2,1:T(8,128)S(1)} %get-tuple-element.78, ...), kind=kLoop, calls=%fused_computation.49 | loop fusion | flops 6283264 | bytes 8687616 | tf_op jit(solution)/shard_map/reduce_sum | solution.py:109
  79.9 0.3 convolution_bitcast_fusion
  80.2 0.3 fusion.48
  80.6 0.3 fusion.45
  80.9 0.3 fusion.24
  81.3 0.3 fusion.23
  81.6 0.4 fusion.25
  82.0 0.9 %copy.178 = bf16[128,1024]{1,0:T(8,128)(2,1)} copy(bf16[128,1024]{0,1:T(8,128)(2,1)S(1)} %bitcast.249) | data formatting | bytes 524288 | tf_op jit(solution)/shard_map/reshape | solution.py:117
  (46 shorter events, 2.3 us)
Async XLA Ops:
  1.8 33.6 %all-to-all-start = ((bf16[64,2,4,4,128]{4,3,2,1,0:T(4,128)(2,1)}), bf16[64,2,4,4,128]{4,3,2,1,0:T(4,128)(2,1)S(1)}, u32[]{:S(2)}, u32[]{:S(2)}) async-start(bf16[64,2,4,4,128]{4,3,2,1,0:T(4,128)(2,1)} %bitcast.12), calls=%async_computation | async-start | bytes 1048576 | tf_op jit(solution)/shard_map/all_to_all | solution.py:30
  19.0 0.7 copy-start.3
  19.7 0.8 copy-start.2
  22.7 1.5 %copy-start = (bf16[128,1024]{1,0:T(8,128)(2,1)S(1)}, bf16[128,1024]{1,0:T(8,128)(2,1)}, u32[]{:S(2)}) copy-start(bf16[128,1024]{1,0:T(8,128)(2,1)} %param.10) | copy-start | bytes 786436
  24.2 1.0 %copy-start.1 = (bf16[128,1024]{1,0:T(8,128)(2,1)S(1)}, bf16[128,1024]{1,0:T(8,128)(2,1)}, u32[]{:S(2)}) copy-start(bf16[128,1024]{1,0:T(8,128)(2,1)} %param.11) | copy-start | bytes 786436
  26.0 0.7 copy-start.4
  35.8 34.5 %collective-permute-start.3 = (bf16[2,4,256,128]{3,2,1,0:T(8,128)(2,1)S(1)}, bf16[2,4,256,128]{3,2,1,0:T(8,128)(2,1)S(1)}, u32[]{:S(2)}, u32[]{:S(2)}) collective-permute-start(bf16[2,4,256,128]{3,2,1,0:T(8,128)(2,1)S(1)} %bitcast.231), channel_id=1, source_target_pairs={{0,384},{128,0},{256,128},{384,256},{1,385},{129,1},{257,129},{385... | collective-permute-start | bytes 1572872 | tf_op jit(solution)/shard_map/ppermute | solution.py:38
  40.2 32.1 %collective-permute-start.1 = (bf16[2,4,256,128]{3,2,1,0:T(8,128)(2,1)S(1)}, bf16[2,4,256,128]{3,2,1,0:T(8,128)(2,1)S(1)}, u32[]{:S(2)}, u32[]{:S(2)}) collective-permute-start(bf16[2,4,256,128]{3,2,1,0:T(8,128)(2,1)S(1)} %bitcast.232), channel_id=1, source_target_pairs={{0,128},{128,256},{256,384},{384,0},{1,129},{129,257},{257,385},{3... | collective-permute-start | bytes 1572872 | tf_op jit(solution)/shard_map/ppermute | solution.py:38
  42.2 33.2 %collective-permute-start = (bf16[2,4,256,128]{3,2,1,0:T(8,128)(2,1)S(1)}, bf16[2,4,256,128]{3,2,1,0:T(8,128)(2,1)S(1)}, u32[]{:S(2)}, u32[]{:S(2)}) collective-permute-start(bf16[2,4,256,128]{3,2,1,0:T(8,128)(2,1)S(1)} %bitcast.233), channel_id=1, source_target_pairs={{0,4},{4,0},{1,5},{5,1},{2,6},{6,2},{3,7},{7,3},{8,12},{12,8},{9,1... | collective-permute-start | bytes 1572872 | tf_op jit(solution)/shard_map/ppermute | solution.py:52
  48.1 17.4 %collective-permute-start.6 = (bf16[2,4,128,128]{3,2,1,0:T(8,128)(2,1)S(1)}, bf16[2,4,128,128]{3,2,1,0:T(8,128)(2,1)S(1)}, u32[]{:S(2)}, u32[]{:S(2)}) collective-permute-start(bf16[2,4,128,128]{3,2,1,0:T(8,128)(2,1)S(1)} %get-tuple-element.39), channel_id=1, source_target_pairs={{0,256},{128,384},{256,0},{384,128},{1,257},{129,385},{257,1},{385... | collective-permute-start | bytes 786440 | tf_op jit(solution)/shard_map/ppermute | solution.py:38
  52.0 13.5 %collective-permute-start.5 = (bf16[2,4,128,128]{3,2,1,0:T(8,128)(2,1)S(1)}, bf16[2,4,128,128]{3,2,1,0:T(8,128)(2,1)S(1)}, u32[]{:S(2)}, u32[]{:S(2)}) collective-permute-start(bf16[2,4,128,128]{3,2,1,0:T(8,128)(2,1)S(1)} %get-tuple-element.40), channel_id=1, source_target_pairs={{0,256},{128,384},{256,0},{384,128},{1,257},{129,385},{257,1},{385... | collective-permute-start | bytes 786440 | tf_op jit(solution)/shard_map/ppermute | solution.py:38
  65.5 10.2 %collective-permute-start.7 = (bf16[2,4,256,128]{3,2,1,0:T(8,128)(2,1)S(1)}, bf16[2,4,256,128]{3,2,1,0:T(8,128)(2,1)S(1)}, u32[]{:S(2)}, u32[]{:S(2)}) collective-permute-start(bf16[2,4,256,128]{3,2,1,0:T(8,128)(2,1)S(1)} %constant_dynamic-update-slice_fusion), channel_id=1, source_target_pairs={{0,4},{4,0},{1,5},{5,1},{2,6},{6,2},{3,7},{7,3},{8,12},{12,8},{9,1... | collective-permute-start | bytes 1572872 | tf_op jit(solution)/shard_map/ppermute | solution.py:52
  70.4 6.2 %collective-permute-start.4 = (bf16[2,4,256,128]{3,2,1,0:T(8,128)(2,1)S(1)}, bf16[2,4,256,128]{3,2,1,0:T(8,128)(2,1)S(1)}, u32[]{:S(2)}, u32[]{:S(2)}) collective-permute-start(bf16[2,4,256,128]{3,2,1,0:T(8,128)(2,1)S(1)} %collective-permute-done.3), channel_id=1, source_target_pairs={{0,4},{4,0},{1,5},{5,1},{2,6},{6,2},{3,7},{7,3},{8,12},{12,8},{9,1... | collective-permute-start | bytes 1572872 | tf_op jit(solution)/shard_map/ppermute | solution.py:52
  72.3 3.9 %collective-permute-start.2 = (bf16[2,4,256,128]{3,2,1,0:T(8,128)(2,1)S(1)}, bf16[2,4,256,128]{3,2,1,0:T(8,128)(2,1)S(1)}, u32[]{:S(2)}, u32[]{:S(2)}) collective-permute-start(bf16[2,4,256,128]{3,2,1,0:T(8,128)(2,1)S(1)} %collective-permute-done.1), channel_id=1, source_target_pairs={{0,4},{4,0},{1,5},{5,1},{2,6},{6,2},{3,7},{7,3},{8,12},{12,8},{9,1... | collective-permute-start | bytes 1572872 | tf_op jit(solution)/shard_map/ppermute | solution.py:52

commit v6 on v5

--- a/solution.py
+++ b/solution.py
@@ -28,7 +28,6 @@
     outgoing = jnp.broadcast_to(local[None], (lines,) + local.shape)
     outgoing = outgoing.reshape((lines * tensor_count,) + local.shape[1:])
     mine = lax.all_to_all(outgoing, ("y", "zh", "tp"), split_axis=0, concat_axis=3, tiled=True)[0]
-    rows = mine.shape[2]
     count = size["x"]
     here = lax.axis_index("x")
     core = lax.axis_index("core")
@@ -37,19 +36,18 @@
     def shift(held, step):
         return lax.ppermute(held, "x", [(i, (i + step) % count) for i in range(count)])
 
-    far = shift(mine[:, :, : rows // 2], 2)
-    near = shift(mine[:, :, rows // 2 :], -2)
-    pieces = [(mine, 0), (shift(mine, 1), -1), (shift(mine, -1), 1), (jnp.concatenate([far, near], axis=2), 2)]
+    arrived = [(shift(mine, step), -step) for step in (1, -1, 2)]
     grid = block_prefix.reshape(size["x"], size["zh"], size["y"], size["core"], tensor_count)
     grid = grid.transpose(0, 2, 1, 3, 4)
-    blocks = []
-    for held, offset in pieces:
-        source = (here + offset) % count
-        line = jnp.take(grid, source, axis=0)
-        own_owner = jnp.repeat(jnp.take(line, core, axis=2).reshape(-1), block_rows)
-        other_owner = jnp.repeat(jnp.take(line, 1 - core, axis=2).reshape(-1), block_rows)
-        blocks.append((held, own_owner))
-        blocks.append((lax.ppermute(held, "core", swap), other_owner))
+
+    def owner_of(offset, which):
+        line = jnp.take(grid, (here + offset) % count, axis=0)
+        return jnp.repeat(jnp.take(line, which, axis=2).reshape(-1), block_rows)
+
+    blocks = [(mine, owner_of(0, core)), (lax.ppermute(mine, "core", swap), owner_of(0, 1 - core))]
+    blocks += [(held, owner_of(offset, core)) for held, offset in arrived]
+    forwarded = lax.ppermute(jnp.concatenate([held for held, _ in arrived], axis=2), "core", swap)
+    blocks.append((forwarded, jnp.concatenate([owner_of(offset, 1 - core) for _, offset in arrived])))
     return blocks
 
 

time: 83.8 us -> 78.3 us (0.934)
  starting transfers between devices: 44.9 us -> 32.4 us
  waiting for transfers between devices: 18.4 us -> 25.9 us
  other arithmetic: 3.5 us -> 4.9 us
  local copies, waits for them, and re-layouts: 9.76 us -> 8.43 us
    ppermute x4 -> x2, starting transfers between devices: 14.6 us -> 5.38 us  [the longest x1 3.46 us: gather_cache(): lax.ppermute(jnp.concatenate([held for held, _ in arrived], axis=2), 'cor...]
    ppermute x4 -> x3, waiting for transfers between devices: 10.2 us -> 14.8 us  [shift(): lax.ppermute(held, 'x', [(i, (i + step) % count) for i in range(count)])]
    ppermute x4 -> x3, starting transfers between devices: 13.1 us -> 9.93 us  [shift(): lax.ppermute(held, 'x', [(i, (i + step) % count) for i in range(count)])]
    all_to_all x1, waiting for transfers between devices: 7.97 us -> 10.9 us  [gather_cache(): lax.all_to_all(outgoing, ('y', 'zh', 'tp'), split_axis=0, concat_axis=3,...]
    unnamed x12 -> x5, local copies, waits for them, and re-layouts: 2.18 us -> 0.18 us
    dot_general x8 -> x6, matrix products: 2.53 us -> 2.21 us  [per_device(): jnp.einsum('thed,hpd->thep', query_rows, rows[0], preferred_element_type=...]
    reduce_sum x1 -> x2, other arithmetic: 1.88 us -> 1.78 us  [per_device(): total_weight = total_weight + jnp.sum(weight, axis=-1)]
    dot_general x8 -> x6, matrix products: 2.72 us -> 2.72 us  [per_device(): jnp.einsum('thep,hpd->thed', weight.astype(jnp.bfloat16), values, preferr...]
  transfers between devices with their start and end apart: 9 -> 6, of which waited for: 3 -> 4; matrix products, arithmetic and copies ran while one was open for 10% -> 13% of each run, Pallas kernels for 0% -> 0%
where the time goes in v6:
time: 78.3 us; the launch traced here: 77.6 us
  starting transfers between devices  32.4 us (41%)
  waiting for transfers between devices  25.9 us (33%)
  local copies, waits for them, and re-layouts  8.43 us (11%)
  matrix products  5.48 us (7%)
  other arithmetic  4.9 us (6%)
    all_to_all x1, starting transfers between devices, gather_cache(): lax.all_to_all(outgoing, ('y', 'zh', 'tp'), split_axis=0, concat_axis=3,...  17.1 us
    ppermute x3, waiting for transfers between devices, shift(): lax.ppermute(held, 'x', [(i, (i + step) % count) for i in range(count)])  14.8 us
    all_to_all x1, waiting for transfers between devices, gather_cache(): lax.all_to_all(outgoing, ('y', 'zh', 'tp'), split_axis=0, concat_axis=3,...  10.9 us
    ppermute x3, starting transfers between devices, shift(): lax.ppermute(held, 'x', [(i, (i + step) % count) for i in range(count)])  9.93 us
    ppermute x1, starting transfers between devices, gather_cache(): lax.ppermute(jnp.concatenate([held for held, _ in arrived], axis=2), 'cor...  3.46 us
    dot_general x6, matrix products, per_device(): jnp.einsum('thep,hpd->thed', weight.astype(jnp.bfloat16), values, preferr...  2.72 us
    dot_general x6, matrix products, per_device(): jnp.einsum('thed,hpd->thep', query_rows, rows[0], preferred_element_type=...  2.21 us
    ppermute x1, starting transfers between devices, gather_cache(): lax.ppermute(mine, 'core', swap)  1.92 us
  transfers between devices with their start and end apart: 6, of which 4 were waited for; matrix products, arithmetic and copies ran while one was open for 13% of the time, Pallas kernels for 0%

profile of v6, /device:TPU:1, one launch (start us, length us, event | category | flops | bytes accessed | tf_op | source)
XLA Modules:
  0.0 77.6 jit_solution(10767848202115114627)
XLA Ops:
  0.0 0.9 %reshape.388 = bf16[4,4,4,2,128]{4,3,2,1,0:T(2,128)(2,1)S(1)} reshape(bf16[4,4096]{1,0:T(4,128)(2,1)} %param.12) | data formatting | bytes 65536 | tf_op jit(solution)/shard_map/reshape | solution.py:26
  0.9 1.0 %broadcast_in_dim.222 = bf16[16,4,2,4,4,128]{5,4,3,2,1,0:T(4,128)(2,1)} broadcast(bf16[4,2,4,4,128]{4,3,2,1,0:T(4,128)(2,1)S(1)} %copy.120), dimensions={1,2,3,4,5} | broadcast | bytes 557056 | tf_op jit(solution)/shard_map/broadcast_in_dim | solution.py:28
  1.9 17.1 %all-to-all-start = ((bf16[64,2,4,4,128]{4,3,2,1,0:T(4,128)(2,1)}), bf16[64,2,4,4,128]{4,3,2,1,0:T(4,128)(2,1)S(1)}, u32[]{:S(2)}, u32[]{:S(2)}) async-start(bf16[64,2,4,4,128]{4,3,2,1,0:T(4,128)(2,1)} %bitcast.12), calls=%async_computation | async-start | bytes 1048576 | tf_op jit(solution)/shard_map/all_to_all | solution.py:30
  19.1 0.8 %reduce-window.4 = s32[4,1]{0,1:T(1,128)S(1)} reduce-window(s32[4,1]{0,1:T(1,128)} %bitcast.227, s32[]{:T(128)} %constant.73.clone.1), window={size=4x1 pad=3_0x0_0}, to_apply=%region_0.0 | reduce-window | flops 12 | bytes 36 | tf_op jit(solution)/shard_map/reduce-window
  19.9 0.6 slice.48
  20.5 0.8 %reshape.386 = s32[4,2,8,2,4]{4,3,2,1,0:T(2,128)S(1)} reshape(s32[512]{0:T(512)} %param.13) | data formatting | bytes 4096 | tf_op jit(solution)/shard_map/reshape | solution.py:40
  21.4 0.1 copy.118
  21.5 0.1 copy.132
  21.6 0.1 copy.129
  21.8 0.1 copy.137
  21.8 0.1 reshape.398
  21.9 0.1 copy.136
  22.0 0.1 reshape.396
  22.1 0.1 copy.126
  22.2 0.1 copy.135
  22.3 0.1 reshape.394
  22.5 0.1 reshape.395
  22.7 0.1 reshape.397
  22.9 0.1 reshape.399
  23.0 0.7 iota_compare_fusion.3
  23.8 0.7 select_reduce_fusion
  24.6 10.9 %all-to-all-done = bf16[64,2,4,4,128]{4,3,2,1,0:T(4,128)(2,1)S(1)} async-done(((bf16[64,2,4,4,128]{4,3,2,1,0:T(4,128)(2,1)}), bf16[64,2,4,4,128]{4,3,2,1,0:T(4,128)(2,1)S(1)}, u32[]{:S(2)}, u32[]{:S(2)}) %all-to-all-start) | async-done | bytes 524320 | tf_op jit(solution)/shard_map/all_to_all | solution.py:30
  35.5 0.2 copy.124
  35.7 4.7 %collective-permute-start.3 = (bf16[2,4,256,128]{3,2,1,0:T(8,128)(2,1)S(1)}, bf16[2,4,256,128]{3,2,1,0:T(8,128)(2,1)S(1)}, u32[]{:S(2)}, u32[]{:S(2)}) collective-permute-start(bf16[2,4,256,128]{3,2,1,0:T(8,128)(2,1)S(1)} %bitcast.199), channel_id=1, source_target_pairs={{0,256},{128,384},{256,0},{384,128},{1,257},{129,385},{257,1},{385... | collective-permute-start | bytes 1572872 | tf_op jit(solution)/shard_map/ppermute | solution.py:37
  40.3 2.8 %collective-permute-start.2 = (bf16[2,4,256,128]{3,2,1,0:T(8,128)(2,1)S(1)}, bf16[2,4,256,128]{3,2,1,0:T(8,128)(2,1)S(1)}, u32[]{:S(2)}, u32[]{:S(2)}) collective-permute-start(bf16[2,4,256,128]{3,2,1,0:T(8,128)(2,1)S(1)} %bitcast.200), channel_id=1, source_target_pairs={{0,384},{128,0},{256,128},{384,256},{1,385},{129,1},{257,129},{385... | collective-permute-start | bytes 1572872 | tf_op jit(solution)/shard_map/ppermute | solution.py:37
  43.1 2.5 %collective-permute-start.1 = (bf16[2,4,256,128]{3,2,1,0:T(8,128)(2,1)S(1)}, bf16[2,4,256,128]{3,2,1,0:T(8,128)(2,1)S(1)}, u32[]{:S(2)}, u32[]{:S(2)}) collective-permute-start(bf16[2,4,256,128]{3,2,1,0:T(8,128)(2,1)S(1)} %bitcast.201), channel_id=1, source_target_pairs={{0,128},{128,256},{256,384},{384,0},{1,129},{129,257},{257,385},{3... | collective-permute-start | bytes 1572872 | tf_op jit(solution)/shard_map/ppermute | solution.py:37
  45.9 0.1 reshape.392
  46.1 0.1 reshape.391
  46.3 0.1 reshape.390
  46.5 0.1 reshape.387
  46.7 0.1 eq.150
  46.9 0.1 eq.153
  47.0 0.1 eq.156
  47.2 0.1 eq.159
  47.4 0.1 eq.162
  47.5 0.2 reshape.385
  47.7 0.2 copy.115
  47.9 0.2 compare_and_fusion.5
  48.2 0.3 fusion.93
  48.4 0.5 collective-permute-done.3
  48.9 14.3 %collective-permute-done.2 = bf16[2,4,256,128]{3,2,1,0:T(8,128)(2,1)S(1)} collective-permute-done((bf16[2,4,256,128]{3,2,1,0:T(8,128)(2,1)S(1)}, bf16[2,4,256,128]{3,2,1,0:T(8,128)(2,1)S(1)}, u32[]{:S(2)}, u32[]{:S(2)}) %collective-permute-start.2) | collective-permute-done | bytes 524320 | tf_op jit(solution)/shard_map/ppermute | solution.py:37
  63.2 0.1 pad_maximum_fusion
  63.3 3.5 %collective-permute-start.4 = (bf16[2,4,768,128]{3,2,1,0:T(8,128)(2,1)S(1)}, bf16[2,4,768,128]{3,2,1,0:T(8,128)(2,1)S(1)}, u32[]{:S(2)}, u32[]{:S(2)}) collective-permute-start(bf16[2,4,768,128]{3,2,1,0:T(8,128)(2,1)S(1)} %pad_maximum_fusion), channel_id=1, source_target_pairs={{0,4},{4,0},{1,5},{5,1},{2,6},{6,2},{3,7},{7,3},{8,12},{12,8},{9,1... | collective-permute-start | bytes 4718600 | tf_op jit(solution)/shard_map/ppermute | solution.py:49
  66.8 0.2 compare_and_fusion
  67.0 1.9 %collective-permute-start = (bf16[2,4,256,128]{3,2,1,0:T(8,128)(2,1)S(1)}, bf16[2,4,256,128]{3,2,1,0:T(8,128)(2,1)S(1)}, u32[]{:S(2)}, u32[]{:S(2)}) collective-permute-start(bf16[2,4,256,128]{3,2,1,0:T(8,128)(2,1)S(1)} %bitcast.202), channel_id=1, source_target_pairs={{0,4},{4,0},{1,5},{5,1},{2,6},{6,2},{3,7},{7,3},{8,12},{12,8},{9,1... | collective-permute-start | bytes 1572872 | tf_op jit(solution)/shard_map/ppermute | solution.py:47
  68.9 0.2 fusion.88
  69.3 0.3 fusion.94
  69.6 0.3 fusion.91
  70.0 0.3 fusion.90
  70.3 0.3 fusion.89
  70.6 0.2 collective-permute-done
  70.8 0.3 fusion.92
  71.1 0.6 fusion
  71.8 0.8 fusion.1
  72.5 0.1 fusion.64
  72.6 0.3 fusion.47
  73.0 0.3 convolution_add_fusion
  73.2 1.0 %fusion.29 = (f32[128,4,2]{0,2,1:T(2,128)S(1)}, f32[128,4,2]{0,2,1:T(2,128)S(1)}, f32[128,4,2]{0,2,1:T(2,128)S(1)}, f32[128,4,2]{0,2,1:T(2,128)S(1)}, f32[128,4,2]{0,2,1:T(2,128)S(1)}) fusion(f32[128,4,2,256]{0,3,2,1:T(8,128)S(1)} %get-tuple-element.66, f32[128,4,2]{0,2,1:T(2,128)S(1)} %bitcast.207, pred[128,256]{0,1:T(8,128)(4,1)S(1)} %get-tuple-element.48, ...), kind=kLoop, calls=%fused_computation.42 | loop fusion | flops 3927040 | bytes 5431296 | tf_op jit(solution)/shard_map/reduce_sum | solution.py:107
  74.3 1.0 %fusion.16 = f32[128,4,2,128]{0,3,2,1:T(8,128)S(1)} fusion(f32[4,768,128,2]{2,1,3,0:T(8,128)S(1)} %get-tuple-element.54, f32[128,4,2]{0,2,1:T(2,128)S(1)} %bitcast.208, pred[128,768]{0,1:T(8,128)(4,1)S(1)} %compare_and_fusion, bf16[2,4,768,128]{3,2,1,0:T(8,128)(2,1)S(1)} %collective-permute-done.4), kind=kOutput, calls=%fused_computation.23 | convolution fusion | flops 205258752 | bytes 4558848 | tf_op jit(solution)/shard_map/thep,hpd->thed/dot_general | solution.py:108
  75.3 0.3 fusion.40
  75.6 0.3 fusion.44
  75.9 0.3 fusion.42
  76.3 0.4 fusion.28
  76.7 0.9 %copy.154 = bf16[128,1024]{1,0:T(8,128)(2,1)} copy(bf16[128,1024]{0,1:T(8,128)(2,1)S(1)} %bitcast.213) | data formatting | bytes 524288 | tf_op jit(solution)/shard_map/reshape | solution.py:115
  (31 shorter events, 1.6 us)
Async XLA Ops:
  0.0 47.5 %copy-start = (bf16[128,1024]{1,0:T(8,128)(2,1)S(1)}, bf16[128,1024]{1,0:T(8,128)(2,1)}, u32[]{:S(2)}) copy-start(bf16[128,1024]{1,0:T(8,128)(2,1)} %param.10) | copy-start | bytes 786436
  0.0 47.7 %copy-start.1 = (bf16[128,1024]{1,0:T(8,128)(2,1)S(1)}, bf16[128,1024]{1,0:T(8,128)(2,1)}, u32[]{:S(2)}) copy-start(bf16[128,1024]{1,0:T(8,128)(2,1)} %param.11) | copy-start | bytes 786436
  1.9 33.6 %all-to-all-start = ((bf16[64,2,4,4,128]{4,3,2,1,0:T(4,128)(2,1)}), bf16[64,2,4,4,128]{4,3,2,1,0:T(4,128)(2,1)S(1)}, u32[]{:S(2)}, u32[]{:S(2)}) async-start(bf16[64,2,4,4,128]{4,3,2,1,0:T(4,128)(2,1)} %bitcast.12), calls=%async_computation | async-start | bytes 1048576 | tf_op jit(solution)/shard_map/all_to_all | solution.py:30
  35.7 13.3 %collective-permute-start.3 = (bf16[2,4,256,128]{3,2,1,0:T(8,128)(2,1)S(1)}, bf16[2,4,256,128]{3,2,1,0:T(8,128)(2,1)S(1)}, u32[]{:S(2)}, u32[]{:S(2)}) collective-permute-start(bf16[2,4,256,128]{3,2,1,0:T(8,128)(2,1)S(1)} %bitcast.199), channel_id=1, source_target_pairs={{0,256},{128,384},{256,0},{384,128},{1,257},{129,385},{257,1},{385... | collective-permute-start | bytes 1572872 | tf_op jit(solution)/shard_map/ppermute | solution.py:37
  40.3 22.9 %collective-permute-start.2 = (bf16[2,4,256,128]{3,2,1,0:T(8,128)(2,1)S(1)}, bf16[2,4,256,128]{3,2,1,0:T(8,128)(2,1)S(1)}, u32[]{:S(2)}, u32[]{:S(2)}) collective-permute-start(bf16[2,4,256,128]{3,2,1,0:T(8,128)(2,1)S(1)} %bitcast.200), channel_id=1, source_target_pairs={{0,384},{128,0},{256,128},{384,256},{1,385},{129,1},{257,129},{385... | collective-permute-start | bytes 1572872 | tf_op jit(solution)/shard_map/ppermute | solution.py:37
  43.1 20.1 %collective-permute-start.1 = (bf16[2,4,256,128]{3,2,1,0:T(8,128)(2,1)S(1)}, bf16[2,4,256,128]{3,2,1,0:T(8,128)(2,1)S(1)}, u32[]{:S(2)}, u32[]{:S(2)}) collective-permute-start(bf16[2,4,256,128]{3,2,1,0:T(8,128)(2,1)S(1)} %bitcast.201), channel_id=1, source_target_pairs={{0,128},{128,256},{256,384},{384,0},{1,129},{129,257},{257,385},{3... | collective-permute-start | bytes 1572872 | tf_op jit(solution)/shard_map/ppermute | solution.py:37
  63.3 7.8 %collective-permute-start.4 = (bf16[2,4,768,128]{3,2,1,0:T(8,128)(2,1)S(1)}, bf16[2,4,768,128]{3,2,1,0:T(8,128)(2,1)S(1)}, u32[]{:S(2)}, u32[]{:S(2)}) collective-permute-start(bf16[2,4,768,128]{3,2,1,0:T(8,128)(2,1)S(1)} %pad_maximum_fusion), channel_id=1, source_target_pairs={{0,4},{4,0},{1,5},{5,1},{2,6},{6,2},{3,7},{7,3},{8,12},{12,8},{9,1... | collective-permute-start | bytes 4718600 | tf_op jit(solution)/shard_map/ppermute | solution.py:49
  67.0 3.8 %collective-permute-start = (bf16[2,4,256,128]{3,2,1,0:T(8,128)(2,1)S(1)}, bf16[2,4,256,128]{3,2,1,0:T(8,128)(2,1)S(1)}, u32[]{:S(2)}, u32[]{:S(2)}) collective-permute-start(bf16[2,4,256,128]{3,2,1,0:T(8,128)(2,1)S(1)} %bitcast.202), channel_id=1, source_target_pairs={{0,4},{4,0},{1,5},{5,1},{2,6},{6,2},{3,7},{7,3},{8,12},{12,8},{9,1... | collective-permute-start | bytes 1572872 | tf_op jit(solution)/shard_map/ppermute | solution.py:47

commit v7 on v6

--- a/solution.py
+++ b/solution.py
@@ -2,10 +2,10 @@
 
 import jax
 import jax.numpy as jnp
-import numpy as np
 from jax import lax
 from jax.sharding import Mesh
 from jax.sharding import PartitionSpec as P
+
 
 HEADS = 16
 HEAD = 128
@@ -13,11 +13,6 @@
 masked_score = -1e30
 
 SEQ_PARTS = (("x", 4), ("zh", 2), ("y", 8), ("core", 2))
-
-
-def spread(held, axes, count):
-    outgoing = jnp.broadcast_to(held[None], (count,) + held.shape)
-    return lax.all_to_all(outgoing, axes, split_axis=0, concat_axis=3, tiled=True)[0]
 
 
 def gather_cache(prefix_cache, block_prefix, tensor_count, local_heads):
@@ -36,6 +31,7 @@
     def shift(held, step):
         return lax.ppermute(held, "x", [(i, (i + step) % count) for i in range(count)])
 
+    partner = lax.ppermute(mine, "core", swap)
     arrived = [(shift(mine, step), -step) for step in (1, -1, 2)]
     grid = block_prefix.reshape(size["x"], size["zh"], size["y"], size["core"], tensor_count)
     grid = grid.transpose(0, 2, 1, 3, 4)
@@ -44,7 +40,7 @@
         line = jnp.take(grid, (here + offset) % count, axis=0)
         return jnp.repeat(jnp.take(line, which, axis=2).reshape(-1), block_rows)
 
-    blocks = [(mine, owner_of(0, core)), (lax.ppermute(mine, "core", swap), owner_of(0, 1 - core))]
+    blocks = [(mine, owner_of(0, core)), (partner, owner_of(0, 1 - core))]
     blocks += [(held, owner_of(offset, core)) for held, offset in arrived]
     forwarded = lax.ppermute(jnp.concatenate([held for held, _ in arrived], axis=2), "core", swap)
     blocks.append((forwarded, jnp.concatenate([owner_of(offset, 1 - core) for _, offset in arrived])))
@@ -67,8 +63,6 @@
     tensor_count = lax.axis_size("tp")
     local_heads = HEADS // tensor_count
     token_rows = queries.shape[0]
-    block_rows = prefix_cache.shape[0]
-    column_count = prefix_cache.shape[1] // tensor_count
     slot_ids, request_ids, live_slots, token_group = token_layout(
         request_lengths, request_prefix, token_rows
     )
@@ -122,6 +116,4 @@
     seq = names[:-1]
     in_specs = (P(seq, "tp"), P(seq, "tp"), P(seq + ("tp",), None), P(), P(seq), P(seq))
     out_specs = P(seq, "tp")
-    return jax.shard_map(
-        per_device, mesh=fine, in_specs=in_specs, out_specs=out_specs, check_vma=False
-    )
+    return jax.shard_map(per_device, mesh=fine, in_specs=in_specs, out_specs=out_specs, check_vma=False)

time: 78.3 us -> 78.3 us (level)
  no operation moved by 1% of the time
where the time goes in v7:
time: 78.3 us; the launch traced here: 77.6 us
  starting transfers between devices  32.4 us (41%)
  waiting for transfers between devices  25.9 us (33%)
  local copies, waits for them, and re-layouts  8.43 us (11%)
  matrix products  5.48 us (7%)
  other arithmetic  4.9 us (6%)
    all_to_all x1, starting transfers between devices, gather_cache(): lax.all_to_all(outgoing, ('y', 'zh', 'tp'), split_axis=0, concat_axis=3,...  17.1 us
    ppermute x3, waiting for transfers between devices, shift(): lax.ppermute(held, 'x', [(i, (i + step) % count) for i in range(count)])  14.8 us
    all_to_all x1, waiting for transfers between devices, gather_cache(): lax.all_to_all(outgoing, ('y', 'zh', 'tp'), split_axis=0, concat_axis=3,...  10.9 us
    ppermute x3, starting transfers between devices, shift(): lax.ppermute(held, 'x', [(i, (i + step) % count) for i in range(count)])  9.93 us
    ppermute x1, starting transfers between devices, gather_cache(): lax.ppermute(jnp.concatenate([held for held, _ in arrived], axis=2), 'cor...  3.46 us
    dot_general x6, matrix products, per_device(): jnp.einsum('thep,hpd->thed', weight.astype(jnp.bfloat16), values, preferr...  2.72 us
    dot_general x6, matrix products, per_device(): jnp.einsum('thed,hpd->thep', query_rows, rows[0], preferred_element_type=...  2.21 us
    ppermute x1, starting transfers between devices, gather_cache(): partner = lax.ppermute(mine, 'core', swap)  1.92 us
  transfers between devices with their start and end apart: 6, of which 4 were waited for; matrix products, arithmetic and copies ran while one was open for 13% of the time, Pallas kernels for 0%

profile of v7, /device:TPU:1, one launch (start us, length us, event | category | flops | bytes accessed | tf_op | source)
XLA Modules:
  0.0 77.6 jit_solution(10767848202115114627)
XLA Ops:
  0.0 0.9 %reshape.388 = bf16[4,4,4,2,128]{4,3,2,1,0:T(2,128)(2,1)S(1)} reshape(bf16[4,4096]{1,0:T(4,128)(2,1)} %param.12) | data formatting | bytes 65536 | tf_op jit(solution)/shard_map/reshape | solution.py:21
  0.9 1.0 %broadcast_in_dim.222 = bf16[16,4,2,4,4,128]{5,4,3,2,1,0:T(4,128)(2,1)} broadcast(bf16[4,2,4,4,128]{4,3,2,1,0:T(4,128)(2,1)S(1)} %copy.120), dimensions={1,2,3,4,5} | broadcast | bytes 557056 | tf_op jit(solution)/shard_map/broadcast_in_dim | solution.py:23
  1.9 17.1 %all-to-all-start = ((bf16[64,2,4,4,128]{4,3,2,1,0:T(4,128)(2,1)}), bf16[64,2,4,4,128]{4,3,2,1,0:T(4,128)(2,1)S(1)}, u32[]{:S(2)}, u32[]{:S(2)}) async-start(bf16[64,2,4,4,128]{4,3,2,1,0:T(4,128)(2,1)} %bitcast.12), calls=%async_computation | async-start | bytes 1048576 | tf_op jit(solution)/shard_map/all_to_all | solution.py:25
  19.1 0.8 %reduce-window.4 = s32[4,1]{0,1:T(1,128)S(1)} reduce-window(s32[4,1]{0,1:T(1,128)} %bitcast.227, s32[]{:T(128)} %constant.73.clone.1), window={size=4x1 pad=3_0x0_0}, to_apply=%region_0.0 | reduce-window | flops 12 | bytes 36 | tf_op jit(solution)/shard_map/reduce-window
  19.9 0.6 slice.48
  20.5 0.8 %reshape.386 = s32[4,2,8,2,4]{4,3,2,1,0:T(2,128)S(1)} reshape(s32[512]{0:T(512)} %param.13) | data formatting | bytes 4096 | tf_op jit(solution)/shard_map/reshape | solution.py:36
  21.4 0.1 copy.118
  21.5 0.1 copy.132
  21.6 0.1 copy.129
  21.8 0.1 copy.137
  21.8 0.1 reshape.398
  21.9 0.1 copy.136
  22.0 0.1 reshape.396
  22.1 0.1 copy.126
  22.2 0.1 copy.135
  22.3 0.1 reshape.394
  22.5 0.1 reshape.395
  22.7 0.1 reshape.397
  22.9 0.1 reshape.399
  23.0 0.7 iota_compare_fusion.3
  23.8 0.7 select_reduce_fusion
  24.6 10.9 %all-to-all-done = bf16[64,2,4,4,128]{4,3,2,1,0:T(4,128)(2,1)S(1)} async-done(((bf16[64,2,4,4,128]{4,3,2,1,0:T(4,128)(2,1)}), bf16[64,2,4,4,128]{4,3,2,1,0:T(4,128)(2,1)S(1)}, u32[]{:S(2)}, u32[]{:S(2)}) %all-to-all-start) | async-done | bytes 524320 | tf_op jit(solution)/shard_map/all_to_all | solution.py:25
  35.5 0.2 copy.124
  35.7 4.7 %collective-permute-start.3 = (bf16[2,4,256,128]{3,2,1,0:T(8,128)(2,1)S(1)}, bf16[2,4,256,128]{3,2,1,0:T(8,128)(2,1)S(1)}, u32[]{:S(2)}, u32[]{:S(2)}) collective-permute-start(bf16[2,4,256,128]{3,2,1,0:T(8,128)(2,1)S(1)} %bitcast.199), channel_id=1, source_target_pairs={{0,256},{128,384},{256,0},{384,128},{1,257},{129,385},{257,1},{385... | collective-permute-start | bytes 1572872 | tf_op jit(solution)/shard_map/ppermute | solution.py:32
  40.3 2.8 %collective-permute-start.2 = (bf16[2,4,256,128]{3,2,1,0:T(8,128)(2,1)S(1)}, bf16[2,4,256,128]{3,2,1,0:T(8,128)(2,1)S(1)}, u32[]{:S(2)}, u32[]{:S(2)}) collective-permute-start(bf16[2,4,256,128]{3,2,1,0:T(8,128)(2,1)S(1)} %bitcast.200), channel_id=1, source_target_pairs={{0,384},{128,0},{256,128},{384,256},{1,385},{129,1},{257,129},{385... | collective-permute-start | bytes 1572872 | tf_op jit(solution)/shard_map/ppermute | solution.py:32
  43.1 2.5 %collective-permute-start.1 = (bf16[2,4,256,128]{3,2,1,0:T(8,128)(2,1)S(1)}, bf16[2,4,256,128]{3,2,1,0:T(8,128)(2,1)S(1)}, u32[]{:S(2)}, u32[]{:S(2)}) collective-permute-start(bf16[2,4,256,128]{3,2,1,0:T(8,128)(2,1)S(1)} %bitcast.201), channel_id=1, source_target_pairs={{0,128},{128,256},{256,384},{384,0},{1,129},{129,257},{257,385},{3... | collective-permute-start | bytes 1572872 | tf_op jit(solution)/shard_map/ppermute | solution.py:32
  45.9 0.1 reshape.392
  46.1 0.1 reshape.391
  46.3 0.1 reshape.390
  46.5 0.1 reshape.387
  46.7 0.1 eq.150
  46.9 0.1 eq.153
  47.0 0.1 eq.156
  47.2 0.1 eq.159
  47.4 0.1 eq.162
  47.5 0.2 reshape.385
  47.7 0.2 copy.115
  47.9 0.2 compare_and_fusion.5
  48.2 0.3 fusion.93
  48.4 0.5 collective-permute-done.3
  48.9 14.3 %collective-permute-done.2 = bf16[2,4,256,128]{3,2,1,0:T(8,128)(2,1)S(1)} collective-permute-done((bf16[2,4,256,128]{3,2,1,0:T(8,128)(2,1)S(1)}, bf16[2,4,256,128]{3,2,1,0:T(8,128)(2,1)S(1)}, u32[]{:S(2)}, u32[]{:S(2)}) %collective-permute-start.2) | collective-permute-done | bytes 524320 | tf_op jit(solution)/shard_map/ppermute | solution.py:32
  63.2 0.1 pad_maximum_fusion
  63.3 3.5 %collective-permute-start.4 = (bf16[2,4,768,128]{3,2,1,0:T(8,128)(2,1)S(1)}, bf16[2,4,768,128]{3,2,1,0:T(8,128)(2,1)S(1)}, u32[]{:S(2)}, u32[]{:S(2)}) collective-permute-start(bf16[2,4,768,128]{3,2,1,0:T(8,128)(2,1)S(1)} %pad_maximum_fusion), channel_id=1, source_target_pairs={{0,4},{4,0},{1,5},{5,1},{2,6},{6,2},{3,7},{7,3},{8,12},{12,8},{9,1... | collective-permute-start | bytes 4718600 | tf_op jit(solution)/shard_map/ppermute | solution.py:45
  66.8 0.2 compare_and_fusion
  67.0 1.9 %collective-permute-start = (bf16[2,4,256,128]{3,2,1,0:T(8,128)(2,1)S(1)}, bf16[2,4,256,128]{3,2,1,0:T(8,128)(2,1)S(1)}, u32[]{:S(2)}, u32[]{:S(2)}) collective-permute-start(bf16[2,4,256,128]{3,2,1,0:T(8,128)(2,1)S(1)} %bitcast.202), channel_id=1, source_target_pairs={{0,4},{4,0},{1,5},{5,1},{2,6},{6,2},{3,7},{7,3},{8,12},{12,8},{9,1... | collective-permute-start | bytes 1572872 | tf_op jit(solution)/shard_map/ppermute | solution.py:34
  68.9 0.2 fusion.88
  69.3 0.3 fusion.94
  69.6 0.3 fusion.91
  70.0 0.3 fusion.90
  70.3 0.3 fusion.89
  70.6 0.2 collective-permute-done
  70.8 0.3 fusion.92
  71.1 0.6 fusion
  71.8 0.8 fusion.1
  72.5 0.1 fusion.64
  72.6 0.3 fusion.47
  73.0 0.3 convolution_add_fusion
  73.2 1.0 %fusion.29 = (f32[128,4,2]{0,2,1:T(2,128)S(1)}, f32[128,4,2]{0,2,1:T(2,128)S(1)}, f32[128,4,2]{0,2,1:T(2,128)S(1)}, f32[128,4,2]{0,2,1:T(2,128)S(1)}, f32[128,4,2]{0,2,1:T(2,128)S(1)}) fusion(f32[128,4,2,256]{0,3,2,1:T(8,128)S(1)} %get-tuple-element.66, f32[128,4,2]{0,2,1:T(2,128)S(1)} %bitcast.207, pred[128,256]{0,1:T(8,128)(4,1)S(1)} %get-tuple-element.48, ...), kind=kLoop, calls=%fused_computation.42 | loop fusion | flops 3927040 | bytes 5431296 | tf_op jit(solution)/shard_map/reduce_sum | solution.py:101
  74.3 1.0 %fusion.16 = f32[128,4,2,128]{0,3,2,1:T(8,128)S(1)} fusion(f32[4,768,128,2]{2,1,3,0:T(8,128)S(1)} %get-tuple-element.54, f32[128,4,2]{0,2,1:T(2,128)S(1)} %bitcast.208, pred[128,768]{0,1:T(8,128)(4,1)S(1)} %compare_and_fusion, bf16[2,4,768,128]{3,2,1,0:T(8,128)(2,1)S(1)} %collective-permute-done.4), kind=kOutput, calls=%fused_computation.23 | convolution fusion | flops 205258752 | bytes 4558848 | tf_op jit(solution)/shard_map/thep,hpd->thed/dot_general | solution.py:102
  75.3 0.3 fusion.40
  75.6 0.3 fusion.44
  75.9 0.3 fusion.42
  76.3 0.4 fusion.28
  76.7 0.9 %copy.154 = bf16[128,1024]{1,0:T(8,128)(2,1)} copy(bf16[128,1024]{0,1:T(8,128)(2,1)S(1)} %bitcast.213) | data formatting | bytes 524288 | tf_op jit(solution)/shard_map/reshape | solution.py:109
  (31 shorter events, 1.6 us)
Async XLA Ops:
  0.0 47.5 %copy-start = (bf16[128,1024]{1,0:T(8,128)(2,1)S(1)}, bf16[128,1024]{1,0:T(8,128)(2,1)}, u32[]{:S(2)}) copy-start(bf16[128,1024]{1,0:T(8,128)(2,1)} %param.10) | copy-start | bytes 786436
  0.0 47.7 %copy-start.1 = (bf16[128,1024]{1,0:T(8,128)(2,1)S(1)}, bf16[128,1024]{1,0:T(8,128)(2,1)}, u32[]{:S(2)}) copy-start(bf16[128,1024]{1,0:T(8,128)(2,1)} %param.11) | copy-start | bytes 786436
  1.9 33.6 %all-to-all-start = ((bf16[64,2,4,4,128]{4,3,2,1,0:T(4,128)(2,1)}), bf16[64,2,4,4,128]{4,3,2,1,0:T(4,128)(2,1)S(1)}, u32[]{:S(2)}, u32[]{:S(2)}) async-start(bf16[64,2,4,4,128]{4,3,2,1,0:T(4,128)(2,1)} %bitcast.12), calls=%async_computation | async-start | bytes 1048576 | tf_op jit(solution)/shard_map/all_to_all | solution.py:25
  35.7 13.3 %collective-permute-start.3 = (bf16[2,4,256,128]{3,2,1,0:T(8,128)(2,1)S(1)}, bf16[2,4,256,128]{3,2,1,0:T(8,128)(2,1)S(1)}, u32[]{:S(2)}, u32[]{:S(2)}) collective-permute-start(bf16[2,4,256,128]{3,2,1,0:T(8,128)(2,1)S(1)} %bitcast.199), channel_id=1, source_target_pairs={{0,256},{128,384},{256,0},{384,128},{1,257},{129,385},{257,1},{385... | collective-permute-start | bytes 1572872 | tf_op jit(solution)/shard_map/ppermute | solution.py:32
  40.3 22.9 %collective-permute-start.2 = (bf16[2,4,256,128]{3,2,1,0:T(8,128)(2,1)S(1)}, bf16[2,4,256,128]{3,2,1,0:T(8,128)(2,1)S(1)}, u32[]{:S(2)}, u32[]{:S(2)}) collective-permute-start(bf16[2,4,256,128]{3,2,1,0:T(8,128)(2,1)S(1)} %bitcast.200), channel_id=1, source_target_pairs={{0,384},{128,0},{256,128},{384,256},{1,385},{129,1},{257,129},{385... | collective-permute-start | bytes 1572872 | tf_op jit(solution)/shard_map/ppermute | solution.py:32
  43.1 20.1 %collective-permute-start.1 = (bf16[2,4,256,128]{3,2,1,0:T(8,128)(2,1)S(1)}, bf16[2,4,256,128]{3,2,1,0:T(8,128)(2,1)S(1)}, u32[]{:S(2)}, u32[]{:S(2)}) collective-permute-start(bf16[2,4,256,128]{3,2,1,0:T(8,128)(2,1)S(1)} %bitcast.201), channel_id=1, source_target_pairs={{0,128},{128,256},{256,384},{384,0},{1,129},{129,257},{257,385},{3... | collective-permute-start | bytes 1572872 | tf_op jit(solution)/shard_map/ppermute | solution.py:32
  63.3 7.8 %collective-permute-start.4 = (bf16[2,4,768,128]{3,2,1,0:T(8,128)(2,1)S(1)}, bf16[2,4,768,128]{3,2,1,0:T(8,128)(2,1)S(1)}, u32[]{:S(2)}, u32[]{:S(2)}) collective-permute-start(bf16[2,4,768,128]{3,2,1,0:T(8,128)(2,1)S(1)} %pad_maximum_fusion), channel_id=1, source_target_pairs={{0,4},{4,0},{1,5},{5,1},{2,6},{6,2},{3,7},{7,3},{8,12},{12,8},{9,1... | collective-permute-start | bytes 4718600 | tf_op jit(solution)/shard_map/ppermute | solution.py:45
  67.0 3.8 %collective-permute-start = (bf16[2,4,256,128]{3,2,1,0:T(8,128)(2,1)S(1)}, bf16[2,4,256,128]{3,2,1,0:T(8,128)(2,1)S(1)}, u32[]{:S(2)}, u32[]{:S(2)}) collective-permute-start(bf16[2,4,256,128]{3,2,1,0:T(8,128)(2,1)S(1)} %bitcast.202), channel_id=1, source_target_pairs={{0,4},{4,0},{1,5},{5,1},{2,6},{6,2},{3,7},{7,3},{8,12},{12,8},{9,1... | collective-permute-start | bytes 1572872 | tf_op jit(solution)/shard_map/ppermute | solution.py:34

commit v8 on v6

--- a/solution.py
+++ b/solution.py
@@ -51,6 +51,27 @@
     return blocks
 
 
+def fold_block(running, query_rows, keys, values, allowed):
+    scores = jnp.einsum("thed,hpd->thep", query_rows, keys, preferred_element_type=jnp.float32)
+    scores = jnp.where(allowed, scores * (1.0 / math.sqrt(HEAD)), masked_score)
+    block_max = jnp.max(scores, axis=-1)
+    if running is None:
+        new_max = block_max
+    else:
+        old_max, old_total, old_sum = running
+        new_max = jnp.maximum(old_max, block_max)
+    weights = jnp.where(allowed, jnp.exp(scores - new_max[..., None]), 0.0)
+    products = jnp.einsum(
+        "thep,hpd->thed", weights.astype(jnp.bfloat16), values, preferred_element_type=jnp.float32
+    )
+    total = jnp.sum(weights, axis=-1)
+    if running is not None:
+        rescale = jnp.exp(old_max - new_max)
+        total = old_total * rescale + total
+        products = old_sum * rescale[..., None] + products
+    return new_max, total, products
+
+
 def token_layout(lengths, prefixes, slots):
     cumulative = jnp.cumsum(lengths)
     slot_ids = jnp.arange(slots, dtype=jnp.int32)
@@ -76,39 +97,18 @@
 
     query_rows = queries.reshape(token_rows, local_heads, 2, HEAD)
     own_entries = suffix_entries.reshape(token_rows, local_heads, 2, HEAD)
-    scale = 1.0 / math.sqrt(HEAD)
     suffix_allowed = (
         (request_ids[:, None] == request_ids[None, :])
         & (slot_ids[None, :] <= slot_ids[:, None])
         & live_slots[:, None]
     )[:, None, None, :]
-    suffix_scores = jnp.einsum(
-        "thed,uhd->theu", query_rows, own_entries[:, :, 0], preferred_element_type=jnp.float32
-    ) * scale
-    suffix_scores = jnp.where(suffix_allowed, suffix_scores, masked_score)
-    parts = []
-    row_max = jnp.max(suffix_scores, axis=-1)
+    own_keys = own_entries[:, :, 0].transpose(1, 0, 2)
+    own_values = own_entries[:, :, 1].transpose(1, 0, 2)
+    running = fold_block(None, query_rows, own_keys, own_values, suffix_allowed)
     for rows, owners in halves:
         allowed = ((token_group[:, None] == owners[None, :]) & live_slots[:, None])[:, None, None, :]
-        scores = jnp.einsum(
-            "thed,hpd->thep", query_rows, rows[0], preferred_element_type=jnp.float32
-        ) * scale
-        scores = jnp.where(allowed, scores, masked_score)
-        row_max = jnp.maximum(row_max, jnp.max(scores, axis=-1))
-        parts.append((scores, allowed, rows[1]))
-    suffix_weight = jnp.where(suffix_allowed, jnp.exp(suffix_scores - row_max[..., None]), 0.0)
-    total_weight = jnp.sum(suffix_weight, axis=-1)
-    weighted = jnp.einsum(
-        "theu,uhd->thed", suffix_weight.astype(jnp.bfloat16), own_entries[:, :, 1],
-        preferred_element_type=jnp.float32,
-    )
-    for scores, allowed, values in parts:
-        weight = jnp.where(allowed, jnp.exp(scores - row_max[..., None]), 0.0)
-        total_weight = total_weight + jnp.sum(weight, axis=-1)
-        weighted = weighted + jnp.einsum(
-            "thep,hpd->thed", weight.astype(jnp.bfloat16), values,
-            preferred_element_type=jnp.float32,
-        )
+        running = fold_block(running, query_rows, rows[0], rows[1], allowed)
+    row_max, total_weight, weighted = running
     live_grid = live_slots[:, None, None]
     safe_total = jnp.where(live_grid, total_weight, 1.0)
     result = jnp.where(live_grid[..., None], weighted / safe_total[..., None], 0.0)

time: 78.3 us -> 78.3 us (level)
    reduce_sum x3 -> x7, other arithmetic: 1.89 us -> 1.89 us  [fold_block(): total = jnp.sum(weights, axis=-1)]
  transfers between devices with their start and end apart: 6 -> 6, of which waited for: 4 -> 4; matrix products, arithmetic and copies ran while one was open for 13% -> 14% of each run, Pallas kernels for 0% -> 0%
where the time goes in v8:
time: 78.3 us; the launch traced here: 77.5 us
  starting transfers between devices  32.4 us (41%)
  waiting for transfers between devices  25.6 us (33%)
  local copies, waits for them, and re-layouts  8.6 us (11%)
  matrix products  5.47 us (7%)
  other arithmetic  4.91 us (6%)
    all_to_all x1, starting transfers between devices, gather_cache(): lax.all_to_all(outgoing, ('y', 'zh', 'tp'), split_axis=0, concat_axis=3,...  17.1 us
    ppermute x3, waiting for transfers between devices, shift(): lax.ppermute(held, 'x', [(i, (i + step) % count) for i in range(count)])  14.6 us
    all_to_all x1, waiting for transfers between devices, gather_cache(): lax.all_to_all(outgoing, ('y', 'zh', 'tp'), split_axis=0, concat_axis=3,...  10.8 us
    ppermute x3, starting transfers between devices, shift(): lax.ppermute(held, 'x', [(i, (i + step) % count) for i in range(count)])  9.93 us
    ppermute x1, starting transfers between devices, gather_cache(): lax.ppermute(jnp.concatenate([held for held, _ in arrived], axis=2), 'cor...  3.46 us
    dot_general x7, matrix products, fold_block(): jnp.einsum('thep,hpd->thed', weights.astype(jnp.bfloat16), values, prefer...  3.03 us
    dot_general x7, matrix products, fold_block(): jnp.einsum('thed,hpd->thep', query_rows, keys, preferred_element_type=jnp...  2.45 us
    ppermute x1, starting transfers between devices, gather_cache(): lax.ppermute(mine, 'core', swap)  1.92 us
  transfers between devices with their start and end apart: 6, of which 4 were waited for; matrix products, arithmetic and copies ran while one was open for 14% of the time, Pallas kernels for 0%

profile of v8, /device:TPU:1, one launch (start us, length us, event | category | flops | bytes accessed | tf_op | source)
XLA Modules:
  0.0 77.5 jit_solution(11079066422312595278)
XLA Ops:
  0.0 0.9 %reshape.515 = bf16[4,4,4,2,128]{4,3,2,1,0:T(2,128)(2,1)S(1)} reshape(bf16[4,4096]{1,0:T(4,128)(2,1)} %param.12) | data formatting | bytes 65536 | tf_op jit(solution)/shard_map/reshape | solution.py:26
  0.9 1.0 %broadcast_in_dim.229 = bf16[16,4,2,4,4,128]{5,4,3,2,1,0:T(4,128)(2,1)} broadcast(bf16[4,2,4,4,128]{4,3,2,1,0:T(4,128)(2,1)S(1)} %copy.122), dimensions={1,2,3,4,5} | broadcast | bytes 557056 | tf_op jit(solution)/shard_map/broadcast_in_dim | solution.py:28
  1.9 17.1 %all-to-all-start = ((bf16[64,2,4,4,128]{4,3,2,1,0:T(4,128)(2,1)}), bf16[64,2,4,4,128]{4,3,2,1,0:T(4,128)(2,1)S(1)}, u32[]{:S(2)}, u32[]{:S(2)}) async-start(bf16[64,2,4,4,128]{4,3,2,1,0:T(4,128)(2,1)} %bitcast.18), calls=%async_computation | async-start | bytes 1048576 | tf_op jit(solution)/shard_map/all_to_all | solution.py:30
  19.1 0.8 %reduce-window.4 = s32[4,1]{0,1:T(1,128)S(1)} reduce-window(s32[4,1]{0,1:T(1,128)} %bitcast.277, s32[]{:T(128)} %constant.73.clone.1), window={size=4x1 pad=3_0x0_0}, to_apply=%region_0.0 | reduce-window | flops 12 | bytes 36 | tf_op jit(solution)/shard_map/reduce-window
  19.9 0.8 %reshape.513 = s32[4,2,8,2,4]{4,3,2,1,0:T(2,128)S(1)} reshape(s32[512]{0:T(512)} %param.13) | data formatting | bytes 4096 | tf_op jit(solution)/shard_map/reshape | solution.py:40
  20.8 0.1 copy.143
  21.0 0.1 copy.138
  21.3 0.1 reshape.526
  21.5 0.1 reshape.523
  21.7 0.1 reshape.524
  21.8 0.1 copy.133
  21.9 0.1 copy.120
  22.1 0.1 reshape.521
  22.3 0.1 reshape.522
  22.4 0.6 slice.48
  23.0 0.6 iota_compare_fusion.3
  23.8 0.7 select_reduce_fusion
  24.5 0.2 compare_and_fusion
  24.7 10.8 %all-to-all-done = bf16[64,2,4,4,128]{4,3,2,1,0:T(4,128)(2,1)S(1)} async-done(((bf16[64,2,4,4,128]{4,3,2,1,0:T(4,128)(2,1)}), bf16[64,2,4,4,128]{4,3,2,1,0:T(4,128)(2,1)S(1)}, u32[]{:S(2)}, u32[]{:S(2)}) %all-to-all-start) | async-done | bytes 524320 | tf_op jit(solution)/shard_map/all_to_all | solution.py:30
  35.5 0.2 copy.129
  35.7 4.7 %collective-permute-start.3 = (bf16[2,4,256,128]{3,2,1,0:T(8,128)(2,1)S(1)}, bf16[2,4,256,128]{3,2,1,0:T(8,128)(2,1)S(1)}, u32[]{:S(2)}, u32[]{:S(2)}) collective-permute-start(bf16[2,4,256,128]{3,2,1,0:T(8,128)(2,1)S(1)} %bitcast.241), channel_id=1, source_target_pairs={{0,256},{128,384},{256,0},{384,128},{1,257},{129,385},{257,1},{385... | collective-permute-start | bytes 1572872 | tf_op jit(solution)/shard_map/ppermute | solution.py:37
  40.3 2.8 %collective-permute-start.2 = (bf16[2,4,256,128]{3,2,1,0:T(8,128)(2,1)S(1)}, bf16[2,4,256,128]{3,2,1,0:T(8,128)(2,1)S(1)}, u32[]{:S(2)}, u32[]{:S(2)}) collective-permute-start(bf16[2,4,256,128]{3,2,1,0:T(8,128)(2,1)S(1)} %bitcast.242), channel_id=1, source_target_pairs={{0,384},{128,0},{256,128},{384,256},{1,385},{129,1},{257,129},{385... | collective-permute-start | bytes 1572872 | tf_op jit(solution)/shard_map/ppermute | solution.py:37
  43.1 2.5 %collective-permute-start.1 = (bf16[2,4,256,128]{3,2,1,0:T(8,128)(2,1)S(1)}, bf16[2,4,256,128]{3,2,1,0:T(8,128)(2,1)S(1)}, u32[]{:S(2)}, u32[]{:S(2)}) collective-permute-start(bf16[2,4,256,128]{3,2,1,0:T(8,128)(2,1)S(1)} %bitcast.243), channel_id=1, source_target_pairs={{0,128},{128,256},{256,384},{384,0},{1,129},{129,257},{257,385},{3... | collective-permute-start | bytes 1572872 | tf_op jit(solution)/shard_map/ppermute | solution.py:37
  45.7 0.2 reshape.512
  46.2 0.1 eq.150
  46.4 0.1 reshape.517
  46.5 0.1 eq.153
  46.8 0.1 reshape.518
  46.9 0.1 eq.156
  47.1 0.1 reshape.519
  47.3 0.1 eq.159
  47.7 0.1 eq.162
  47.8 0.2 copy.115
  48.0 0.1 copy.189
  48.1 0.2 compare_and_fusion.5
  48.4 0.2 fusion.98
  48.6 0.3 collective-permute-done.3
  48.9 14.3 %collective-permute-done.2 = bf16[2,4,256,128]{3,2,1,0:T(8,128)(2,1)S(1)} collective-permute-done((bf16[2,4,256,128]{3,2,1,0:T(8,128)(2,1)S(1)}, bf16[2,4,256,128]{3,2,1,0:T(8,128)(2,1)S(1)}, u32[]{:S(2)}, u32[]{:S(2)}) %collective-permute-start.2) | collective-permute-done | bytes 524320 | tf_op jit(solution)/shard_map/ppermute | solution.py:37
  63.2 0.1 pad_maximum_fusion
  63.3 3.5 %collective-permute-start.4 = (bf16[2,4,768,128]{3,2,1,0:T(8,128)(2,1)S(1)}, bf16[2,4,768,128]{3,2,1,0:T(8,128)(2,1)S(1)}, u32[]{:S(2)}, u32[]{:S(2)}) collective-permute-start(bf16[2,4,768,128]{3,2,1,0:T(8,128)(2,1)S(1)} %pad_maximum_fusion), channel_id=1, source_target_pairs={{0,4},{4,0},{1,5},{5,1},{2,6},{6,2},{3,7},{7,3},{8,12},{12,8},{9,1... | collective-permute-start | bytes 4718600 | tf_op jit(solution)/shard_map/ppermute | solution.py:49
  66.8 0.1 fusion.67
  66.9 1.9 %collective-permute-start = (bf16[2,4,256,128]{3,2,1,0:T(8,128)(2,1)S(1)}, bf16[2,4,256,128]{3,2,1,0:T(8,128)(2,1)S(1)}, u32[]{:S(2)}, u32[]{:S(2)}) collective-permute-start(bf16[2,4,256,128]{3,2,1,0:T(8,128)(2,1)S(1)} %bitcast.244), channel_id=1, source_target_pairs={{0,4},{4,0},{1,5},{5,1},{2,6},{6,2},{3,7},{7,3},{8,12},{12,8},{9,1... | collective-permute-start | bytes 1572872 | tf_op jit(solution)/shard_map/ppermute | solution.py:47
  68.8 0.2 fusion.93
  69.2 0.3 fusion.99
  69.6 0.3 fusion.94
  69.9 0.3 fusion.95
  70.2 0.3 fusion.96
  70.5 0.2 collective-permute-done
  70.7 0.3 fusion.97
  71.0 0.6 fusion
  71.7 0.2 fusion.36
  71.9 0.3 convolution_bitcast_fusion.5
  72.2 0.8 fusion.1
  73.0 0.2 fusion.44
  73.2 0.2 fusion.42
  73.4 0.2 fusion.40
  73.6 0.2 fusion.38
  73.9 0.3 fusion.21
  74.1 1.0 %fusion.16 = f32[128,4,2,128]{0,3,2,1:T(8,128)S(1)} fusion(f32[4,768,128,2]{2,1,3,0:T(8,128)S(1)} %get-tuple-element.62, f32[128,4,2]{0,2,1:T(2,128)S(1)} %bitcast.266, pred[128,768]{0,1:T(8,128)(4,1)S(1)} %compare_and_fusion, bf16[2,4,768,128]{3,2,1,0:T(8,128)(2,1)S(1)} %collective-permute-done.4), kind=kOutput, calls=%fused_computation.23 | convolution fusion | flops 205258752 | bytes 4558848 | tf_op jit(solution)/shard_map/thep,hpd->thed/dot_general | solution.py:64
  75.1 0.3 convolution_bitcast_fusion.1
  75.5 0.3 convolution_bitcast_fusion.2
  75.8 0.3 convolution_bitcast_fusion.3
  76.1 0.5 fusion.35
  76.6 0.9 %copy.154 = bf16[128,1024]{1,0:T(8,128)(2,1)} copy(bf16[128,1024]{0,1:T(8,128)(2,1)S(1)} %bitcast.245) | data formatting | bytes 524288 | tf_op jit(solution)/shard_map/reshape | solution.py:115
  (37 shorter events, 2.1 us)
Async XLA Ops:
  0.0 45.7 %copy-start = (bf16[128,1024]{1,0:T(8,128)(2,1)S(1)}, bf16[128,1024]{1,0:T(8,128)(2,1)}, u32[]{:S(2)}) copy-start(bf16[128,1024]{1,0:T(8,128)(2,1)} %param.10) | copy-start | bytes 786436
  0.0 47.8 %copy-start.1 = (bf16[128,1024]{1,0:T(8,128)(2,1)S(1)}, bf16[128,1024]{1,0:T(8,128)(2,1)}, u32[]{:S(2)}) copy-start(bf16[128,1024]{1,0:T(8,128)(2,1)} %param.11) | copy-start | bytes 786436
  1.9 33.6 %all-to-all-start = ((bf16[64,2,4,4,128]{4,3,2,1,0:T(4,128)(2,1)}), bf16[64,2,4,4,128]{4,3,2,1,0:T(4,128)(2,1)S(1)}, u32[]{:S(2)}, u32[]{:S(2)}) async-start(bf16[64,2,4,4,128]{4,3,2,1,0:T(4,128)(2,1)} %bitcast.18), calls=%async_computation | async-start | bytes 1048576 | tf_op jit(solution)/shard_map/all_to_all | solution.py:30
  35.7 13.3 %collective-permute-start.3 = (bf16[2,4,256,128]{3,2,1,0:T(8,128)(2,1)S(1)}, bf16[2,4,256,128]{3,2,1,0:T(8,128)(2,1)S(1)}, u32[]{:S(2)}, u32[]{:S(2)}) collective-permute-start(bf16[2,4,256,128]{3,2,1,0:T(8,128)(2,1)S(1)} %bitcast.241), channel_id=1, source_target_pairs={{0,256},{128,384},{256,0},{384,128},{1,257},{129,385},{257,1},{385... | collective-permute-start | bytes 1572872 | tf_op jit(solution)/shard_map/ppermute | solution.py:37
  40.3 22.9 %collective-permute-start.2 = (bf16[2,4,256,128]{3,2,1,0:T(8,128)(2,1)S(1)}, bf16[2,4,256,128]{3,2,1,0:T(8,128)(2,1)S(1)}, u32[]{:S(2)}, u32[]{:S(2)}) collective-permute-start(bf16[2,4,256,128]{3,2,1,0:T(8,128)(2,1)S(1)} %bitcast.242), channel_id=1, source_target_pairs={{0,384},{128,0},{256,128},{384,256},{1,385},{129,1},{257,129},{385... | collective-permute-start | bytes 1572872 | tf_op jit(solution)/shard_map/ppermute | solution.py:37
  43.1 20.1 %collective-permute-start.1 = (bf16[2,4,256,128]{3,2,1,0:T(8,128)(2,1)S(1)}, bf16[2,4,256,128]{3,2,1,0:T(8,128)(2,1)S(1)}, u32[]{:S(2)}, u32[]{:S(2)}) collective-permute-start(bf16[2,4,256,128]{3,2,1,0:T(8,128)(2,1)S(1)} %bitcast.243), channel_id=1, source_target_pairs={{0,128},{128,256},{256,384},{384,0},{1,129},{129,257},{257,385},{3... | collective-permute-start | bytes 1572872 | tf_op jit(solution)/shard_map/ppermute | solution.py:37
  63.3 7.7 %collective-permute-start.4 = (bf16[2,4,768,128]{3,2,1,0:T(8,128)(2,1)S(1)}, bf16[2,4,768,128]{3,2,1,0:T(8,128)(2,1)S(1)}, u32[]{:S(2)}, u32[]{:S(2)}) collective-permute-start(bf16[2,4,768,128]{3,2,1,0:T(8,128)(2,1)S(1)} %pad_maximum_fusion), channel_id=1, source_target_pairs={{0,4},{4,0},{1,5},{5,1},{2,6},{6,2},{3,7},{7,3},{8,12},{12,8},{9,1... | collective-permute-start | bytes 4718600 | tf_op jit(solution)/shard_map/ppermute | solution.py:49
  66.9 3.8 %collective-permute-start = (bf16[2,4,256,128]{3,2,1,0:T(8,128)(2,1)S(1)}, bf16[2,4,256,128]{3,2,1,0:T(8,128)(2,1)S(1)}, u32[]{:S(2)}, u32[]{:S(2)}) collective-permute-start(bf16[2,4,256,128]{3,2,1,0:T(8,128)(2,1)S(1)} %bitcast.244), channel_id=1, source_target_pairs={{0,4},{4,0},{1,5},{5,1},{2,6},{6,2},{3,7},{7,3},{8,12},{12,8},{9,1... | collective-permute-start | bytes 1572872 | tf_op jit(solution)/shard_map/ppermute | solution.py:47

commit v9 on v8

--- a/solution.py
+++ b/solution.py
@@ -2,10 +2,10 @@
 
 import jax
 import jax.numpy as jnp
-import numpy as np
 from jax import lax
 from jax.sharding import Mesh
 from jax.sharding import PartitionSpec as P
+
 
 HEADS = 16
 HEAD = 128
@@ -13,11 +13,6 @@
 masked_score = -1e30
 
 SEQ_PARTS = (("x", 4), ("zh", 2), ("y", 8), ("core", 2))
-
-
-def spread(held, axes, count):
-    outgoing = jnp.broadcast_to(held[None], (count,) + held.shape)
-    return lax.all_to_all(outgoing, axes, split_axis=0, concat_axis=3, tiled=True)[0]
 
 
 def gather_cache(prefix_cache, block_prefix, tensor_count, local_heads):
@@ -88,8 +83,6 @@
     tensor_count = lax.axis_size("tp")
     local_heads = HEADS // tensor_count
     token_rows = queries.shape[0]
-    block_rows = prefix_cache.shape[0]
-    column_count = prefix_cache.shape[1] // tensor_count
     slot_ids, request_ids, live_slots, token_group = token_layout(
         request_lengths, request_prefix, token_rows
     )
@@ -108,7 +101,7 @@
     for rows, owners in halves:
         allowed = ((token_group[:, None] == owners[None, :]) & live_slots[:, None])[:, None, None, :]
         running = fold_block(running, query_rows, rows[0], rows[1], allowed)
-    row_max, total_weight, weighted = running
+    _, total_weight, weighted = running
     live_grid = live_slots[:, None, None]
     safe_total = jnp.where(live_grid, total_weight, 1.0)
     result = jnp.where(live_grid[..., None], weighted / safe_total[..., None], 0.0)
@@ -122,6 +115,4 @@
     seq = names[:-1]
     in_specs = (P(seq, "tp"), P(seq, "tp"), P(seq + ("tp",), None), P(), P(seq), P(seq))
     out_specs = P(seq, "tp")
-    return jax.shard_map(
-        per_device, mesh=fine, in_specs=in_specs, out_specs=out_specs, check_vma=False
-    )
+    return jax.shard_map(per_device, mesh=fine, in_specs=in_specs, out_specs=out_specs, check_vma=False)

time: 78.3 us -> 78.3 us (level)
  no operation moved by 1% of the time
where the time goes in v9:
time: 78.3 us; the launch traced here: 77.5 us
  starting transfers between devices  32.4 us (41%)
  waiting for transfers between devices  25.6 us (33%)
  local copies, waits for them, and re-layouts  8.6 us (11%)
  matrix products  5.47 us (7%)
  other arithmetic  4.91 us (6%)
    all_to_all x1, starting transfers between devices, gather_cache(): lax.all_to_all(outgoing, ('y', 'zh', 'tp'), split_axis=0, concat_axis=3,...  17.1 us
    ppermute x3, waiting for transfers between devices, shift(): lax.ppermute(held, 'x', [(i, (i + step) % count) for i in range(count)])  14.6 us
    all_to_all x1, waiting for transfers between devices, gather_cache(): lax.all_to_all(outgoing, ('y', 'zh', 'tp'), split_axis=0, concat_axis=3,...  10.8 us
    ppermute x3, starting transfers between devices, shift(): lax.ppermute(held, 'x', [(i, (i + step) % count) for i in range(count)])  9.93 us
    ppermute x1, starting transfers between devices, gather_cache(): lax.ppermute(jnp.concatenate([held for held, _ in arrived], axis=2), 'cor...  3.46 us
    dot_general x7, matrix products, fold_block(): jnp.einsum('thep,hpd->thed', weights.astype(jnp.bfloat16), values, prefer...  3.03 us
    dot_general x7, matrix products, fold_block(): jnp.einsum('thed,hpd->thep', query_rows, keys, preferred_element_type=jnp...  2.45 us
    ppermute x1, starting transfers between devices, gather_cache(): lax.ppermute(mine, 'core', swap)  1.92 us
  transfers between devices with their start and end apart: 6, of which 4 were waited for; matrix products, arithmetic and copies ran while one was open for 14% of the time, Pallas kernels for 0%

profile of v9, /device:TPU:1, one launch (start us, length us, event | category | flops | bytes accessed | tf_op | source)
XLA Modules:
  0.0 77.5 jit_solution(11079066422312595278)
XLA Ops:
  0.0 0.9 %reshape.515 = bf16[4,4,4,2,128]{4,3,2,1,0:T(2,128)(2,1)S(1)} reshape(bf16[4,4096]{1,0:T(4,128)(2,1)} %param.12) | data formatting | bytes 65536 | tf_op jit(solution)/shard_map/reshape | solution.py:21
  0.9 1.0 %broadcast_in_dim.229 = bf16[16,4,2,4,4,128]{5,4,3,2,1,0:T(4,128)(2,1)} broadcast(bf16[4,2,4,4,128]{4,3,2,1,0:T(4,128)(2,1)S(1)} %copy.122), dimensions={1,2,3,4,5} | broadcast | bytes 557056 | tf_op jit(solution)/shard_map/broadcast_in_dim | solution.py:23
  1.9 17.1 %all-to-all-start = ((bf16[64,2,4,4,128]{4,3,2,1,0:T(4,128)(2,1)}), bf16[64,2,4,4,128]{4,3,2,1,0:T(4,128)(2,1)S(1)}, u32[]{:S(2)}, u32[]{:S(2)}) async-start(bf16[64,2,4,4,128]{4,3,2,1,0:T(4,128)(2,1)} %bitcast.18), calls=%async_computation | async-start | bytes 1048576 | tf_op jit(solution)/shard_map/all_to_all | solution.py:25
  19.1 0.8 %reduce-window.4 = s32[4,1]{0,1:T(1,128)S(1)} reduce-window(s32[4,1]{0,1:T(1,128)} %bitcast.277, s32[]{:T(128)} %constant.73.clone.1), window={size=4x1 pad=3_0x0_0}, to_apply=%region_0.0 | reduce-window | flops 12 | bytes 36 | tf_op jit(solution)/shard_map/reduce-window
  19.9 0.8 %reshape.513 = s32[4,2,8,2,4]{4,3,2,1,0:T(2,128)S(1)} reshape(s32[512]{0:T(512)} %param.13) | data formatting | bytes 4096 | tf_op jit(solution)/shard_map/reshape | solution.py:35
  20.8 0.1 copy.143
  21.0 0.1 copy.138
  21.3 0.1 reshape.526
  21.5 0.1 reshape.523
  21.7 0.1 reshape.524
  21.8 0.1 copy.133
  21.9 0.1 copy.120
  22.1 0.1 reshape.521
  22.3 0.1 reshape.522
  22.4 0.6 slice.48
  23.0 0.6 iota_compare_fusion.3
  23.8 0.7 select_reduce_fusion
  24.5 0.2 compare_and_fusion
  24.7 10.8 %all-to-all-done = bf16[64,2,4,4,128]{4,3,2,1,0:T(4,128)(2,1)S(1)} async-done(((bf16[64,2,4,4,128]{4,3,2,1,0:T(4,128)(2,1)}), bf16[64,2,4,4,128]{4,3,2,1,0:T(4,128)(2,1)S(1)}, u32[]{:S(2)}, u32[]{:S(2)}) %all-to-all-start) | async-done | bytes 524320 | tf_op jit(solution)/shard_map/all_to_all | solution.py:25
  35.5 0.2 copy.129
  35.7 4.7 %collective-permute-start.3 = (bf16[2,4,256,128]{3,2,1,0:T(8,128)(2,1)S(1)}, bf16[2,4,256,128]{3,2,1,0:T(8,128)(2,1)S(1)}, u32[]{:S(2)}, u32[]{:S(2)}) collective-permute-start(bf16[2,4,256,128]{3,2,1,0:T(8,128)(2,1)S(1)} %bitcast.241), channel_id=1, source_target_pairs={{0,256},{128,384},{256,0},{384,128},{1,257},{129,385},{257,1},{385... | collective-permute-start | bytes 1572872 | tf_op jit(solution)/shard_map/ppermute | solution.py:32
  40.3 2.8 %collective-permute-start.2 = (bf16[2,4,256,128]{3,2,1,0:T(8,128)(2,1)S(1)}, bf16[2,4,256,128]{3,2,1,0:T(8,128)(2,1)S(1)}, u32[]{:S(2)}, u32[]{:S(2)}) collective-permute-start(bf16[2,4,256,128]{3,2,1,0:T(8,128)(2,1)S(1)} %bitcast.242), channel_id=1, source_target_pairs={{0,384},{128,0},{256,128},{384,256},{1,385},{129,1},{257,129},{385... | collective-permute-start | bytes 1572872 | tf_op jit(solution)/shard_map/ppermute | solution.py:32
  43.1 2.5 %collective-permute-start.1 = (bf16[2,4,256,128]{3,2,1,0:T(8,128)(2,1)S(1)}, bf16[2,4,256,128]{3,2,1,0:T(8,128)(2,1)S(1)}, u32[]{:S(2)}, u32[]{:S(2)}) collective-permute-start(bf16[2,4,256,128]{3,2,1,0:T(8,128)(2,1)S(1)} %bitcast.243), channel_id=1, source_target_pairs={{0,128},{128,256},{256,384},{384,0},{1,129},{129,257},{257,385},{3... | collective-permute-start | bytes 1572872 | tf_op jit(solution)/shard_map/ppermute | solution.py:32
  45.7 0.2 reshape.512
  46.2 0.1 eq.150
  46.4 0.1 reshape.517
  46.5 0.1 eq.153
  46.8 0.1 reshape.518
  46.9 0.1 eq.156
  47.1 0.1 reshape.519
  47.3 0.1 eq.159
  47.7 0.1 eq.162
  47.8 0.2 copy.115
  48.0 0.1 copy.189
  48.1 0.2 compare_and_fusion.5
  48.4 0.2 fusion.98
  48.6 0.3 collective-permute-done.3
  48.9 14.3 %collective-permute-done.2 = bf16[2,4,256,128]{3,2,1,0:T(8,128)(2,1)S(1)} collective-permute-done((bf16[2,4,256,128]{3,2,1,0:T(8,128)(2,1)S(1)}, bf16[2,4,256,128]{3,2,1,0:T(8,128)(2,1)S(1)}, u32[]{:S(2)}, u32[]{:S(2)}) %collective-permute-start.2) | collective-permute-done | bytes 524320 | tf_op jit(solution)/shard_map/ppermute | solution.py:32
  63.2 0.1 pad_maximum_fusion
  63.3 3.5 %collective-permute-start.4 = (bf16[2,4,768,128]{3,2,1,0:T(8,128)(2,1)S(1)}, bf16[2,4,768,128]{3,2,1,0:T(8,128)(2,1)S(1)}, u32[]{:S(2)}, u32[]{:S(2)}) collective-permute-start(bf16[2,4,768,128]{3,2,1,0:T(8,128)(2,1)S(1)} %pad_maximum_fusion), channel_id=1, source_target_pairs={{0,4},{4,0},{1,5},{5,1},{2,6},{6,2},{3,7},{7,3},{8,12},{12,8},{9,1... | collective-permute-start | bytes 4718600 | tf_op jit(solution)/shard_map/ppermute | solution.py:44
  66.8 0.1 fusion.67
  66.9 1.9 %collective-permute-start = (bf16[2,4,256,128]{3,2,1,0:T(8,128)(2,1)S(1)}, bf16[2,4,256,128]{3,2,1,0:T(8,128)(2,1)S(1)}, u32[]{:S(2)}, u32[]{:S(2)}) collective-permute-start(bf16[2,4,256,128]{3,2,1,0:T(8,128)(2,1)S(1)} %bitcast.244), channel_id=1, source_target_pairs={{0,4},{4,0},{1,5},{5,1},{2,6},{6,2},{3,7},{7,3},{8,12},{12,8},{9,1... | collective-permute-start | bytes 1572872 | tf_op jit(solution)/shard_map/ppermute | solution.py:42
  68.8 0.2 fusion.93
  69.2 0.3 fusion.99
  69.6 0.3 fusion.94
  69.9 0.3 fusion.95
  70.2 0.3 fusion.96
  70.5 0.2 collective-permute-done
  70.7 0.3 fusion.97
  71.0 0.6 fusion
  71.7 0.2 fusion.36
  71.9 0.3 convolution_bitcast_fusion.5
  72.2 0.8 fusion.1
  73.0 0.2 fusion.44
  73.2 0.2 fusion.42
  73.4 0.2 fusion.40
  73.6 0.2 fusion.38
  73.9 0.3 fusion.21
  74.1 1.0 %fusion.16 = f32[128,4,2,128]{0,3,2,1:T(8,128)S(1)} fusion(f32[4,768,128,2]{2,1,3,0:T(8,128)S(1)} %get-tuple-element.62, f32[128,4,2]{0,2,1:T(2,128)S(1)} %bitcast.266, pred[128,768]{0,1:T(8,128)(4,1)S(1)} %compare_and_fusion, bf16[2,4,768,128]{3,2,1,0:T(8,128)(2,1)S(1)} %collective-permute-done.4), kind=kOutput, calls=%fused_computation.23 | convolution fusion | flops 205258752 | bytes 4558848 | tf_op jit(solution)/shard_map/thep,hpd->thed/dot_general | solution.py:59
  75.1 0.3 convolution_bitcast_fusion.1
  75.5 0.3 convolution_bitcast_fusion.2
  75.8 0.3 convolution_bitcast_fusion.3
  76.1 0.5 fusion.35
  76.6 0.9 %copy.154 = bf16[128,1024]{1,0:T(8,128)(2,1)} copy(bf16[128,1024]{0,1:T(8,128)(2,1)S(1)} %bitcast.245) | data formatting | bytes 524288 | tf_op jit(solution)/shard_map/reshape | solution.py:108
  (37 shorter events, 2.1 us)
Async XLA Ops:
  0.0 45.7 %copy-start = (bf16[128,1024]{1,0:T(8,128)(2,1)S(1)}, bf16[128,1024]{1,0:T(8,128)(2,1)}, u32[]{:S(2)}) copy-start(bf16[128,1024]{1,0:T(8,128)(2,1)} %param.10) | copy-start | bytes 786436
  0.0 47.8 %copy-start.1 = (bf16[128,1024]{1,0:T(8,128)(2,1)S(1)}, bf16[128,1024]{1,0:T(8,128)(2,1)}, u32[]{:S(2)}) copy-start(bf16[128,1024]{1,0:T(8,128)(2,1)} %param.11) | copy-start | bytes 786436
  1.9 33.6 %all-to-all-start = ((bf16[64,2,4,4,128]{4,3,2,1,0:T(4,128)(2,1)}), bf16[64,2,4,4,128]{4,3,2,1,0:T(4,128)(2,1)S(1)}, u32[]{:S(2)}, u32[]{:S(2)}) async-start(bf16[64,2,4,4,128]{4,3,2,1,0:T(4,128)(2,1)} %bitcast.18), calls=%async_computation | async-start | bytes 1048576 | tf_op jit(solution)/shard_map/all_to_all | solution.py:25
  35.7 13.3 %collective-permute-start.3 = (bf16[2,4,256,128]{3,2,1,0:T(8,128)(2,1)S(1)}, bf16[2,4,256,128]{3,2,1,0:T(8,128)(2,1)S(1)}, u32[]{:S(2)}, u32[]{:S(2)}) collective-permute-start(bf16[2,4,256,128]{3,2,1,0:T(8,128)(2,1)S(1)} %bitcast.241), channel_id=1, source_target_pairs={{0,256},{128,384},{256,0},{384,128},{1,257},{129,385},{257,1},{385... | collective-permute-start | bytes 1572872 | tf_op jit(solution)/shard_map/ppermute | solution.py:32
  40.3 22.9 %collective-permute-start.2 = (bf16[2,4,256,128]{3,2,1,0:T(8,128)(2,1)S(1)}, bf16[2,4,256,128]{3,2,1,0:T(8,128)(2,1)S(1)}, u32[]{:S(2)}, u32[]{:S(2)}) collective-permute-start(bf16[2,4,256,128]{3,2,1,0:T(8,128)(2,1)S(1)} %bitcast.242), channel_id=1, source_target_pairs={{0,384},{128,0},{256,128},{384,256},{1,385},{129,1},{257,129},{385... | collective-permute-start | bytes 1572872 | tf_op jit(solution)/shard_map/ppermute | solution.py:32
  43.1 20.1 %collective-permute-start.1 = (bf16[2,4,256,128]{3,2,1,0:T(8,128)(2,1)S(1)}, bf16[2,4,256,128]{3,2,1,0:T(8,128)(2,1)S(1)}, u32[]{:S(2)}, u32[]{:S(2)}) collective-permute-start(bf16[2,4,256,128]{3,2,1,0:T(8,128)(2,1)S(1)} %bitcast.243), channel_id=1, source_target_pairs={{0,128},{128,256},{256,384},{384,0},{1,129},{129,257},{257,385},{3... | collective-permute-start | bytes 1572872 | tf_op jit(solution)/shard_map/ppermute | solution.py:32
  63.3 7.7 %collective-permute-start.4 = (bf16[2,4,768,128]{3,2,1,0:T(8,128)(2,1)S(1)}, bf16[2,4,768,128]{3,2,1,0:T(8,128)(2,1)S(1)}, u32[]{:S(2)}, u32[]{:S(2)}) collective-permute-start(bf16[2,4,768,128]{3,2,1,0:T(8,128)(2,1)S(1)} %pad_maximum_fusion), channel_id=1, source_target_pairs={{0,4},{4,0},{1,5},{5,1},{2,6},{6,2},{3,7},{7,3},{8,12},{12,8},{9,1... | collective-permute-start | bytes 4718600 | tf_op jit(solution)/shard_map/ppermute | solution.py:44
  66.9 3.8 %collective-permute-start = (bf16[2,4,256,128]{3,2,1,0:T(8,128)(2,1)S(1)}, bf16[2,4,256,128]{3,2,1,0:T(8,128)(2,1)S(1)}, u32[]{:S(2)}, u32[]{:S(2)}) collective-permute-start(bf16[2,4,256,128]{3,2,1,0:T(8,128)(2,1)S(1)} %bitcast.244), channel_id=1, source_target_pairs={{0,4},{4,0},{1,5},{5,1},{2,6},{6,2},{3,7},{7,3},{8,12},{12,8},{9,1... | collective-permute-start | bytes 1572872 | tf_op jit(solution)/shard_map/ppermute | solution.py:42

commit v10 on v8

--- a/solution.py
+++ b/solution.py
@@ -44,10 +44,11 @@
         line = jnp.take(grid, (here + offset) % count, axis=0)
         return jnp.repeat(jnp.take(line, which, axis=2).reshape(-1), block_rows)
 
-    blocks = [(mine, owner_of(0, core)), (lax.ppermute(mine, "core", swap), owner_of(0, 1 - core))]
+    blocks = [(mine, owner_of(0, core))]
     blocks += [(held, owner_of(offset, core)) for held, offset in arrived]
-    forwarded = lax.ppermute(jnp.concatenate([held for held, _ in arrived], axis=2), "core", swap)
-    blocks.append((forwarded, jnp.concatenate([owner_of(offset, 1 - core) for _, offset in arrived])))
+    everything = [(mine, 0)] + arrived
+    forwarded = lax.ppermute(jnp.concatenate([held for held, _ in everything], axis=2), "core", swap)
+    blocks.append((forwarded, jnp.concatenate([owner_of(offset, 1 - core) for _, offset in everything])))
     return blocks
 
 

time: 78.3 us -> 77.9 us (level)
  starting transfers between devices: 32.4 us -> 30.5 us
  local copies, waits for them, and re-layouts: 8.6 us -> 10.4 us
    all_to_all x1, waiting for transfers between devices: 10.8 us -> 8.14 us  [gather_cache(): lax.all_to_all(outgoing, ('y', 'zh', 'tp'), split_axis=0, concat_axis=3,...]
    ppermute x3, waiting for transfers between devices: 14.6 us -> 16.7 us  [shift(): lax.ppermute(held, 'x', [(i, (i + step) % count) for i in range(count)])]
    ppermute x2 -> x1, starting transfers between devices: 5.38 us -> 3.46 us  [gather_cache(): lax.ppermute(jnp.concatenate([held for held, _ in everything], axis=2), '...]
    ppermute x2 -> x1, waiting for transfers between devices: 0.2 us -> 1.29 us  [gather_cache(): lax.ppermute(jnp.concatenate([held for held, _ in everything], axis=2), '...]
    unnamed x6 -> x4, local copies, waits for them, and re-layouts: 0.31 us -> 1.26 us
    reshape x1, local copies, waits for them, and re-layouts: 0.17 us -> 1.12 us  [per_device(): query_rows = queries.reshape(token_rows, local_heads, 2, HEAD)]
    dot_general x7 -> x6, matrix products: 2.45 us -> 2.27 us  [fold_block(): jnp.einsum('thed,hpd->thep', query_rows, keys, preferred_element_type=jnp...]
    dot_general x7 -> x6, matrix products: 3.03 us -> 2.96 us  [fold_block(): jnp.einsum('thep,hpd->thed', weights.astype(jnp.bfloat16), values, prefer...]
  transfers between devices with their start and end apart: 6 -> 5, of which waited for: 4 -> 4; matrix products, arithmetic and copies ran while one was open for 14% -> 15% of each run, Pallas kernels for 0% -> 0%
where the time goes in v10:
time: 77.9 us; the launch traced here: 77.1 us
  starting transfers between devices  30.5 us (39%)
  waiting for transfers between devices  26.1 us (34%)
  local copies, waits for them, and re-layouts  10.4 us (13%)
  matrix products  5.23 us (7%)
  other arithmetic  4.32 us (6%)
    all_to_all x1, starting transfers between devices, gather_cache(): lax.all_to_all(outgoing, ('y', 'zh', 'tp'), split_axis=0, concat_axis=3,...  17.1 us
    ppermute x3, waiting for transfers between devices, shift(): lax.ppermute(held, 'x', [(i, (i + step) % count) for i in range(count)])  16.7 us
    ppermute x3, starting transfers between devices, shift(): lax.ppermute(held, 'x', [(i, (i + step) % count) for i in range(count)])  9.93 us
    all_to_all x1, waiting for transfers between devices, gather_cache(): lax.all_to_all(outgoing, ('y', 'zh', 'tp'), split_axis=0, concat_axis=3,...  8.14 us
    ppermute x1, starting transfers between devices, gather_cache(): lax.ppermute(jnp.concatenate([held for held, _ in everything], axis=2), '...  3.46 us
    dot_general x6, matrix products, fold_block(): jnp.einsum('thep,hpd->thed', weights.astype(jnp.bfloat16), values, prefer...  2.96 us
    dot_general x6, matrix products, fold_block(): jnp.einsum('thed,hpd->thep', query_rows, keys, preferred_element_type=jnp...  2.27 us
    reduce_sum x6, other arithmetic, fold_block(): total = jnp.sum(weights, axis=-1)  1.93 us
  transfers between devices with their start and end apart: 5, of which 4 were waited for; matrix products, arithmetic and copies ran while one was open for 15% of the time, Pallas kernels for 0%

profile of v10, /device:TPU:1, one launch (start us, length us, event | category | flops | bytes accessed | tf_op | source)
XLA Modules:
  0.0 77.1 jit_solution(8132057890899931394)
XLA Ops:
  0.0 0.8 %reshape.445 = bf16[4,4,4,2,128]{4,3,2,1,0:T(2,128)(2,1)S(1)} reshape(bf16[4,4096]{1,0:T(4,128)(2,1)} %param.12) | data formatting | bytes 65536 | tf_op jit(solution)/shard_map/reshape | solution.py:26
  0.8 1.0 %broadcast_in_dim.214 = bf16[16,4,2,4,4,128]{5,4,3,2,1,0:T(4,128)(2,1)} broadcast(bf16[4,2,4,4,128]{4,3,2,1,0:T(4,128)(2,1)S(1)} %copy.113), dimensions={1,2,3,4,5} | broadcast | bytes 557056 | tf_op jit(solution)/shard_map/broadcast_in_dim | solution.py:28
  1.8 17.1 %all-to-all-start = ((bf16[64,2,4,4,128]{4,3,2,1,0:T(4,128)(2,1)}), bf16[64,2,4,4,128]{4,3,2,1,0:T(4,128)(2,1)S(1)}, u32[]{:S(2)}, u32[]{:S(2)}) async-start(bf16[64,2,4,4,128]{4,3,2,1,0:T(4,128)(2,1)} %bitcast.18), calls=%async_computation | async-start | bytes 1048576 | tf_op jit(solution)/shard_map/all_to_all | solution.py:30
  19.1 0.8 %reduce-window.4 = s32[4,1]{0,1:T(1,128)S(1)} reduce-window(s32[4,1]{0,1:T(1,128)} %bitcast.246, s32[]{:T(128)} %constant.73.clone.1), window={size=4x1 pad=3_0x0_0}, to_apply=%region_0.0 | reduce-window | flops 12 | bytes 36 | tf_op jit(solution)/shard_map/reduce-window
  19.9 0.8 %reshape.443 = s32[4,2,8,2,4]{4,3,2,1,0:T(2,128)S(1)} reshape(s32[512]{0:T(512)} %param.13) | data formatting | bytes 4096 | tf_op jit(solution)/shard_map/reshape | solution.py:40
  20.8 0.1 copy.130
  20.9 0.1 copy.125
  21.0 0.1 copy.138
  21.1 0.1 reshape.456
  21.3 0.1 reshape.457
  21.4 0.1 copy.137
  21.5 0.1 reshape.454
  21.7 0.1 reshape.455
  21.8 0.1 copy.119
  21.9 0.1 copy.111
  22.0 0.1 copy.136
  22.1 0.1 reshape.452
  22.3 0.1 reshape.453
  22.5 0.1 reshape.450
  22.6 0.1 reshape.451
  22.8 0.6 slice.42
  23.3 1.1 %reshape.442 = bf16[128,4,2,128]{3,2,1,0:T(2,128)(2,1)S(1)} reshape(bf16[128,1024]{1,0:T(8,128)(2,1)} %param.10) | data formatting | bytes 524288 | tf_op jit(solution)/shard_map/reshape | solution.py:99
  24.7 0.1 eq.133
  24.9 0.1 reshape.447
  25.1 0.1 eq.136
  25.3 0.1 reshape.448
  25.5 0.1 eq.139
  25.7 0.1 reshape.449
  25.9 0.1 eq.142
  26.0 1.1 %copy.106 = bf16[128,1024]{0,1:T(8,128)(2,1)S(1)} copy(bf16[128,1024]{1,0:T(8,128)(2,1)} %param.11) | data formatting | bytes 524288 | tf_op args[1]
  27.1 0.1 copy.172
  27.3 8.1 %all-to-all-done = bf16[64,2,4,4,128]{4,3,2,1,0:T(4,128)(2,1)S(1)} async-done(((bf16[64,2,4,4,128]{4,3,2,1,0:T(4,128)(2,1)}), bf16[64,2,4,4,128]{4,3,2,1,0:T(4,128)(2,1)S(1)}, u32[]{:S(2)}, u32[]{:S(2)}) %all-to-all-start) | async-done | bytes 524320 | tf_op jit(solution)/shard_map/all_to_all | solution.py:30
  35.4 0.2 copy.121
  35.6 4.7 %collective-permute-start.2 = (bf16[2,4,256,128]{3,2,1,0:T(8,128)(2,1)S(1)}, bf16[2,4,256,128]{3,2,1,0:T(8,128)(2,1)S(1)}, u32[]{:S(2)}, u32[]{:S(2)}) collective-permute-start(bf16[2,4,256,128]{3,2,1,0:T(8,128)(2,1)S(1)} %bitcast.210), channel_id=1, source_target_pairs={{0,256},{128,384},{256,0},{384,128},{1,257},{129,385},{257,1},{385... | collective-permute-start | bytes 1572872 | tf_op jit(solution)/shard_map/ppermute | solution.py:37
  40.3 2.8 %collective-permute-start.1 = (bf16[2,4,256,128]{3,2,1,0:T(8,128)(2,1)S(1)}, bf16[2,4,256,128]{3,2,1,0:T(8,128)(2,1)S(1)}, u32[]{:S(2)}, u32[]{:S(2)}) collective-permute-start(bf16[2,4,256,128]{3,2,1,0:T(8,128)(2,1)S(1)} %bitcast.211), channel_id=1, source_target_pairs={{0,384},{128,0},{256,128},{384,256},{1,385},{129,1},{257,129},{385... | collective-permute-start | bytes 1572872 | tf_op jit(solution)/shard_map/ppermute | solution.py:37
  43.1 2.5 %collective-permute-start = (bf16[2,4,256,128]{3,2,1,0:T(8,128)(2,1)S(1)}, bf16[2,4,256,128]{3,2,1,0:T(8,128)(2,1)S(1)}, u32[]{:S(2)}, u32[]{:S(2)}) collective-permute-start(bf16[2,4,256,128]{3,2,1,0:T(8,128)(2,1)S(1)} %bitcast.212), channel_id=1, source_target_pairs={{0,128},{128,256},{256,384},{384,0},{1,129},{129,257},{257,385},{3... | collective-permute-start | bytes 1572872 | tf_op jit(solution)/shard_map/ppermute | solution.py:37
  45.6 0.7 iota_compare_fusion.3
  46.5 2.4 %collective-permute-done.2 = bf16[2,4,256,128]{3,2,1,0:T(8,128)(2,1)S(1)} collective-permute-done((bf16[2,4,256,128]{3,2,1,0:T(8,128)(2,1)S(1)}, bf16[2,4,256,128]{3,2,1,0:T(8,128)(2,1)S(1)}, u32[]{:S(2)}, u32[]{:S(2)}) %collective-permute-start.2) | collective-permute-done | bytes 524320 | tf_op jit(solution)/shard_map/ppermute | solution.py:37
  48.9 14.3 %collective-permute-done.1 = bf16[2,4,256,128]{3,2,1,0:T(8,128)(2,1)S(1)} collective-permute-done((bf16[2,4,256,128]{3,2,1,0:T(8,128)(2,1)S(1)}, bf16[2,4,256,128]{3,2,1,0:T(8,128)(2,1)S(1)}, u32[]{:S(2)}, u32[]{:S(2)}) %collective-permute-start.1) | collective-permute-done | bytes 524320 | tf_op jit(solution)/shard_map/ppermute | solution.py:37
  63.2 0.1 pad_maximum_fusion
  63.3 3.5 %collective-permute-start.3 = (bf16[2,4,1024,128]{3,2,1,0:T(8,128)(2,1)S(1)}, bf16[2,4,1024,128]{3,2,1,0:T(8,128)(2,1)S(1)}, u32[]{:S(2)}, u32[]{:S(2)}) collective-permute-start(bf16[2,4,1024,128]{3,2,1,0:T(8,128)(2,1)S(1)} %pad_maximum_fusion), channel_id=1, source_target_pairs={{0,4},{4,0},{1,5},{5,1},{2,6},{6,2},{3,7},{7,3},{8,12},{12,8},{9,1... | collective-permute-start | bytes 6291464 | tf_op jit(solution)/shard_map/ppermute | solution.py:50
  66.8 0.3 fusion.85
  67.0 0.1 fusion.57
  67.1 0.2 compare_and_fusion
  67.4 0.2 compare_and_fusion.4
  67.6 0.2 fusion.81
  68.0 0.3 fusion.86
  68.3 0.3 fusion.82
  68.6 0.3 fusion.83
  68.9 0.3 fusion.84
  69.2 1.3 %collective-permute-done.3 = bf16[2,4,1024,128]{3,2,1,0:T(8,128)(2,1)S(1)} collective-permute-done((bf16[2,4,1024,128]{3,2,1,0:T(8,128)(2,1)S(1)}, bf16[2,4,1024,128]{3,2,1,0:T(8,128)(2,1)S(1)}, u32[]{:S(2)}, u32[]{:S(2)}) %collective-permute-start.3) | collective-permute-done | bytes 2097184 | tf_op jit(solution)/shard_map/ppermute | solution.py:50
  70.5 0.8 fusion
  71.3 0.2 fusion.33
  71.5 0.3 convolution_bitcast_fusion.4
  71.9 1.0 %fusion.1 = f32[128,4,2]{0,2,1:T(2,128)S(1)} fusion(f32[4,1024,128,2]{2,1,3,0:T(8,128)S(1)} %get-tuple-element.59, f32[128,4,2]{0,2,1:T(2,128)S(1)} %bitcast.234, pred[128,1024]{0,1:T(8,128)(4,1)S(1)} %compare_and_fusion), kind=kLoop, calls=%fused_computation.3 | loop fusion | flops 5241856 | bytes 4333568 | tf_op jit(solution)/shard_map/reduce_sum | solution.py:68
  72.9 0.2 fusion.39
  73.1 0.2 fusion.37
  73.3 0.2 fusion.35
  73.5 0.3 fusion.19
  73.8 1.3 %fusion.14 = f32[128,4,2,128]{0,3,2,1:T(8,128)S(1)} fusion(f32[4,1024,128,2]{2,1,3,0:T(8,128)S(1)} %get-tuple-element.59, f32[128,4,2]{0,2,1:T(2,128)S(1)} %bitcast.236, pred[128,1024]{0,1:T(8,128)(4,1)S(1)} %compare_and_fusion, bf16[2,4,1024,128]{3,2,1,0:T(8,128)(2,1)S(1)} %collective-permute-done.3), kind=kOutput, calls=%fused_computation.20 | convolution fusion | flops 273678336 | bytes 5902336 | tf_op jit(solution)/shard_map/thep,hpd->thed/dot_general | solution.py:65
  75.1 0.3 convolution_bitcast_fusion.1
  75.4 0.3 convolution_bitcast_fusion.2
  75.8 0.4 fusion.31
  76.2 0.9 %copy.142 = bf16[128,1024]{1,0:T(8,128)(2,1)} copy(bf16[128,1024]{0,1:T(8,128)(2,1)S(1)} %bitcast.218) | data formatting | bytes 524288 | tf_op jit(solution)/shard_map/reshape | solution.py:116
  (30 shorter events, 1.7 us)
Async XLA Ops:
  0.0 46.3 %copy-start = (s32[4]{0:T(128)S(1)}, s32[4]{0:T(128)}, u32[]{:S(2)}) copy-start(s32[4]{0:T(128)} %param.15) | copy-start | bytes 52
  1.8 33.6 %all-to-all-start = ((bf16[64,2,4,4,128]{4,3,2,1,0:T(4,128)(2,1)}), bf16[64,2,4,4,128]{4,3,2,1,0:T(4,128)(2,1)S(1)}, u32[]{:S(2)}, u32[]{:S(2)}) async-start(bf16[64,2,4,4,128]{4,3,2,1,0:T(4,128)(2,1)} %bitcast.18), calls=%async_computation | async-start | bytes 1048576 | tf_op jit(solution)/shard_map/all_to_all | solution.py:30
  35.6 13.3 %collective-permute-start.2 = (bf16[2,4,256,128]{3,2,1,0:T(8,128)(2,1)S(1)}, bf16[2,4,256,128]{3,2,1,0:T(8,128)(2,1)S(1)}, u32[]{:S(2)}, u32[]{:S(2)}) collective-permute-start(bf16[2,4,256,128]{3,2,1,0:T(8,128)(2,1)S(1)} %bitcast.210), channel_id=1, source_target_pairs={{0,256},{128,384},{256,0},{384,128},{1,257},{129,385},{257,1},{385... | collective-permute-start | bytes 1572872 | tf_op jit(solution)/shard_map/ppermute | solution.py:37
  40.3 22.9 %collective-permute-start.1 = (bf16[2,4,256,128]{3,2,1,0:T(8,128)(2,1)S(1)}, bf16[2,4,256,128]{3,2,1,0:T(8,128)(2,1)S(1)}, u32[]{:S(2)}, u32[]{:S(2)}) collective-permute-start(bf16[2,4,256,128]{3,2,1,0:T(8,128)(2,1)S(1)} %bitcast.211), channel_id=1, source_target_pairs={{0,384},{128,0},{256,128},{384,256},{1,385},{129,1},{257,129},{385... | collective-permute-start | bytes 1572872 | tf_op jit(solution)/shard_map/ppermute | solution.py:37
  43.1 20.1 %collective-permute-start = (bf16[2,4,256,128]{3,2,1,0:T(8,128)(2,1)S(1)}, bf16[2,4,256,128]{3,2,1,0:T(8,128)(2,1)S(1)}, u32[]{:S(2)}, u32[]{:S(2)}) collective-permute-start(bf16[2,4,256,128]{3,2,1,0:T(8,128)(2,1)S(1)} %bitcast.212), channel_id=1, source_target_pairs={{0,128},{128,256},{256,384},{384,0},{1,129},{129,257},{257,385},{3... | collective-permute-start | bytes 1572872 | tf_op jit(solution)/shard_map/ppermute | solution.py:37
  63.3 7.2 %collective-permute-start.3 = (bf16[2,4,1024,128]{3,2,1,0:T(8,128)(2,1)S(1)}, bf16[2,4,1024,128]{3,2,1,0:T(8,128)(2,1)S(1)}, u32[]{:S(2)}, u32[]{:S(2)}) collective-permute-start(bf16[2,4,1024,128]{3,2,1,0:T(8,128)(2,1)S(1)} %pad_maximum_fusion), channel_id=1, source_target_pairs={{0,4},{4,0},{1,5},{5,1},{2,6},{6,2},{3,7},{7,3},{8,12},{12,8},{9,1... | collective-permute-start | bytes 6291464 | tf_op jit(solution)/shard_map/ppermute | solution.py:50

commit v11 on v10

--- a/solution.py
+++ b/solution.py
@@ -44,10 +44,10 @@
         line = jnp.take(grid, (here + offset) % count, axis=0)
         return jnp.repeat(jnp.take(line, which, axis=2).reshape(-1), block_rows)
 
-    blocks = [(mine, owner_of(0, core))]
-    blocks += [(held, owner_of(offset, core)) for held, offset in arrived]
     everything = [(mine, 0)] + arrived
-    forwarded = lax.ppermute(jnp.concatenate([held for held, _ in everything], axis=2), "core", swap)
+    own_rows = jnp.concatenate([held for held, _ in everything], axis=2)
+    forwarded = lax.ppermute(own_rows, "core", swap)
+    blocks = [(own_rows, jnp.concatenate([owner_of(offset, core) for _, offset in everything]))]
     blocks.append((forwarded, jnp.concatenate([owner_of(offset, 1 - core) for _, offset in everything])))
     return blocks
 

time: 77.9 us -> 85.2 us (1.094)
  blocking collectives: 0 us -> 33.4 us
  starting transfers between devices: 30.5 us -> 13.4 us
  waiting for transfers between devices: 26.1 us -> 15.2 us
  matrix products: 5.23 us -> 7.1 us
  other arithmetic: 4.32 us -> 5.69 us
  local copies, waits for them, and re-layouts: 10.4 us -> 9.13 us
    all_to_all x0 -> x1, blocking collectives: none -> 33.4 us  [gather_cache(): lax.all_to_all(outgoing, ('y', 'zh', 'tp'), split_axis=0, concat_axis=3,...]
    all_to_all x1 -> x0, starting transfers between devices: 17.1 us -> none  [gather_cache(): lax.all_to_all(outgoing, ('y', 'zh', 'tp'), split_axis=0, concat_axis=3,...]
    all_to_all x1 -> x0, waiting for transfers between devices: 8.14 us -> none  [gather_cache(): lax.all_to_all(outgoing, ('y', 'zh', 'tp'), split_axis=0, concat_axis=3,...]
    ppermute x3, waiting for transfers between devices: 16.7 us -> 15.2 us  [shift(): lax.ppermute(held, 'x', [(i, (i + step) % count) for i in range(count)])]
    ppermute x1, waiting for transfers between devices: 1.29 us -> 0.01 us  [gather_cache(): forwarded = lax.ppermute(own_rows, 'core', swap)]
    concatenate x1 -> x2, other arithmetic: 0.14 us -> 1.36 us  [the longest x1 1.35 us: gather_cache(): own_rows = jnp.concatenate([held for held, _ in everything], axis=2)]
    dot_general x6 -> x3, matrix products: 2.96 us -> 4.1 us  [fold_block(): jnp.einsum('thep,hpd->thed', weights.astype(jnp.bfloat16), values, prefer...]
    reshape x1, local copies, waits for them, and re-layouts: 1.12 us -> 0.17 us  [per_device(): query_rows = queries.reshape(token_rows, local_heads, 2, HEAD)]
  transfers between devices with their start and end apart: 5 -> 4, of which waited for: 4 -> 2; matrix products, arithmetic and copies ran while one was open for 15% -> 11% of each run, Pallas kernels for 0% -> 0%
where the time goes in v11:
time: 85.2 us; the launch traced here: 84.3 us
  blocking collectives  33.4 us (39%)
  waiting for transfers between devices  15.2 us (18%)
  starting transfers between devices  13.4 us (16%)
  local copies, waits for them, and re-layouts  9.13 us (11%)
  matrix products  7.1 us (8%)
  other arithmetic  5.69 us (7%)
    all_to_all x1, blocking collectives, gather_cache(): lax.all_to_all(outgoing, ('y', 'zh', 'tp'), split_axis=0, concat_axis=3,...  33.4 us
    ppermute x3, waiting for transfers between devices, shift(): lax.ppermute(held, 'x', [(i, (i + step) % count) for i in range(count)])  15.2 us
    ppermute x3, starting transfers between devices, shift(): lax.ppermute(held, 'x', [(i, (i + step) % count) for i in range(count)])  9.94 us
    dot_general x3, matrix products, fold_block(): jnp.einsum('thep,hpd->thed', weights.astype(jnp.bfloat16), values, prefer...  4.1 us
    ppermute x1, starting transfers between devices, gather_cache(): forwarded = lax.ppermute(own_rows, 'core', swap)  3.46 us
    dot_general x3, matrix products, fold_block(): jnp.einsum('thed,hpd->thep', query_rows, keys, preferred_element_type=jnp...  3 us
    reduce_sum x3, other arithmetic, fold_block(): total = jnp.sum(weights, axis=-1)  2.16 us
    unnamed x8, local copies, waits for them, and re-layouts  2.05 us
  transfers between devices with their start and end apart: 4, of which 2 were waited for; matrix products, arithmetic and copies ran while one was open for 11% of the time, Pallas kernels for 0%

profile of v11, /device:TPU:1, one launch (start us, length us, event | category | flops | bytes accessed | tf_op | source)
XLA Modules:
  0.0 84.3 jit_solution(14734390335637886841)
XLA Ops:
  0.0 0.8 %reshape.262 = bf16[4,4,4,2,128]{4,3,2,1,0:T(2,128)(2,1)S(1)} reshape(bf16[4,4096]{1,0:T(4,128)(2,1)} %param.12) | data formatting | bytes 65536 | tf_op jit(solution)/shard_map/reshape | solution.py:26
  0.9 0.2 broadcast_in_dim.165
  1.1 33.4 %all_to_all.15 = bf16[64,2,4,4,128]{4,3,2,1,0:T(4,128)(2,1)S(1)} all-to-all(bf16[64,2,4,4,128]{4,3,2,1,0:T(4,128)(2,1)S(1)} %bitcast.157), channel_id=1, replica_groups=mesh['x'=4,'zh'=2,'y'=8,'core'=2,'tp'=4] {'y','zh','tp'}, dimensions={0} | all-to-all | bytes 1048576 | tf_op jit(solution)/shard_map/all_to_all | solution.py:30
  34.5 0.2 copy.91
  34.7 4.7 %collective-permute-start.2 = (bf16[2,4,256,128]{3,2,1,0:T(8,128)(2,1)S(1)}, bf16[2,4,256,128]{3,2,1,0:T(8,128)(2,1)S(1)}, u32[]{:S(2)}, u32[]{:S(2)}) collective-permute-start(bf16[2,4,256,128]{3,2,1,0:T(8,128)(2,1)S(1)} %bitcast.159), channel_id=1, source_target_pairs={{0,256},{128,384},{256,0},{384,128},{1,257},{129,385},{257,1},{385... | collective-permute-start | bytes 1572872 | tf_op jit(solution)/shard_map/ppermute | solution.py:37
  39.3 2.8 %collective-permute-start.1 = (bf16[2,4,256,128]{3,2,1,0:T(8,128)(2,1)S(1)}, bf16[2,4,256,128]{3,2,1,0:T(8,128)(2,1)S(1)}, u32[]{:S(2)}, u32[]{:S(2)}) collective-permute-start(bf16[2,4,256,128]{3,2,1,0:T(8,128)(2,1)S(1)} %bitcast.160), channel_id=1, source_target_pairs={{0,384},{128,0},{256,128},{384,256},{1,385},{129,1},{257,129},{385... | collective-permute-start | bytes 1572872 | tf_op jit(solution)/shard_map/ppermute | solution.py:37
  42.1 2.5 %collective-permute-start = (bf16[2,4,256,128]{3,2,1,0:T(8,128)(2,1)S(1)}, bf16[2,4,256,128]{3,2,1,0:T(8,128)(2,1)}, u32[]{:S(2)}, u32[]{:S(2)}) collective-permute-start(bf16[2,4,256,128]{3,2,1,0:T(8,128)(2,1)S(1)} %bitcast.161), channel_id=1, source_target_pairs={{0,128},{128,256},{256,384},{384,0},{1,129},{129,257},{257,385},{3... | collective-permute-start | bytes 1572872 | tf_op jit(solution)/shard_map/ppermute | solution.py:37
  44.7 0.8 reduce-window.4
  45.5 0.6 slice.22
  46.1 0.8 reshape.253
  47.0 1.0 %collective-permute-done.2 = bf16[2,4,256,128]{3,2,1,0:T(8,128)(2,1)S(1)} collective-permute-done((bf16[2,4,256,128]{3,2,1,0:T(8,128)(2,1)S(1)}, bf16[2,4,256,128]{3,2,1,0:T(8,128)(2,1)S(1)}, u32[]{:S(2)}, u32[]{:S(2)}) %collective-permute-start.2) | collective-permute-done | bytes 524320 | tf_op jit(solution)/shard_map/ppermute | solution.py:37
  47.9 14.3 %collective-permute-done.1 = bf16[2,4,256,128]{3,2,1,0:T(8,128)(2,1)S(1)} collective-permute-done((bf16[2,4,256,128]{3,2,1,0:T(8,128)(2,1)S(1)}, bf16[2,4,256,128]{3,2,1,0:T(8,128)(2,1)S(1)}, u32[]{:S(2)}, u32[]{:S(2)}) %collective-permute-start.1) | collective-permute-done | bytes 524320 | tf_op jit(solution)/shard_map/ppermute | solution.py:37
  62.2 0.8 copy-done
  63.0 1.3 %pad_maximum_fusion = bf16[2,4,1024,128]{3,2,1,0:T(8,128)(2,1)S(1)} fusion(bf16[2,4,256,128]{3,2,1,0:T(8,128)(2,1)S(1)} %collective-permute-done.2, bf16[2,4,256,128]{3,2,1,0:T(8,128)(2,1)} %copy-done, bf16[2,4,256,128]{3,2,1,0:T(8,128)(2,1)} %collective-permute-done, bf16[2,4,256,128]{3,2,1,0:T(8,128)(2,1)S(1)} %bitcast.162), kind=kLoop, calls=%fused_computation.10 | loop fusion | flops 8388608 | bytes 4194304 | tf_op jit(solution)/shard_map/concatenate | solution.py:48
  64.4 3.5 %collective-permute-start.3 = (bf16[2,4,1024,128]{3,2,1,0:T(8,128)(2,1)S(1)}, bf16[2,4,1024,128]{3,2,1,0:T(8,128)(2,1)}, u32[]{:S(2)}, u32[]{:S(2)}) collective-permute-start(bf16[2,4,1024,128]{3,2,1,0:T(8,128)(2,1)S(1)} %pad_maximum_fusion), channel_id=1, source_target_pairs={{0,4},{4,0},{1,5},{5,1},{2,6},{6,2},{3,7},{7,3},{8,12},{12,8},{9,1... | collective-permute-start | bytes 6291464 | tf_op jit(solution)/shard_map/ppermute | solution.py:49
  67.9 0.1 copy.82
  68.0 0.1 copy.88
  68.1 0.1 copy.86
  68.2 0.1 copy.89
  68.3 0.1 reshape.260
  68.4 0.1 copy.98
  68.5 0.1 reshape.270
  68.6 0.1 copy.97
  68.7 0.1 reshape.268
  68.8 0.1 copy.87
  68.9 0.1 reshape.258
  69.0 0.1 copy.84
  69.1 0.1 copy.85
  69.2 0.1 reshape.256
  69.3 0.1 copy.96
  69.4 0.1 reshape.266
  69.5 0.1 copy.95
  69.6 0.1 reshape.264
  69.7 0.1 copy.83
  69.8 0.1 reshape.254
  69.8 0.1 broadcast_in_dim.160
  69.9 0.1 reshape.255
  70.0 0.1 broadcast_in_dim.168
  70.1 0.1 reshape.265
  70.2 0.1 broadcast_in_dim.169
  70.3 0.1 reshape.267
  70.5 0.1 reshape.257
  70.7 0.1 reshape.259
  70.9 0.1 reshape.269
  71.0 0.1 reshape.271
  71.2 0.1 reshape.261
  71.4 0.2 reshape.252
  71.5 1.1 %copy.77 = bf16[128,1024]{0,1:T(8,128)(2,1)S(1)} copy(bf16[128,1024]{1,0:T(8,128)(2,1)} %param.11) | data formatting | bytes 524288 | tf_op args[1]
  72.7 0.1 copy.117
  72.8 0.7 iota_compare_fusion.3
  73.5 0.1 convert_reduce_fusion
  73.6 0.1 select_reduce_fusion
  73.7 0.1 fusion.52
  73.8 0.2 fusion.61
  74.0 0.1 fusion.41
  74.1 0.3 compare_and_fusion.1
  74.5 0.8 fusion
  75.3 2.0 %fusion.1 = (f32[128,4,2]{0,2,1:T(2,128)S(1)}, f32[4,1024,128,2]{2,1,3,0:T(8,128)S(1)}) fusion(pred[128,1024]{0,1:T(8,128)(4,1)S(1)} %get-tuple-element.47, bf16[128,4,2,128]{3,2,1,0:T(2,128)(2,1)S(1)} %reshape.252, bf16[2,4,1024,128]{3,2,1,0:T(8,128)(2,1)} %collective-permute-done.3), kind=kOutput, calls=%fused_computation.5 | convolution fusion | flops 271580160 | bytes 5640192 | tf_op jit(solution)/shard_map/thed,hpd->thep/dot_general | solution.py:56
  77.3 1.0 %fusion.4 = f32[128,4,2]{0,2,1:T(2,128)S(1)} fusion(f32[4,1024,128,2]{2,1,3,0:T(8,128)S(1)} %get-tuple-element.49, f32[128,4,2]{0,2,1:T(2,128)S(1)} %bitcast.169, pred[128,1024]{0,1:T(8,128)(4,1)S(1)} %get-tuple-element.47), kind=kLoop, calls=%fused_computation.8 | loop fusion | flops 5241856 | bytes 4333568 | tf_op jit(solution)/shard_map/reduce_sum | solution.py:68
  78.3 1.0 %fusion.2 = f32[128,4,2]{0,2,1:T(2,128)S(1)} fusion(f32[4,1024,128,2]{2,1,3,0:T(8,128)S(1)} %get-tuple-element.53, f32[128,4,2]{0,2,1:T(2,128)S(1)} %bitcast.172, pred[128,1024]{0,1:T(8,128)(4,1)S(1)} %get-tuple-element.46), kind=kLoop, calls=%fused_computation.6 | loop fusion | flops 5241856 | bytes 4333568 | tf_op jit(solution)/shard_map/reduce_sum | solution.py:68
  79.3 0.2 fusion.18
  79.6 1.3 %fusion.27 = f32[128,4,2,128]{0,3,2,1:T(8,128)S(1)} fusion(f32[128,4,2,128]{0,3,2,1:T(8,128)S(1)} %fusion.18, f32[4,1024,128,2]{2,1,3,0:T(8,128)S(1)} %get-tuple-element.53, f32[128,4,2]{0,2,1:T(2,128)S(1)} %bitcast.174, pred[128,1024]{0,1:T(8,128)(4,1)S(1)} %get-tuple-element.46, bf16[2,4,1024,128]{3,2,1,0:T(8,128)(2,1)S(1)} %pad_maximum_fusion, ...), kind=kOutput, calls=%fused_computation.24 | convolution fusion | flops 273940480 | bytes 6430720 | tf_op jit(solution)/shard_map/thep,hpd->thed/dot_general | solution.py:65
  80.9 2.5 %fusion.38 = bf16[128,4,2,128]{0,3,2,1:T(8,128)(2,1)S(1)} fusion(f32[128,4,2,128]{0,3,2,1:T(8,128)S(1)} %fusion.27, f32[4,1024,128,2]{2,1,3,0:T(8,128)S(1)} %get-tuple-element.49, f32[128,4,2]{0,2,1:T(2,128)S(1)} %bitcast.171, pred[128,1024]{0,1:T(8,128)(4,1)S(1)} %get-tuple-element.47, bf16[2,4,1024,128]{3,2,1,0:T(8,128)(2,1)} %collective-permute-done.3, ...), kind=kOutput, calls=%fused_computation.33 | convolution fusion | flops 274202624 | bytes 6168704 | tf_op jit(solution)/shard_map/thep,hpd->thed/dot_general | solution.py:65
  83.5 0.8 %copy.102 = bf16[128,1024]{1,0:T(8,128)(2,1)} copy(bf16[128,1024]{0,1:T(8,128)(2,1)S(1)} %bitcast.165) | data formatting | bytes 524288 | tf_op jit(solution)/shard_map/reshape | solution.py:116
  (21 shorter events, 0.5 us)
Async XLA Ops:
  0.0 71.3 %copy-start.1 = (bf16[128,1024]{1,0:T(8,128)(2,1)S(1)}, bf16[128,1024]{1,0:T(8,128)(2,1)}, u32[]{:S(2)}) copy-start(bf16[128,1024]{1,0:T(8,128)(2,1)} %param.10) | copy-start | bytes 786436
  34.5 39.1 %copy-start.2 = (s32[4]{0:T(128)S(1)}, s32[4]{0:T(128)}, u32[]{:S(2)}) copy-start(s32[4]{0:T(128)} %param.15) | copy-start | bytes 52
  34.7 13.3 %collective-permute-start.2 = (bf16[2,4,256,128]{3,2,1,0:T(8,128)(2,1)S(1)}, bf16[2,4,256,128]{3,2,1,0:T(8,128)(2,1)S(1)}, u32[]{:S(2)}, u32[]{:S(2)}) collective-permute-start(bf16[2,4,256,128]{3,2,1,0:T(8,128)(2,1)S(1)} %bitcast.159), channel_id=1, source_target_pairs={{0,256},{128,384},{256,0},{384,128},{1,257},{129,385},{257,1},{385... | collective-permute-start | bytes 1572872 | tf_op jit(solution)/shard_map/ppermute | solution.py:37
  39.3 22.9 %collective-permute-start.1 = (bf16[2,4,256,128]{3,2,1,0:T(8,128)(2,1)S(1)}, bf16[2,4,256,128]{3,2,1,0:T(8,128)(2,1)S(1)}, u32[]{:S(2)}, u32[]{:S(2)}) collective-permute-start(bf16[2,4,256,128]{3,2,1,0:T(8,128)(2,1)S(1)} %bitcast.160), channel_id=1, source_target_pairs={{0,384},{128,0},{256,128},{384,256},{1,385},{129,1},{257,129},{385... | collective-permute-start | bytes 1572872 | tf_op jit(solution)/shard_map/ppermute | solution.py:37
  42.1 20.9 %collective-permute-start = (bf16[2,4,256,128]{3,2,1,0:T(8,128)(2,1)S(1)}, bf16[2,4,256,128]{3,2,1,0:T(8,128)(2,1)}, u32[]{:S(2)}, u32[]{:S(2)}) collective-permute-start(bf16[2,4,256,128]{3,2,1,0:T(8,128)(2,1)S(1)} %bitcast.161), channel_id=1, source_target_pairs={{0,128},{128,256},{256,384},{384,0},{1,129},{129,257},{257,385},{3... | collective-permute-start | bytes 1572872 | tf_op jit(solution)/shard_map/ppermute | solution.py:37
  62.2 0.8 copy-start
  64.4 10.9 %collective-permute-start.3 = (bf16[2,4,1024,128]{3,2,1,0:T(8,128)(2,1)S(1)}, bf16[2,4,1024,128]{3,2,1,0:T(8,128)(2,1)}, u32[]{:S(2)}, u32[]{:S(2)}) collective-permute-start(bf16[2,4,1024,128]{3,2,1,0:T(8,128)(2,1)S(1)} %pad_maximum_fusion), channel_id=1, source_target_pairs={{0,4},{4,0},{1,5},{5,1},{2,6},{6,2},{3,7},{7,3},{8,12},{12,8},{9,1... | collective-permute-start | bytes 6291464 | tf_op jit(solution)/shard_map/ppermute | solution.py:49

commit v12 on v10

--- a/solution.py
+++ b/solution.py
@@ -36,7 +36,7 @@
     def shift(held, step):
         return lax.ppermute(held, "x", [(i, (i + step) % count) for i in range(count)])
 
-    arrived = [(shift(mine, step), -step) for step in (1, -1, 2)]
+    arrived = [(shift(mine, step), -step) for step in (2, 1, -1)]
     grid = block_prefix.reshape(size["x"], size["zh"], size["y"], size["core"], tensor_count)
     grid = grid.transpose(0, 2, 1, 3, 4)
 

time: 77.9 us -> 81.9 us (1.051)
  starting transfers between devices: 30.5 us -> 34.6 us
    ppermute x1, starting transfers between devices: 3.46 us -> 7.55 us  [gather_cache(): lax.ppermute(jnp.concatenate([held for held, _ in everything], axis=2), '...]
  transfers between devices with their start and end apart: 5 -> 5, of which waited for: 4 -> 5; matrix products, arithmetic and copies ran while one was open for 15% -> 14% of each run, Pallas kernels for 0% -> 0%
where the time goes in v12:
time: 81.9 us; the launch traced here: 81 us
  starting transfers between devices  34.6 us (42%)
  waiting for transfers between devices  26 us (32%)
  local copies, waits for them, and re-layouts  10.4 us (13%)
  matrix products  5.24 us (6%)
  other arithmetic  4.32 us (5%)
    all_to_all x1, starting transfers between devices, gather_cache(): lax.all_to_all(outgoing, ('y', 'zh', 'tp'), split_axis=0, concat_axis=3,...  17.1 us
    ppermute x3, waiting for transfers between devices, shift(): lax.ppermute(held, 'x', [(i, (i + step) % count) for i in range(count)])  16.6 us
    ppermute x3, starting transfers between devices, shift(): lax.ppermute(held, 'x', [(i, (i + step) % count) for i in range(count)])  9.93 us
    all_to_all x1, waiting for transfers between devices, gather_cache(): lax.all_to_all(outgoing, ('y', 'zh', 'tp'), split_axis=0, concat_axis=3,...  8.14 us
    ppermute x1, starting transfers between devices, gather_cache(): lax.ppermute(jnp.concatenate([held for held, _ in everything], axis=2), '...  7.55 us
    dot_general x6, matrix products, fold_block(): jnp.einsum('thep,hpd->thed', weights.astype(jnp.bfloat16), values, prefer...  2.96 us
    dot_general x6, matrix products, fold_block(): jnp.einsum('thed,hpd->thep', query_rows, keys, preferred_element_type=jnp...  2.28 us
    reduce_sum x6, other arithmetic, fold_block(): total = jnp.sum(weights, axis=-1)  1.93 us
  transfers between devices with their start and end apart: 5, of which 5 were waited for; matrix products, arithmetic and copies ran while one was open for 14% of the time, Pallas kernels for 0%

profile of v12, /device:TPU:1, one launch (start us, length us, event | category | flops | bytes accessed | tf_op | source)
XLA Modules:
  0.0 81.0 jit_solution(2243120259258859310)
XLA Ops:
  0.0 0.8 %reshape.445 = bf16[4,4,4,2,128]{4,3,2,1,0:T(2,128)(2,1)S(1)} reshape(bf16[4,4096]{1,0:T(4,128)(2,1)} %param.12) | data formatting | bytes 65536 | tf_op jit(solution)/shard_map/reshape | solution.py:26
  0.8 1.0 %broadcast_in_dim.214 = bf16[16,4,2,4,4,128]{5,4,3,2,1,0:T(4,128)(2,1)} broadcast(bf16[4,2,4,4,128]{4,3,2,1,0:T(4,128)(2,1)S(1)} %copy.113), dimensions={1,2,3,4,5} | broadcast | bytes 557056 | tf_op jit(solution)/shard_map/broadcast_in_dim | solution.py:28
  1.8 17.1 %all-to-all-start = ((bf16[64,2,4,4,128]{4,3,2,1,0:T(4,128)(2,1)}), bf16[64,2,4,4,128]{4,3,2,1,0:T(4,128)(2,1)S(1)}, u32[]{:S(2)}, u32[]{:S(2)}) async-start(bf16[64,2,4,4,128]{4,3,2,1,0:T(4,128)(2,1)} %bitcast.18), calls=%async_computation | async-start | bytes 1048576 | tf_op jit(solution)/shard_map/all_to_all | solution.py:30
  19.1 0.8 %reduce-window.4 = s32[4,1]{0,1:T(1,128)S(1)} reduce-window(s32[4,1]{0,1:T(1,128)} %bitcast.246, s32[]{:T(128)} %constant.73.clone.1), window={size=4x1 pad=3_0x0_0}, to_apply=%region_0.0 | reduce-window | flops 12 | bytes 36 | tf_op jit(solution)/shard_map/reduce-window
  19.9 0.8 %reshape.443 = s32[4,2,8,2,4]{4,3,2,1,0:T(2,128)S(1)} reshape(s32[512]{0:T(512)} %param.13) | data formatting | bytes 4096 | tf_op jit(solution)/shard_map/reshape | solution.py:40
  20.8 0.1 copy.130
  20.9 0.1 copy.125
  21.0 0.1 copy.138
  21.1 0.1 reshape.456
  21.3 0.1 reshape.457
  21.5 0.1 reshape.454
  21.7 0.1 reshape.455
  21.8 0.1 copy.119
  21.9 0.1 copy.111
  22.0 0.1 copy.136
  22.1 0.1 reshape.452
  22.3 0.1 reshape.453
  22.5 0.1 reshape.450
  22.6 0.1 reshape.451
  22.8 0.6 slice.42
  23.3 1.1 %reshape.442 = bf16[128,4,2,128]{3,2,1,0:T(2,128)(2,1)S(1)} reshape(bf16[128,1024]{1,0:T(8,128)(2,1)} %param.10) | data formatting | bytes 524288 | tf_op jit(solution)/shard_map/reshape | solution.py:99
  24.7 0.1 eq.133
  24.9 0.1 reshape.447
  25.1 0.1 eq.136
  25.3 0.1 reshape.448
  25.5 0.1 eq.139
  25.7 0.1 reshape.449
  25.9 0.1 eq.142
  26.0 1.1 %copy.106 = bf16[128,1024]{0,1:T(8,128)(2,1)S(1)} copy(bf16[128,1024]{1,0:T(8,128)(2,1)} %param.11) | data formatting | bytes 524288 | tf_op args[1]
  27.1 0.1 copy.172
  27.3 8.1 %all-to-all-done = bf16[64,2,4,4,128]{4,3,2,1,0:T(4,128)(2,1)S(1)} async-done(((bf16[64,2,4,4,128]{4,3,2,1,0:T(4,128)(2,1)}), bf16[64,2,4,4,128]{4,3,2,1,0:T(4,128)(2,1)S(1)}, u32[]{:S(2)}, u32[]{:S(2)}) %all-to-all-start) | async-done | bytes 524320 | tf_op jit(solution)/shard_map/all_to_all | solution.py:30
  35.4 0.2 copy.121
  35.6 4.4 %collective-permute-start.2 = (bf16[2,4,256,128]{3,2,1,0:T(8,128)(2,1)S(1)}, bf16[2,4,256,128]{3,2,1,0:T(8,128)(2,1)S(1)}, u32[]{:S(2)}, u32[]{:S(2)}) collective-permute-start(bf16[2,4,256,128]{3,2,1,0:T(8,128)(2,1)S(1)} %bitcast.210), channel_id=1, source_target_pairs={{0,384},{128,0},{256,128},{384,256},{1,385},{129,1},{257,129},{385... | collective-permute-start | bytes 1572872 | tf_op jit(solution)/shard_map/ppermute | solution.py:37
  40.0 1.9 %collective-permute-start.1 = (bf16[2,4,256,128]{3,2,1,0:T(8,128)(2,1)S(1)}, bf16[2,4,256,128]{3,2,1,0:T(8,128)(2,1)S(1)}, u32[]{:S(2)}, u32[]{:S(2)}) collective-permute-start(bf16[2,4,256,128]{3,2,1,0:T(8,128)(2,1)S(1)} %bitcast.211), channel_id=1, source_target_pairs={{0,128},{128,256},{256,384},{384,0},{1,129},{129,257},{257,385},{3... | collective-permute-start | bytes 1572872 | tf_op jit(solution)/shard_map/ppermute | solution.py:37
  41.9 3.6 %collective-permute-start = (bf16[2,4,256,128]{3,2,1,0:T(8,128)(2,1)S(1)}, bf16[2,4,256,128]{3,2,1,0:T(8,128)(2,1)S(1)}, u32[]{:S(2)}, u32[]{:S(2)}) collective-permute-start(bf16[2,4,256,128]{3,2,1,0:T(8,128)(2,1)S(1)} %bitcast.212), channel_id=1, source_target_pairs={{0,256},{128,384},{256,0},{384,128},{1,257},{129,385},{257,1},{385... | collective-permute-start | bytes 1572872 | tf_op jit(solution)/shard_map/ppermute | solution.py:37
  45.6 0.7 iota_compare_fusion.3
  46.5 1.1 %collective-permute-done.2 = bf16[2,4,256,128]{3,2,1,0:T(8,128)(2,1)S(1)} collective-permute-done((bf16[2,4,256,128]{3,2,1,0:T(8,128)(2,1)S(1)}, bf16[2,4,256,128]{3,2,1,0:T(8,128)(2,1)S(1)}, u32[]{:S(2)}, u32[]{:S(2)}) %collective-permute-start.2) | collective-permute-done | bytes 524320 | tf_op jit(solution)/shard_map/ppermute | solution.py:37
  47.5 6.1 %collective-permute-done.1 = bf16[2,4,256,128]{3,2,1,0:T(8,128)(2,1)S(1)} collective-permute-done((bf16[2,4,256,128]{3,2,1,0:T(8,128)(2,1)S(1)}, bf16[2,4,256,128]{3,2,1,0:T(8,128)(2,1)S(1)}, u32[]{:S(2)}, u32[]{:S(2)}) %collective-permute-start.1) | collective-permute-done | bytes 524320 | tf_op jit(solution)/shard_map/ppermute | solution.py:37
  53.7 9.4 %collective-permute-done = bf16[2,4,256,128]{3,2,1,0:T(8,128)(2,1)S(1)} collective-permute-done((bf16[2,4,256,128]{3,2,1,0:T(8,128)(2,1)S(1)}, bf16[2,4,256,128]{3,2,1,0:T(8,128)(2,1)S(1)}, u32[]{:S(2)}, u32[]{:S(2)}) %collective-permute-start) | collective-permute-done | bytes 524320 | tf_op jit(solution)/shard_map/ppermute | solution.py:37
  63.1 0.1 pad_maximum_fusion
  63.2 7.5 %collective-permute-start.3 = (bf16[2,4,1024,128]{3,2,1,0:T(8,128)(2,1)S(1)}, bf16[2,4,1024,128]{3,2,1,0:T(8,128)(2,1)S(1)}, u32[]{:S(2)}, u32[]{:S(2)}) collective-permute-start(bf16[2,4,1024,128]{3,2,1,0:T(8,128)(2,1)S(1)} %pad_maximum_fusion), channel_id=1, source_target_pairs={{0,4},{4,0},{1,5},{5,1},{2,6},{6,2},{3,7},{7,3},{8,12},{12,8},{9,1... | collective-permute-start | bytes 6291464 | tf_op jit(solution)/shard_map/ppermute | solution.py:50
  70.8 0.3 fusion.85
  71.0 0.1 fusion.57
  71.1 0.2 compare_and_fusion
  71.3 0.2 compare_and_fusion.4
  71.5 0.2 fusion.81
  71.9 0.3 fusion.86
  72.3 0.3 fusion.82
  72.6 0.3 fusion.83
  72.9 0.3 fusion.84
  73.2 1.3 %collective-permute-done.3 = bf16[2,4,1024,128]{3,2,1,0:T(8,128)(2,1)S(1)} collective-permute-done((bf16[2,4,1024,128]{3,2,1,0:T(8,128)(2,1)S(1)}, bf16[2,4,1024,128]{3,2,1,0:T(8,128)(2,1)S(1)}, u32[]{:S(2)}, u32[]{:S(2)}) %collective-permute-start.3) | collective-permute-done | bytes 2097184 | tf_op jit(solution)/shard_map/ppermute | solution.py:50
  74.5 0.8 fusion
  75.3 0.2 fusion.33
  75.5 0.3 convolution_bitcast_fusion.4
  75.8 1.0 %fusion.1 = f32[128,4,2]{0,2,1:T(2,128)S(1)} fusion(f32[4,1024,128,2]{2,1,3,0:T(8,128)S(1)} %get-tuple-element.59, f32[128,4,2]{0,2,1:T(2,128)S(1)} %bitcast.234, pred[128,1024]{0,1:T(8,128)(4,1)S(1)} %compare_and_fusion), kind=kLoop, calls=%fused_computation.3 | loop fusion | flops 5241856 | bytes 4333568 | tf_op jit(solution)/shard_map/reduce_sum | solution.py:68
  76.9 0.2 fusion.39
  77.1 0.2 fusion.37
  77.3 0.2 fusion.35
  77.5 0.3 fusion.19
  77.8 1.3 %fusion.14 = f32[128,4,2,128]{0,3,2,1:T(8,128)S(1)} fusion(f32[4,1024,128,2]{2,1,3,0:T(8,128)S(1)} %get-tuple-element.59, f32[128,4,2]{0,2,1:T(2,128)S(1)} %bitcast.236, pred[128,1024]{0,1:T(8,128)(4,1)S(1)} %compare_and_fusion, bf16[2,4,1024,128]{3,2,1,0:T(8,128)(2,1)S(1)} %collective-permute-done.3), kind=kOutput, calls=%fused_computation.20 | convolution fusion | flops 273678336 | bytes 5902336 | tf_op jit(solution)/shard_map/thep,hpd->thed/dot_general | solution.py:65
  79.1 0.3 convolution_bitcast_fusion.1
  79.4 0.3 convolution_bitcast_fusion.2
  79.7 0.4 fusion.31
  80.2 0.9 %copy.142 = bf16[128,1024]{1,0:T(8,128)(2,1)} copy(bf16[128,1024]{0,1:T(8,128)(2,1)S(1)} %bitcast.218) | data formatting | bytes 524288 | tf_op jit(solution)/shard_map/reshape | solution.py:116
  (30 shorter events, 1.8 us)
Async XLA Ops:
  0.0 46.3 %copy-start = (s32[4]{0:T(128)S(1)}, s32[4]{0:T(128)}, u32[]{:S(2)}) copy-start(s32[4]{0:T(128)} %param.15) | copy-start | bytes 52
  1.8 33.6 %all-to-all-start = ((bf16[64,2,4,4,128]{4,3,2,1,0:T(4,128)(2,1)}), bf16[64,2,4,4,128]{4,3,2,1,0:T(4,128)(2,1)S(1)}, u32[]{:S(2)}, u32[]{:S(2)}) async-start(bf16[64,2,4,4,128]{4,3,2,1,0:T(4,128)(2,1)} %bitcast.18), calls=%async_computation | async-start | bytes 1048576 | tf_op jit(solution)/shard_map/all_to_all | solution.py:30
  35.6 11.9 %collective-permute-start.2 = (bf16[2,4,256,128]{3,2,1,0:T(8,128)(2,1)S(1)}, bf16[2,4,256,128]{3,2,1,0:T(8,128)(2,1)S(1)}, u32[]{:S(2)}, u32[]{:S(2)}) collective-permute-start(bf16[2,4,256,128]{3,2,1,0:T(8,128)(2,1)S(1)} %bitcast.210), channel_id=1, source_target_pairs={{0,384},{128,0},{256,128},{384,256},{1,385},{129,1},{257,129},{385... | collective-permute-start | bytes 1572872 | tf_op jit(solution)/shard_map/ppermute | solution.py:37
  40.0 13.6 %collective-permute-start.1 = (bf16[2,4,256,128]{3,2,1,0:T(8,128)(2,1)S(1)}, bf16[2,4,256,128]{3,2,1,0:T(8,128)(2,1)S(1)}, u32[]{:S(2)}, u32[]{:S(2)}) collective-permute-start(bf16[2,4,256,128]{3,2,1,0:T(8,128)(2,1)S(1)} %bitcast.211), channel_id=1, source_target_pairs={{0,128},{128,256},{256,384},{384,0},{1,129},{129,257},{257,385},{3... | collective-permute-start | bytes 1572872 | tf_op jit(solution)/shard_map/ppermute | solution.py:37
  41.9 21.1 %collective-permute-start = (bf16[2,4,256,128]{3,2,1,0:T(8,128)(2,1)S(1)}, bf16[2,4,256,128]{3,2,1,0:T(8,128)(2,1)S(1)}, u32[]{:S(2)}, u32[]{:S(2)}) collective-permute-start(bf16[2,4,256,128]{3,2,1,0:T(8,128)(2,1)S(1)} %bitcast.212), channel_id=1, source_target_pairs={{0,256},{128,384},{256,0},{384,128},{1,257},{129,385},{257,1},{385... | collective-permute-start | bytes 1572872 | tf_op jit(solution)/shard_map/ppermute | solution.py:37
  63.2 11.3 %collective-permute-start.3 = (bf16[2,4,1024,128]{3,2,1,0:T(8,128)(2,1)S(1)}, bf16[2,4,1024,128]{3,2,1,0:T(8,128)(2,1)S(1)}, u32[]{:S(2)}, u32[]{:S(2)}) collective-permute-start(bf16[2,4,1024,128]{3,2,1,0:T(8,128)(2,1)S(1)} %pad_maximum_fusion), channel_id=1, source_target_pairs={{0,4},{4,0},{1,5},{5,1},{2,6},{6,2},{3,7},{7,3},{8,12},{12,8},{9,1... | collective-permute-start | bytes 6291464 | tf_op jit(solution)/shard_map/ppermute | solution.py:50

commit v13 on v12

--- a/solution.py
+++ b/solution.py
@@ -36,7 +36,7 @@
     def shift(held, step):
         return lax.ppermute(held, "x", [(i, (i + step) % count) for i in range(count)])
 
-    arrived = [(shift(mine, step), -step) for step in (2, 1, -1)]
+    arrived = [(shift(mine, step), -step) for step in (-1, 1, 2)]
     grid = block_prefix.reshape(size["x"], size["zh"], size["y"], size["core"], tensor_count)
     grid = grid.transpose(0, 2, 1, 3, 4)
 

time: 81.9 us -> 77.9 us (0.951)
  starting transfers between devices: 34.6 us -> 31.4 us
  waiting for transfers between devices: 26 us -> 25.1 us
    ppermute x1, starting transfers between devices: 7.55 us -> 3.17 us  [gather_cache(): lax.ppermute(jnp.concatenate([held for held, _ in everything], axis=2), '...]
    ppermute x3, starting transfers between devices: 9.93 us -> 11.1 us  [shift(): lax.ppermute(held, 'x', [(i, (i + step) % count) for i in range(count)])]
    ppermute x3, waiting for transfers between devices: 16.6 us -> 15.7 us  [shift(): lax.ppermute(held, 'x', [(i, (i + step) % count) for i in range(count)])]
  transfers between devices with their start and end apart: 5 -> 5, of which waited for: 5 -> 4; matrix products, arithmetic and copies ran while one was open for 14% -> 15% of each run, Pallas kernels for 0% -> 0%
where the time goes in v13:
time: 77.9 us; the launch traced here: 77 us
  starting transfers between devices  31.4 us (40%)
  waiting for transfers between devices  25.1 us (32%)
  local copies, waits for them, and re-layouts  10.4 us (13%)
  matrix products  5.24 us (7%)
  other arithmetic  4.32 us (6%)
    all_to_all x1, starting transfers between devices, gather_cache(): lax.all_to_all(outgoing, ('y', 'zh', 'tp'), split_axis=0, concat_axis=3,...  17.1 us
    ppermute x3, waiting for transfers between devices, shift(): lax.ppermute(held, 'x', [(i, (i + step) % count) for i in range(count)])  15.7 us
    ppermute x3, starting transfers between devices, shift(): lax.ppermute(held, 'x', [(i, (i + step) % count) for i in range(count)])  11.1 us
    all_to_all x1, waiting for transfers between devices, gather_cache(): lax.all_to_all(outgoing, ('y', 'zh', 'tp'), split_axis=0, concat_axis=3,...  8.14 us
    ppermute x1, starting transfers between devices, gather_cache(): lax.ppermute(jnp.concatenate([held for held, _ in everything], axis=2), '...  3.17 us
    dot_general x6, matrix products, fold_block(): jnp.einsum('thep,hpd->thed', weights.astype(jnp.bfloat16), values, prefer...  2.96 us
    dot_general x6, matrix products, fold_block(): jnp.einsum('thed,hpd->thep', query_rows, keys, preferred_element_type=jnp...  2.29 us
    reduce_sum x6, other arithmetic, fold_block(): total = jnp.sum(weights, axis=-1)  1.93 us
  transfers between devices with their start and end apart: 5, of which 4 were waited for; matrix products, arithmetic and copies ran while one was open for 15% of the time, Pallas kernels for 0%

profile of v13, /device:TPU:1, one launch (start us, length us, event | category | flops | bytes accessed | tf_op | source)
XLA Modules:
  0.0 77.0 jit_solution(3330358283697125302)
XLA Ops:
  0.0 0.8 %reshape.445 = bf16[4,4,4,2,128]{4,3,2,1,0:T(2,128)(2,1)S(1)} reshape(bf16[4,4096]{1,0:T(4,128)(2,1)} %param.12) | data formatting | bytes 65536 | tf_op jit(solution)/shard_map/reshape | solution.py:26
  0.8 1.0 %broadcast_in_dim.214 = bf16[16,4,2,4,4,128]{5,4,3,2,1,0:T(4,128)(2,1)} broadcast(bf16[4,2,4,4,128]{4,3,2,1,0:T(4,128)(2,1)S(1)} %copy.113), dimensions={1,2,3,4,5} | broadcast | bytes 557056 | tf_op jit(solution)/shard_map/broadcast_in_dim | solution.py:28
  1.8 17.1 %all-to-all-start = ((bf16[64,2,4,4,128]{4,3,2,1,0:T(4,128)(2,1)}), bf16[64,2,4,4,128]{4,3,2,1,0:T(4,128)(2,1)S(1)}, u32[]{:S(2)}, u32[]{:S(2)}) async-start(bf16[64,2,4,4,128]{4,3,2,1,0:T(4,128)(2,1)} %bitcast.18), calls=%async_computation | async-start | bytes 1048576 | tf_op jit(solution)/shard_map/all_to_all | solution.py:30
  19.1 0.8 %reduce-window.4 = s32[4,1]{0,1:T(1,128)S(1)} reduce-window(s32[4,1]{0,1:T(1,128)} %bitcast.246, s32[]{:T(128)} %constant.73.clone.1), window={size=4x1 pad=3_0x0_0}, to_apply=%region_0.0 | reduce-window | flops 12 | bytes 36 | tf_op jit(solution)/shard_map/reduce-window
  19.9 0.8 %reshape.443 = s32[4,2,8,2,4]{4,3,2,1,0:T(2,128)S(1)} reshape(s32[512]{0:T(512)} %param.13) | data formatting | bytes 4096 | tf_op jit(solution)/shard_map/reshape | solution.py:40
  20.8 0.1 copy.130
  20.9 0.1 copy.125
  21.0 0.1 copy.138
  21.1 0.1 reshape.456
  21.3 0.1 reshape.457
  21.4 0.1 copy.137
  21.5 0.1 reshape.454
  21.7 0.1 reshape.455
  21.8 0.1 copy.119
  21.9 0.1 copy.111
  22.0 0.1 copy.136
  22.1 0.1 reshape.452
  22.3 0.1 reshape.453
  22.5 0.1 reshape.450
  22.6 0.1 reshape.451
  22.8 0.6 slice.42
  23.3 1.1 %reshape.442 = bf16[128,4,2,128]{3,2,1,0:T(2,128)(2,1)S(1)} reshape(bf16[128,1024]{1,0:T(8,128)(2,1)} %param.10) | data formatting | bytes 524288 | tf_op jit(solution)/shard_map/reshape | solution.py:99
  24.7 0.1 eq.133
  24.9 0.1 reshape.447
  25.1 0.1 eq.136
  25.3 0.1 reshape.448
  25.5 0.1 eq.139
  25.7 0.1 reshape.449
  25.9 0.1 eq.142
  26.0 1.1 %copy.106 = bf16[128,1024]{0,1:T(8,128)(2,1)S(1)} copy(bf16[128,1024]{1,0:T(8,128)(2,1)} %param.11) | data formatting | bytes 524288 | tf_op args[1]
  27.1 0.1 copy.172
  27.3 8.1 %all-to-all-done = bf16[64,2,4,4,128]{4,3,2,1,0:T(4,128)(2,1)S(1)} async-done(((bf16[64,2,4,4,128]{4,3,2,1,0:T(4,128)(2,1)}), bf16[64,2,4,4,128]{4,3,2,1,0:T(4,128)(2,1)S(1)}, u32[]{:S(2)}, u32[]{:S(2)}) %all-to-all-start) | async-done | bytes 524320 | tf_op jit(solution)/shard_map/all_to_all | solution.py:30
  35.4 0.2 copy.121
  35.6 4.7 %collective-permute-start.2 = (bf16[2,4,256,128]{3,2,1,0:T(8,128)(2,1)S(1)}, bf16[2,4,256,128]{3,2,1,0:T(8,128)(2,1)S(1)}, u32[]{:S(2)}, u32[]{:S(2)}) collective-permute-start(bf16[2,4,256,128]{3,2,1,0:T(8,128)(2,1)S(1)} %bitcast.210), channel_id=1, source_target_pairs={{0,256},{128,384},{256,0},{384,128},{1,257},{129,385},{257,1},{385... | collective-permute-start | bytes 1572872 | tf_op jit(solution)/shard_map/ppermute | solution.py:37
  40.3 2.2 %collective-permute-start.1 = (bf16[2,4,256,128]{3,2,1,0:T(8,128)(2,1)S(1)}, bf16[2,4,256,128]{3,2,1,0:T(8,128)(2,1)S(1)}, u32[]{:S(2)}, u32[]{:S(2)}) collective-permute-start(bf16[2,4,256,128]{3,2,1,0:T(8,128)(2,1)S(1)} %bitcast.211), channel_id=1, source_target_pairs={{0,128},{128,256},{256,384},{384,0},{1,129},{129,257},{257,385},{3... | collective-permute-start | bytes 1572872 | tf_op jit(solution)/shard_map/ppermute | solution.py:37
  42.5 4.3 %collective-permute-start = (bf16[2,4,256,128]{3,2,1,0:T(8,128)(2,1)S(1)}, bf16[2,4,256,128]{3,2,1,0:T(8,128)(2,1)S(1)}, u32[]{:S(2)}, u32[]{:S(2)}) collective-permute-start(bf16[2,4,256,128]{3,2,1,0:T(8,128)(2,1)S(1)} %bitcast.212), channel_id=1, source_target_pairs={{0,384},{128,0},{256,128},{384,256},{1,385},{129,1},{257,129},{385... | collective-permute-start | bytes 1572872 | tf_op jit(solution)/shard_map/ppermute | solution.py:37
  46.8 0.7 iota_compare_fusion.3
  47.7 1.2 %collective-permute-done.2 = bf16[2,4,256,128]{3,2,1,0:T(8,128)(2,1)S(1)} collective-permute-done((bf16[2,4,256,128]{3,2,1,0:T(8,128)(2,1)S(1)}, bf16[2,4,256,128]{3,2,1,0:T(8,128)(2,1)S(1)}, u32[]{:S(2)}, u32[]{:S(2)}) %collective-permute-start.2) | collective-permute-done | bytes 524320 | tf_op jit(solution)/shard_map/ppermute | solution.py:37
  48.9 14.5 %collective-permute-done.1 = bf16[2,4,256,128]{3,2,1,0:T(8,128)(2,1)S(1)} collective-permute-done((bf16[2,4,256,128]{3,2,1,0:T(8,128)(2,1)S(1)}, bf16[2,4,256,128]{3,2,1,0:T(8,128)(2,1)S(1)}, u32[]{:S(2)}, u32[]{:S(2)}) %collective-permute-start.1) | collective-permute-done | bytes 524320 | tf_op jit(solution)/shard_map/ppermute | solution.py:37
  63.4 0.1 pad_maximum_fusion
  63.6 3.2 %collective-permute-start.3 = (bf16[2,4,1024,128]{3,2,1,0:T(8,128)(2,1)S(1)}, bf16[2,4,1024,128]{3,2,1,0:T(8,128)(2,1)S(1)}, u32[]{:S(2)}, u32[]{:S(2)}) collective-permute-start(bf16[2,4,1024,128]{3,2,1,0:T(8,128)(2,1)S(1)} %pad_maximum_fusion), channel_id=1, source_target_pairs={{0,4},{4,0},{1,5},{5,1},{2,6},{6,2},{3,7},{7,3},{8,12},{12,8},{9,1... | collective-permute-start | bytes 6291464 | tf_op jit(solution)/shard_map/ppermute | solution.py:50
  66.7 0.2 fusion.85
  67.0 0.1 fusion.57
  67.1 0.2 compare_and_fusion
  67.3 0.2 compare_and_fusion.4
  67.5 0.2 fusion.81
  67.9 0.3 fusion.86
  68.2 0.3 fusion.82
  68.6 0.3 fusion.83
  68.9 0.3 fusion.84
  69.2 1.3 %collective-permute-done.3 = bf16[2,4,1024,128]{3,2,1,0:T(8,128)(2,1)S(1)} collective-permute-done((bf16[2,4,1024,128]{3,2,1,0:T(8,128)(2,1)S(1)}, bf16[2,4,1024,128]{3,2,1,0:T(8,128)(2,1)S(1)}, u32[]{:S(2)}, u32[]{:S(2)}) %collective-permute-start.3) | collective-permute-done | bytes 2097184 | tf_op jit(solution)/shard_map/ppermute | solution.py:50
  70.5 0.8 fusion
  71.3 0.2 fusion.33
  71.5 0.3 convolution_bitcast_fusion.4
  71.8 1.0 %fusion.1 = f32[128,4,2]{0,2,1:T(2,128)S(1)} fusion(f32[4,1024,128,2]{2,1,3,0:T(8,128)S(1)} %get-tuple-element.59, f32[128,4,2]{0,2,1:T(2,128)S(1)} %bitcast.234, pred[128,1024]{0,1:T(8,128)(4,1)S(1)} %compare_and_fusion), kind=kLoop, calls=%fused_computation.3 | loop fusion | flops 5241856 | bytes 4333568 | tf_op jit(solution)/shard_map/reduce_sum | solution.py:68
  72.8 0.2 fusion.39
  73.0 0.2 fusion.37
  73.2 0.2 fusion.35
  73.5 0.3 fusion.19
  73.8 1.3 %fusion.14 = f32[128,4,2,128]{0,3,2,1:T(8,128)S(1)} fusion(f32[4,1024,128,2]{2,1,3,0:T(8,128)S(1)} %get-tuple-element.59, f32[128,4,2]{0,2,1:T(2,128)S(1)} %bitcast.236, pred[128,1024]{0,1:T(8,128)(4,1)S(1)} %compare_and_fusion, bf16[2,4,1024,128]{3,2,1,0:T(8,128)(2,1)S(1)} %collective-permute-done.3), kind=kOutput, calls=%fused_computation.20 | convolution fusion | flops 273678336 | bytes 5902336 | tf_op jit(solution)/shard_map/thep,hpd->thed/dot_general | solution.py:65
  75.0 0.3 convolution_bitcast_fusion.1
  75.4 0.3 convolution_bitcast_fusion.2
  75.7 0.4 fusion.31
  76.2 0.9 %copy.142 = bf16[128,1024]{1,0:T(8,128)(2,1)} copy(bf16[128,1024]{0,1:T(8,128)(2,1)S(1)} %bitcast.218) | data formatting | bytes 524288 | tf_op jit(solution)/shard_map/reshape | solution.py:116
  (30 shorter events, 1.7 us)
Async XLA Ops:
  0.0 47.5 %copy-start = (s32[4]{0:T(128)S(1)}, s32[4]{0:T(128)}, u32[]{:S(2)}) copy-start(s32[4]{0:T(128)} %param.15) | copy-start | bytes 52
  1.8 33.6 %all-to-all-start = ((bf16[64,2,4,4,128]{4,3,2,1,0:T(4,128)(2,1)}), bf16[64,2,4,4,128]{4,3,2,1,0:T(4,128)(2,1)S(1)}, u32[]{:S(2)}, u32[]{:S(2)}) async-start(bf16[64,2,4,4,128]{4,3,2,1,0:T(4,128)(2,1)} %bitcast.18), calls=%async_computation | async-start | bytes 1048576 | tf_op jit(solution)/shard_map/all_to_all | solution.py:30
  35.6 13.3 %collective-permute-start.2 = (bf16[2,4,256,128]{3,2,1,0:T(8,128)(2,1)S(1)}, bf16[2,4,256,128]{3,2,1,0:T(8,128)(2,1)S(1)}, u32[]{:S(2)}, u32[]{:S(2)}) collective-permute-start(bf16[2,4,256,128]{3,2,1,0:T(8,128)(2,1)S(1)} %bitcast.210), channel_id=1, source_target_pairs={{0,256},{128,384},{256,0},{384,128},{1,257},{129,385},{257,1},{385... | collective-permute-start | bytes 1572872 | tf_op jit(solution)/shard_map/ppermute | solution.py:37
  40.3 23.1 %collective-permute-start.1 = (bf16[2,4,256,128]{3,2,1,0:T(8,128)(2,1)S(1)}, bf16[2,4,256,128]{3,2,1,0:T(8,128)(2,1)S(1)}, u32[]{:S(2)}, u32[]{:S(2)}) collective-permute-start(bf16[2,4,256,128]{3,2,1,0:T(8,128)(2,1)S(1)} %bitcast.211), channel_id=1, source_target_pairs={{0,128},{128,256},{256,384},{384,0},{1,129},{129,257},{257,385},{3... | collective-permute-start | bytes 1572872 | tf_op jit(solution)/shard_map/ppermute | solution.py:37
  42.5 20.9 %collective-permute-start = (bf16[2,4,256,128]{3,2,1,0:T(8,128)(2,1)S(1)}, bf16[2,4,256,128]{3,2,1,0:T(8,128)(2,1)S(1)}, u32[]{:S(2)}, u32[]{:S(2)}) collective-permute-start(bf16[2,4,256,128]{3,2,1,0:T(8,128)(2,1)S(1)} %bitcast.212), channel_id=1, source_target_pairs={{0,384},{128,0},{256,128},{384,256},{1,385},{129,1},{257,129},{385... | collective-permute-start | bytes 1572872 | tf_op jit(solution)/shard_map/ppermute | solution.py:37
  63.6 6.9 %collective-permute-start.3 = (bf16[2,4,1024,128]{3,2,1,0:T(8,128)(2,1)S(1)}, bf16[2,4,1024,128]{3,2,1,0:T(8,128)(2,1)S(1)}, u32[]{:S(2)}, u32[]{:S(2)}) collective-permute-start(bf16[2,4,1024,128]{3,2,1,0:T(8,128)(2,1)S(1)} %pad_maximum_fusion), channel_id=1, source_target_pairs={{0,4},{4,0},{1,5},{5,1},{2,6},{6,2},{3,7},{7,3},{8,12},{12,8},{9,1... | collective-permute-start | bytes 6291464 | tf_op jit(solution)/shard_map/ppermute | solution.py:50
